TPU v7x, 32 devices: a whole 2x2x4 slice. The times are simulated.
32 devices in a mesh: groups: 2 (over y), seq: 16 (over z, x, core).
Axes of the slice: x: 2, y: 2, z: 4, core: 2. Of those that a mesh axis runs over, the one named last changes fastest.
Arguments:
- queries: bfloat16 [8192, 2048], P(('groups', 'seq')), parts along dimension 0, may hold values from -64 to 64
- keys: bfloat16 [8192, 2048], P(('groups', 'seq')), parts along dimension 0, may hold values from -6 to 6
- values: bfloat16 [8192, 2048], P(('groups', 'seq')), parts along dimension 0, may hold values from -6 to 6
- d_out: bfloat16 [8192, 2048], P(('groups', 'seq')), parts along dimension 0, may hold values from -6 to 6
- key_lists: int32 [64, 4], P(('groups', 'seq')), parts along dimension 0, may hold values from 0 to 31, as said below
Outputs:
- d_queries: bfloat16 [8192, 2048], P(('groups', 'seq')), parts along dimension 0
- d_keys: bfloat16 [8192, 2048], P(('groups', 'seq')), parts along dimension 0
- d_values: bfloat16 [8192, 2048], P(('groups', 'seq')), parts along dimension 0
There are 2 independent parts, one for each index of `groups`. A program takes and returns all parts, laid end to end along the dimension named above; each array names one. Nothing has to cross between parts.
Inputs may be any that keep to these rules, and one draw needn't show every extreme that they name: `key_lists`: row b holds b, then (b - 1) modulo 32 if b is the first block of its aligned group of 2 blocks, (b + 1) modulo 32 if it is the last, else either of the two; then a block of the aligned group of 2 blocks that lies 4 groups before block b's group (cyclically), then a block of the group 4 groups after it (cyclically).
All inputs are finite; a program needn't handle non-finite values.
Results may differ from a plain program's by a relative error of at most 0.017.
Values may be sent and summed in bfloat16 or wider, within the bound.
No kernel may reach another device: no remote copies, remote signals or barrier semaphores. Data moves between devices by JAX's collectives and lax.ppermute only.
A program may use at most 128 MiB of HBM per device.

v0:
```python
import math

import jax
import jax.numpy as jnp
from jax import lax
from jax.experimental import pallas as pl
from jax.experimental.pallas import tpu as pltpu
from jax.sharding import PartitionSpec as P

BLK = 128
LOCAL_HEADS = 16
HEAD_SIZE = 128
FRAME_DEV = 4
BLK_DEV = 2

NT = (((1,), (1,)), ((), ()))
TN = (((0,), (0,)), ((), ()))
F32 = jnp.float32
BF16 = jnp.bfloat16


def shifted(tree, axis, distance):
    count = lax.axis_size(axis)
    route = [(i, (i + distance) % count) for i in range(count)]
    return lax.ppermute(tree, axis, route)


def row_block(ref, index):
    start = pl.multiple_of(index * BLK, BLK)
    return ref[pl.ds(start, BLK), :]


def query_kernel(kl_ref, q_ref, do_ref, k_ref, v_ref, lk_ref, lv_ref, rk_ref, rv_ref,
                 ek_ref, ev_ref, tk_ref, tv_ref, dq_ref, st_ref, *, scale):
    for i in range(BLK_DEV):
        rows = slice(i * BLK, (i + 1) * BLK)
        q = q_ref[rows, :]
        do = do_ref[rows, :]
        side_k, side_v = (lk_ref, lv_ref) if i == 0 else (rk_ref, rv_ref)
        early = lax.rem(kl_ref[i, 2], BLK_DEV)
        late = lax.rem(kl_ref[i, 3], BLK_DEV)
        keys = jnp.concatenate(
            [k_ref[rows, :], side_k[...], row_block(ek_ref, early), row_block(tk_ref, late)], axis=0
        )
        vals = jnp.concatenate(
            [v_ref[rows, :], side_v[...], row_block(ev_ref, early), row_block(tv_ref, late)], axis=0
        )
        s = lax.dot_general(keys, q, NT, preferred_element_type=F32) * scale
        top = jnp.max(s, axis=0, keepdims=True)
        lse = top + jnp.log(jnp.sum(jnp.exp(s - top), axis=0, keepdims=True))
        p = jnp.exp(s - lse)
        p_low = p.astype(BF16)
        dp = lax.dot_general(vals, do, NT, preferred_element_type=F32)
        delta = jnp.sum(p_low.astype(F32) * dp, axis=0, keepdims=True)
        ds = (p * (dp - delta)).astype(BF16)
        dq = lax.dot_general(ds, keys, TN, preferred_element_type=F32) * scale
        dq_ref[rows, :] = dq.astype(BF16)
        st_ref[0, 0:1, rows] = lse
        st_ref[0, 1:2, rows] = delta


def key_terms(keys, vals, q, do, lse, delta, scale):
    s = lax.dot_general(keys, q, NT, preferred_element_type=F32) * scale
    p = jnp.exp(s - lse)
    p_low = p.astype(BF16)
    dp = lax.dot_general(vals, do, NT, preferred_element_type=F32)
    ds = (p * (dp - delta)).astype(BF16)
    d_value = jnp.dot(p_low, do, preferred_element_type=F32)
    d_key = jnp.dot(ds, q, preferred_element_type=F32)
    return d_key, d_value


def key_kernel(klp_ref, klm_ref, k_ref, v_ref, q_ref, do_ref, st_ref,
               lq_ref, ldo_ref, lst_ref, rq_ref, rdo_ref, rst_ref,
               pq_ref, pdo_ref, pst_ref, mq_ref, mdo_ref, mst_ref,
               dk_ref, dv_ref, acc_k, acc_v, *, scale):
    sides = ((lq_ref, ldo_ref, lst_ref, 1), (rq_ref, rdo_ref, rst_ref, 0))
    for j in range(BLK_DEV):
        rows = slice(j * BLK, (j + 1) * BLK)
        side_q, side_do, side_st, side_blk = sides[j]
        far = slice(side_blk * BLK, (side_blk + 1) * BLK)
        q = jnp.concatenate([q_ref[rows, :], side_q[...]], axis=0)
        do = jnp.concatenate([do_ref[rows, :], side_do[...]], axis=0)
        lse = jnp.concatenate([st_ref[0, 0:1, rows], side_st[0, 0:1, far]], axis=1)
        delta = jnp.concatenate([st_ref[0, 1:2, rows], side_st[0, 1:2, far]], axis=1)
        d_key, d_value = key_terms(k_ref[rows, :], v_ref[rows, :], q, do, lse, delta, scale)
        acc_k[rows, :] = d_key
        acc_v[rows, :] = d_value
    for kl_ref, column, rq, rdo, rst in ((klp_ref, 2, pq_ref, pdo_ref, pst_ref),
                                         (klm_ref, 3, mq_ref, mdo_ref, mst_ref)):
        for r in range(BLK_DEV):
            rows = slice(r * BLK, (r + 1) * BLK)
            pick = lax.rem(kl_ref[r, column], BLK_DEV)
            start = pl.multiple_of(pick * BLK, BLK)
            mine = pl.ds(start, BLK)
            d_key, d_value = key_terms(
                k_ref[mine, :], v_ref[mine, :], rq[rows, :], rdo[rows, :],
                rst[0, 0:1, rows], rst[0, 1:2, rows], scale,
            )
            acc_k[mine, :] += d_key
            acc_v[mine, :] += d_value
    dk_ref[...] = (acc_k[...] * scale).astype(BF16)
    dv_ref[...] = acc_v[...].astype(BF16)


def body(queries, keys, values, d_out, key_lists):
    rows, width = queries.shape
    heads = width // HEAD_SIZE
    assert rows == BLK_DEV * BLK and key_lists.shape[0] == BLK_DEV
    scale = 1.0 / math.sqrt(HEAD_SIZE)

    tail = slice(rows - BLK, rows)
    head = slice(0, BLK)
    from_left = shifted(
        (keys[tail], values[tail], queries[tail], d_out[tail]), "seq", 1
    )
    from_right = shifted(
        (keys[head], values[head], queries[head], d_out[head]), "seq", -1
    )
    from_early = shifted((keys, values, queries, d_out, key_lists), "seq", FRAME_DEV)
    from_late = shifted((keys, values, queries, d_out, key_lists), "seq", -FRAME_DEV)

    full = pl.BlockSpec((rows, HEAD_SIZE), lambda h, *_: (0, h))
    edge = pl.BlockSpec((BLK, HEAD_SIZE), lambda h, *_: (0, h))
    stat = pl.BlockSpec((1, 2, rows), lambda h, *_: (h, 0, 0))

    d_queries, stats = pl.pallas_call(
        lambda *refs: query_kernel(*refs, scale=scale),
        grid_spec=pltpu.PrefetchScalarGridSpec(
            num_scalar_prefetch=1,
            grid=(heads,),
            in_specs=[full, full, full, full, edge, edge, edge, edge, full, full, full, full],
            out_specs=[full, stat],
        ),
        out_shape=[
            jax.ShapeDtypeStruct((rows, width), BF16),
            jax.ShapeDtypeStruct((heads, 2, rows), F32),
        ],
    )(
        key_lists, queries, d_out, keys, values,
        from_left[0], from_left[1], from_right[0], from_right[1],
        from_early[0], from_early[1], from_late[0], from_late[1],
    )

    stats_left = shifted(stats, "seq", 1)
    stats_right = shifted(stats, "seq", -1)
    stats_early = shifted(stats, "seq", FRAME_DEV)
    stats_late = shifted(stats, "seq", -FRAME_DEV)

    d_keys, d_values = pl.pallas_call(
        lambda *refs: key_kernel(*refs, scale=scale),
        grid_spec=pltpu.PrefetchScalarGridSpec(
            num_scalar_prefetch=2,
            grid=(heads,),
            in_specs=[full, full, full, full, stat,
                      edge, edge, stat, edge, edge, stat,
                      full, full, stat, full, full, stat],
            out_specs=[full, full],
            scratch_shapes=[pltpu.VMEM((rows, HEAD_SIZE), F32), pltpu.VMEM((rows, HEAD_SIZE), F32)],
        ),
        out_shape=[
            jax.ShapeDtypeStruct((rows, width), BF16),
            jax.ShapeDtypeStruct((rows, width), BF16),
        ],
    )(
        from_late[4], from_early[4],
        keys, values, queries, d_out, stats,
        from_left[2], from_left[3], stats_left,
        from_right[2], from_right[3], stats_right,
        from_late[2], from_late[3], stats_late,
        from_early[2], from_early[3], stats_early,
    )
    return (d_queries, d_keys, d_values)


def solution(mesh):
    spec = P(("groups", "seq"), None)
    return jax.shard_map(
        body,
        mesh=mesh,
        in_specs=(spec, spec, spec, spec, spec),
        out_specs=(spec, spec, spec),
        check_vma=False,
    )
```

profile of v0, /device:TPU:0, one launch (start us, length us, event | category | flops | bytes accessed | tf_op | source)
XLA Modules:
  0.0 255.4 jit_solution(10181865511906671244)
XLA Ops:
  0.6 1.4 fusion.3
  2.0 0.5 collective-permute-start
  2.5 0.1 fusion.2
  2.6 2.7 %collective-permute-start.1 = (bf16[128,2048]{1,0:T(8,128)(2,1)S(1)}, bf16[128,2048]{1,0:T(8,128)(2,1)S(1)}, u32[]{:S(2)}, u32[]{:S(2)}) collective-permute-start(bf16[128,2048]{1,0:T(8,128)(2,1)S(1)} %get-tuple-element.16), channel_id=1, source_target_pairs={{0,1},{1,2},{2,3},{3,4},{4,5},{5,6},{6,7},{7,8},{8,9},{9,10},{10,1... | collective-permute-start | bytes 1572872 | tf_op jit(solution)/shard_map/ppermute | solution.py:25
  5.3 2.5 collective-permute-start.2
  7.8 0.7 collective-permute-start.3
  8.5 1.9 collective-permute-start.8
  10.6 0.9 fusion
  11.5 9.4 %collective-permute-done.8.refs_0_ = s32[2,4]{1,0:T(2,128)S(1)} collective-permute-done((s32[2,4]{1,0:T(2,128)S(1)}, s32[2,4]{1,0:T(2,128)S(1)}, u32[]{:S(2)}, u32[]{:S(2)}) %collective-permute-start.8) | collective-permute-done | bytes 64 | tf_op jit(solution)/shard_map/ppermute | solution.py:25
  20.9 1.6 collective-permute-start.9
  22.4 3.8 %collective-permute-done.9.refs_1_ = s32[2,4]{1,0:T(2,128)S(1)} collective-permute-done((s32[2,4]{1,0:T(2,128)S(1)}, s32[2,4]{1,0:T(2,128)S(1)}, u32[]{:S(2)}, u32[]{:S(2)}) %collective-permute-start.9) | collective-permute-done | bytes 64 | tf_op jit(solution)/shard_map/ppermute | solution.py:25
  26.2 0.5 copy-done.20
  26.9 1.3 collective-permute-start.5
  28.2 2.6 %collective-permute-start.6 = (bf16[256,2048]{1,0:T(8,128)(2,1)S(1)}, bf16[256,2048]{1,0:T(8,128)(2,1)S(1)}, u32[]{:S(2)}, u32[]{:S(2)}) collective-permute-start(bf16[256,2048]{1,0:T(8,128)(2,1)S(1)} %copy-done.2), channel_id=1, source_target_pairs={{0,12},{1,13},{2,14},{3,15},{4,0},{5,1},{6,2},{7,3},{8,4},{9,5},{1... | collective-permute-start | bytes 3145736 | tf_op jit(solution)/shard_map/ppermute | solution.py:25
  30.7 9.2 %collective-permute-done.10.refs_7_ = bf16[128,2048]{1,0:T(8,128)(2,1)} collective-permute-done((bf16[128,2048]{1,0:T(8,128)(2,1)S(1)}, bf16[128,2048]{1,0:T(8,128)(2,1)}, u32[]{:S(2)}, u32[]{:S(2)}) %collective-permute-start.10) | collective-permute-done | bytes 524320 | tf_op jit(solution)/shard_map/ppermute | solution.py:25
  40.0 11.1 %collective-permute-done.11.refs_8_ = bf16[128,2048]{1,0:T(8,128)(2,1)S(1)} collective-permute-done((bf16[128,2048]{1,0:T(8,128)(2,1)S(1)}, bf16[128,2048]{1,0:T(8,128)(2,1)S(1)}, u32[]{:S(2)}, u32[]{:S(2)}) %collective-permute-start.11) | collective-permute-done | bytes 524320 | tf_op jit(solution)/shard_map/ppermute | solution.py:25
  51.1 76.0 %collective-permute-done.13.refs_10_ = bf16[128,2048]{1,0:T(8,128)(2,1)S(1)} collective-permute-done((bf16[128,2048]{1,0:T(8,128)(2,1)S(1)}, bf16[128,2048]{1,0:T(8,128)(2,1)S(1)}, u32[]{:S(2)}, u32[]{:S(2)}) %collective-permute-start.13) | collective-permute-done | bytes 524320 | tf_op jit(solution)/shard_map/ppermute | solution.py:25
  127.1 5.5 %collective-permute-start.16 = (bf16[256,2048]{1,0:T(8,128)(2,1)S(1)}, bf16[256,2048]{1,0:T(8,128)(2,1)}, u32[]{:S(2)}, u32[]{:S(2)}) collective-permute-start(bf16[256,2048]{1,0:T(8,128)(2,1)S(1)} %copy-done), channel_id=1, source_target_pairs={{0,12},{1,13},{2,14},{3,15},{4,0},{5,1},{6,2},{7,3},{8,4},{9,5},{1... | collective-permute-start | bytes 3145736 | tf_op jit(solution)/shard_map/ppermute | solution.py:25
  132.6 1.6 collective-permute-start.17
  134.2 0.4 collective-permute-start.19
  134.8 0.4 copy-done.6
  135.2 0.4 copy-done.7
  135.6 0.4 copy-done.8
  136.0 46.3 %collective-permute-start.14 = (bf16[128,2048]{1,0:T(8,128)(2,1)}, bf16[128,2048]{1,0:T(8,128)(2,1)}, u32[]{:S(2)}, u32[]{:S(2)}) collective-permute-start(bf16[128,2048]{1,0:T(8,128)(2,1)} %get-tuple-element.11), channel_id=1, source_target_pairs={{0,15},{1,0},{2,1},{3,2},{4,3},{5,4},{6,5},{7,6},{8,7},{9,8},{10,9... | collective-permute-start | bytes 1572872 | tf_op jit(solution)/shard_map/ppermute | solution.py:25
  182.3 21.7 %shard_map.76 = (bf16[256,2048]{1,0:T(8,128)(2,1)}, f32[16,2,256]{2,1,0:T(2,128)}) custom-call(s32[2,4]{1,0:T(2,128)} %refs_0_.1, bf16[256,2048]{1,0:T(8,128)(2,1)} %refs_4_.3, bf16[256,2048]{1,0:T(8,128)(2,1)} %refs_5_.1, bf16[256,2048]{1,0:T(8,128)(2,1)} %refs_2_.3, bf16[256,2048]{1,0:T(8,128)(2,1)} %refs_3_.3, bf16[128,2048]{1,0:T(8,128)(2,1)} %copy-done.11, ...), custom_call_target="tpu_custom_call" | custom-call | tf_op jit(solution)/shard_map/pallas_call | solution.py:127
  204.0 15.1 %collective-permute-done.14.refs_11_ = bf16[128,2048]{1,0:T(8,128)(2,1)} collective-permute-done((bf16[128,2048]{1,0:T(8,128)(2,1)}, bf16[128,2048]{1,0:T(8,128)(2,1)}, u32[]{:S(2)}, u32[]{:S(2)}) %collective-permute-start.14) | collective-permute-done | bytes 524320 | tf_op jit(solution)/shard_map/ppermute | solution.py:25
  219.1 4.6 %collective-permute-start.15 = (f32[16,2,256]{2,1,0:T(2,128)}, f32[16,2,256]{2,1,0:T(2,128)S(1)}, u32[]{:S(2)}, u32[]{:S(2)}) collective-permute-start(f32[16,2,256]{2,1,0:T(2,128)} %get-tuple-element.8.refs_6_), channel_id=1, source_target_pairs={{0,15},{1,0},{2,1},{3,2},{4,3},{5,4},{6,5},{7,6},{8,7},{9,8},{10,9... | collective-permute-start | bytes 98312 | tf_op jit(solution)/shard_map/ppermute | solution.py:25
  223.7 2.1 collective-permute-start.18
  225.8 2.7 %collective-permute-done.18.refs_15_ = f32[16,2,256]{2,1,0:T(2,128)S(1)} collective-permute-done((f32[16,2,256]{2,1,0:T(2,128)}, f32[16,2,256]{2,1,0:T(2,128)S(1)}, u32[]{:S(2)}, u32[]{:S(2)}) %collective-permute-start.18) | collective-permute-done | bytes 32800 | tf_op jit(solution)/shard_map/ppermute | solution.py:25
  228.5 3.2 %collective-permute-done.21.refs_18_ = f32[16,2,256]{2,1,0:T(2,128)S(1)} collective-permute-done((f32[16,2,256]{2,1,0:T(2,128)}, f32[16,2,256]{2,1,0:T(2,128)S(1)}, u32[]{:S(2)}, u32[]{:S(2)}) %collective-permute-start.21) | collective-permute-done | bytes 32800 | tf_op jit(solution)/shard_map/ppermute | solution.py:25
  231.7 0.6 copy-done.18
  232.3 23.1 %shard_map.77 = (bf16[256,2048]{1,0:T(8,128)(2,1)}, bf16[256,2048]{1,0:T(8,128)(2,1)}) custom-call(s32[2,4]{1,0:T(2,128)} %copy-done.19, s32[2,4]{1,0:T(2,128)} %copy-done.20, bf16[256,2048]{1,0:T(8,128)(2,1)} %refs_2_.3, bf16[256,2048]{1,0:T(8,128)(2,1)} %refs_3_.3, bf16[256,2048]{1,0:T(8,128)(2,1)} %refs_4_.3, bf16[256,2048]{1,0:T(8,128)(2,1)} %refs_5_.1, ...), custom_call_target="tpu_custom_call" | custom-call | tf_op jit(solution)/shard_map/pallas_call | solution.py:150
  (62 shorter events, 0.4 us)
Async XLA Ops:
  2.0 8.4 %copy-start = (bf16[256,2048]{1,0:T(8,128)(2,1)S(1)}, bf16[256,2048]{1,0:T(8,128)(2,1)}, u32[]{:S(2)}) copy-start(bf16[256,2048]{1,0:T(8,128)(2,1)} %refs_4_.3) | copy-start | bytes 3145732
  2.0 24.2 %collective-permute-start = (bf16[128,2048]{1,0:T(8,128)(2,1)S(1)}, bf16[128,2048]{1,0:T(8,128)(2,1)S(1)}, u32[]{:S(2)}, u32[]{:S(2)}) collective-permute-start(bf16[128,2048]{1,0:T(8,128)(2,1)S(1)} %get-tuple-element.18), channel_id=1, source_target_pairs={{0,1},{1,2},{2,3},{3,4},{4,5},{5,6},{6,7},{7,8},{8,9},{9,10},{10,1... | collective-permute-start | bytes 1572872 | tf_op jit(solution)/shard_map/ppermute | solution.py:25
  2.6 24.1 %collective-permute-start.1 = (bf16[128,2048]{1,0:T(8,128)(2,1)S(1)}, bf16[128,2048]{1,0:T(8,128)(2,1)S(1)}, u32[]{:S(2)}, u32[]{:S(2)}) collective-permute-start(bf16[128,2048]{1,0:T(8,128)(2,1)S(1)} %get-tuple-element.16), channel_id=1, source_target_pairs={{0,1},{1,2},{2,3},{3,4},{4,5},{5,6},{6,7},{7,8},{8,9},{9,10},{10,1... | collective-permute-start | bytes 1572872 | tf_op jit(solution)/shard_map/ppermute | solution.py:25
  5.3 21.6 %collective-permute-start.2 = (bf16[128,2048]{1,0:T(8,128)(2,1)S(1)}, bf16[128,2048]{1,0:T(8,128)(2,1)S(1)}, u32[]{:S(2)}, u32[]{:S(2)}) collective-permute-start(bf16[128,2048]{1,0:T(8,128)(2,1)S(1)} %get-tuple-element.17), channel_id=1, source_target_pairs={{0,15},{1,0},{2,1},{3,2},{4,3},{5,4},{6,5},{7,6},{8,7},{9,8},{10,9... | collective-permute-start | bytes 1572872 | tf_op jit(solution)/shard_map/ppermute | solution.py:25
  7.8 20.4 %collective-permute-start.3 = (bf16[128,2048]{1,0:T(8,128)(2,1)S(1)}, bf16[128,2048]{1,0:T(8,128)(2,1)S(1)}, u32[]{:S(2)}, u32[]{:S(2)}) collective-permute-start(bf16[128,2048]{1,0:T(8,128)(2,1)S(1)} %get-tuple-element.15), channel_id=1, source_target_pairs={{0,15},{1,0},{2,1},{3,2},{4,3},{5,4},{6,5},{7,6},{8,7},{9,8},{10,9... | collective-permute-start | bytes 1572872 | tf_op jit(solution)/shard_map/ppermute | solution.py:25
  8.5 12.3 %collective-permute-start.8 = (s32[2,4]{1,0:T(2,128)S(1)}, s32[2,4]{1,0:T(2,128)S(1)}, u32[]{:S(2)}, u32[]{:S(2)}) collective-permute-start(s32[2,4]{1,0:T(2,128)S(1)} %copy-done.21), channel_id=1, source_target_pairs={{0,12},{1,13},{2,14},{3,15},{4,0},{5,1},{6,2},{7,3},{8,4},{9,5},{1... | collective-permute-start | bytes 104 | tf_op jit(solution)/shard_map/ppermute | solution.py:25
  10.6 16.2 %copy-start.2 = (bf16[256,2048]{1,0:T(8,128)(2,1)S(1)}, bf16[256,2048]{1,0:T(8,128)(2,1)}, u32[]{:S(2)}) copy-start(bf16[256,2048]{1,0:T(8,128)(2,1)} %refs_2_.3) | copy-start | bytes 3145732
  20.9 5.4 %collective-permute-start.9 = (s32[2,4]{1,0:T(2,128)S(1)}, s32[2,4]{1,0:T(2,128)S(1)}, u32[]{:S(2)}, u32[]{:S(2)}) collective-permute-start(s32[2,4]{1,0:T(2,128)S(1)} %copy-done.21), channel_id=1, source_target_pairs={{0,4},{1,5},{2,6},{3,7},{4,8},{5,9},{6,10},{7,11},{8,12},{9,13},{1... | collective-permute-start | bytes 104 | tf_op jit(solution)/shard_map/ppermute | solution.py:25
  26.2 13.8 %collective-permute-start.10 = (bf16[128,2048]{1,0:T(8,128)(2,1)S(1)}, bf16[128,2048]{1,0:T(8,128)(2,1)}, u32[]{:S(2)}, u32[]{:S(2)}) collective-permute-start(bf16[128,2048]{1,0:T(8,128)(2,1)S(1)} %get-tuple-element.14), channel_id=1, source_target_pairs={{0,1},{1,2},{2,3},{3,4},{4,5},{5,6},{6,7},{7,8},{8,9},{9,10},{10,1... | collective-permute-start | bytes 1572872 | tf_op jit(solution)/shard_map/ppermute | solution.py:25
  26.2 108.5 %copy-start.11 = (bf16[128,2048]{1,0:T(8,128)(2,1)}, bf16[128,2048]{1,0:T(8,128)(2,1)S(1)}, u32[]{:S(2)}) copy-start(bf16[128,2048]{1,0:T(8,128)(2,1)S(1)} %collective-permute-done.refs_5_) | copy-start | bytes 1572868
  26.8 24.4 %collective-permute-start.11 = (bf16[128,2048]{1,0:T(8,128)(2,1)S(1)}, bf16[128,2048]{1,0:T(8,128)(2,1)S(1)}, u32[]{:S(2)}, u32[]{:S(2)}) collective-permute-start(bf16[128,2048]{1,0:T(8,128)(2,1)S(1)} %get-tuple-element.12), channel_id=1, source_target_pairs={{0,1},{1,2},{2,3},{3,4},{4,5},{5,6},{6,7},{7,8},{8,9},{9,10},{10,1... | collective-permute-start | bytes 1572872 | tf_op jit(solution)/shard_map/ppermute | solution.py:25
  26.8 108.0 %copy-start.12 = (bf16[128,2048]{1,0:T(8,128)(2,1)}, bf16[128,2048]{1,0:T(8,128)(2,1)S(1)}, u32[]{:S(2)}) copy-start(bf16[128,2048]{1,0:T(8,128)(2,1)S(1)} %collective-permute-done.1.refs_6_) | copy-start | bytes 1572868
  26.8 105.8 %collective-permute-start.4 = (bf16[256,2048]{1,0:T(8,128)(2,1)S(1)}, bf16[256,2048]{1,0:T(8,128)(2,1)S(1)}, u32[]{:S(2)}, u32[]{:S(2)}) collective-permute-start(bf16[256,2048]{1,0:T(8,128)(2,1)S(1)} %copy-done.2), channel_id=1, source_target_pairs={{0,4},{1,5},{2,6},{3,7},{4,8},{5,9},{6,10},{7,11},{8,12},{9,13},{1... | collective-permute-start | bytes 3145736 | tf_op jit(solution)/shard_map/ppermute | solution.py:25
  26.9 107.9 %copy-start.13 = (bf16[128,2048]{1,0:T(8,128)(2,1)}, bf16[128,2048]{1,0:T(8,128)(2,1)S(1)}, u32[]{:S(2)}) copy-start(bf16[128,2048]{1,0:T(8,128)(2,1)S(1)} %collective-permute-done.2.refs_7_) | copy-start | bytes 1572868
  26.9 107.4 %collective-permute-start.5 = (bf16[256,2048]{1,0:T(8,128)(2,1)S(1)}, bf16[256,2048]{1,0:T(8,128)(2,1)S(1)}, u32[]{:S(2)}, u32[]{:S(2)}) collective-permute-start(bf16[256,2048]{1,0:T(8,128)(2,1)S(1)} %copy-done.3), channel_id=1, source_target_pairs={{0,4},{1,5},{2,6},{3,7},{4,8},{5,9},{6,10},{7,11},{8,12},{9,13},{1... | collective-permute-start | bytes 3145736 | tf_op jit(solution)/shard_map/ppermute | solution.py:25
  28.2 106.6 %copy-start.14 = (bf16[128,2048]{1,0:T(8,128)(2,1)}, bf16[128,2048]{1,0:T(8,128)(2,1)S(1)}, u32[]{:S(2)}) copy-start(bf16[128,2048]{1,0:T(8,128)(2,1)S(1)} %collective-permute-done.3.refs_8_) | copy-start | bytes 1572868
  28.2 106.5 %collective-permute-start.6 = (bf16[256,2048]{1,0:T(8,128)(2,1)S(1)}, bf16[256,2048]{1,0:T(8,128)(2,1)S(1)}, u32[]{:S(2)}, u32[]{:S(2)}) collective-permute-start(bf16[256,2048]{1,0:T(8,128)(2,1)S(1)} %copy-done.2), channel_id=1, source_target_pairs={{0,12},{1,13},{2,14},{3,15},{4,0},{5,1},{6,2},{7,3},{8,4},{9,5},{1... | collective-permute-start | bytes 3145736 | tf_op jit(solution)/shard_map/ppermute | solution.py:25
  40.0 94.8 %collective-permute-start.7 = (bf16[256,2048]{1,0:T(8,128)(2,1)S(1)}, bf16[256,2048]{1,0:T(8,128)(2,1)S(1)}, u32[]{:S(2)}, u32[]{:S(2)}) collective-permute-start(bf16[256,2048]{1,0:T(8,128)(2,1)S(1)} %copy-done.3), channel_id=1, source_target_pairs={{0,12},{1,13},{2,14},{3,15},{4,0},{5,1},{6,2},{7,3},{8,4},{9,5},{1... | collective-permute-start | bytes 3145736 | tf_op jit(solution)/shard_map/ppermute | solution.py:25
  51.1 83.7 %copy-start.9 = (bf16[128,2048]{1,0:T(8,128)(2,1)}, bf16[128,2048]{1,0:T(8,128)(2,1)S(1)}, u32[]{:S(2)}) copy-start(bf16[128,2048]{1,0:T(8,128)(2,1)S(1)} %collective-permute-done.11.refs_8_) | copy-start | bytes 1572868
  51.1 76.0 %collective-permute-start.13 = (bf16[128,2048]{1,0:T(8,128)(2,1)S(1)}, bf16[128,2048]{1,0:T(8,128)(2,1)S(1)}, u32[]{:S(2)}, u32[]{:S(2)}) collective-permute-start(bf16[128,2048]{1,0:T(8,128)(2,1)S(1)} %get-tuple-element.13), channel_id=1, source_target_pairs={{0,15},{1,0},{2,1},{3,2},{4,3},{5,4},{6,5},{7,6},{8,7},{9,8},{10,9... | collective-permute-start | bytes 1572872 | tf_op jit(solution)/shard_map/ppermute | solution.py:25
  127.1 7.7 %copy-start.10 = (bf16[128,2048]{1,0:T(8,128)(2,1)}, bf16[128,2048]{1,0:T(8,128)(2,1)S(1)}, u32[]{:S(2)}) copy-start(bf16[128,2048]{1,0:T(8,128)(2,1)S(1)} %collective-permute-done.13.refs_10_) | copy-start | bytes 1572868
  127.1 91.9 %collective-permute-start.16 = (bf16[256,2048]{1,0:T(8,128)(2,1)S(1)}, bf16[256,2048]{1,0:T(8,128)(2,1)}, u32[]{:S(2)}, u32[]{:S(2)}) collective-permute-start(bf16[256,2048]{1,0:T(8,128)(2,1)S(1)} %copy-done), channel_id=1, source_target_pairs={{0,12},{1,13},{2,14},{3,15},{4,0},{5,1},{6,2},{7,3},{8,4},{9,5},{1... | collective-permute-start | bytes 3145736 | tf_op jit(solution)/shard_map/ppermute | solution.py:25
  132.6 91.1 %collective-permute-start.17 = (bf16[256,2048]{1,0:T(8,128)(2,1)S(1)}, bf16[256,2048]{1,0:T(8,128)(2,1)}, u32[]{:S(2)}, u32[]{:S(2)}) collective-permute-start(bf16[256,2048]{1,0:T(8,128)(2,1)S(1)} %copy-done.1), channel_id=1, source_target_pairs={{0,12},{1,13},{2,14},{3,15},{4,0},{5,1},{6,2},{7,3},{8,4},{9,5},{1... | collective-permute-start | bytes 3145736 | tf_op jit(solution)/shard_map/ppermute | solution.py:25
  134.2 91.5 %collective-permute-start.19 = (bf16[256,2048]{1,0:T(8,128)(2,1)S(1)}, bf16[256,2048]{1,0:T(8,128)(2,1)}, u32[]{:S(2)}, u32[]{:S(2)}) collective-permute-start(bf16[256,2048]{1,0:T(8,128)(2,1)S(1)} %copy-done), channel_id=1, source_target_pairs={{0,4},{1,5},{2,6},{3,7},{4,8},{5,9},{6,10},{7,11},{8,12},{9,13},{1... | collective-permute-start | bytes 3145736 | tf_op jit(solution)/shard_map/ppermute | solution.py:25
  134.7 91.1 %collective-permute-start.20 = (bf16[256,2048]{1,0:T(8,128)(2,1)S(1)}, bf16[256,2048]{1,0:T(8,128)(2,1)S(1)}, u32[]{:S(2)}, u32[]{:S(2)}) collective-permute-start(bf16[256,2048]{1,0:T(8,128)(2,1)S(1)} %copy-done.1), channel_id=1, source_target_pairs={{0,4},{1,5},{2,6},{3,7},{4,8},{5,9},{6,10},{7,11},{8,12},{9,13},{1... | collective-permute-start | bytes 3145736 | tf_op jit(solution)/shard_map/ppermute | solution.py:25
  136.0 83.1 %collective-permute-start.14 = (bf16[128,2048]{1,0:T(8,128)(2,1)}, bf16[128,2048]{1,0:T(8,128)(2,1)}, u32[]{:S(2)}, u32[]{:S(2)}) collective-permute-start(bf16[128,2048]{1,0:T(8,128)(2,1)} %get-tuple-element.11), channel_id=1, source_target_pairs={{0,15},{1,0},{2,1},{3,2},{4,3},{5,4},{6,5},{7,6},{8,7},{9,8},{10,9... | collective-permute-start | bytes 1572872 | tf_op jit(solution)/shard_map/ppermute | solution.py:25
  219.1 6.7 %collective-permute-start.12 = (f32[16,2,256]{2,1,0:T(2,128)}, f32[16,2,256]{2,1,0:T(2,128)S(1)}, u32[]{:S(2)}, u32[]{:S(2)}) collective-permute-start(f32[16,2,256]{2,1,0:T(2,128)} %get-tuple-element.8.refs_6_), channel_id=1, source_target_pairs={{0,1},{1,2},{2,3},{3,4},{4,5},{5,6},{6,7},{7,8},{8,9},{9,10},{10,1... | collective-permute-start | bytes 98312 | tf_op jit(solution)/shard_map/ppermute | solution.py:25
  219.1 6.7 %collective-permute-start.15 = (f32[16,2,256]{2,1,0:T(2,128)}, f32[16,2,256]{2,1,0:T(2,128)S(1)}, u32[]{:S(2)}, u32[]{:S(2)}) collective-permute-start(f32[16,2,256]{2,1,0:T(2,128)} %get-tuple-element.8.refs_6_), channel_id=1, source_target_pairs={{0,15},{1,0},{2,1},{3,2},{4,3},{5,4},{6,5},{7,6},{8,7},{9,8},{10,9... | collective-permute-start | bytes 98312 | tf_op jit(solution)/shard_map/ppermute | solution.py:25
  223.7 4.8 %collective-permute-start.18 = (f32[16,2,256]{2,1,0:T(2,128)}, f32[16,2,256]{2,1,0:T(2,128)S(1)}, u32[]{:S(2)}, u32[]{:S(2)}) collective-permute-start(f32[16,2,256]{2,1,0:T(2,128)} %get-tuple-element.8.refs_6_), channel_id=1, source_target_pairs={{0,12},{1,13},{2,14},{3,15},{4,0},{5,1},{6,2},{7,3},{8,4},{9,5},{1... | collective-permute-start | bytes 98312 | tf_op jit(solution)/shard_map/ppermute | solution.py:25
  225.7 5.9 %collective-permute-start.21 = (f32[16,2,256]{2,1,0:T(2,128)}, f32[16,2,256]{2,1,0:T(2,128)S(1)}, u32[]{:S(2)}, u32[]{:S(2)}) collective-permute-start(f32[16,2,256]{2,1,0:T(2,128)} %get-tuple-element.8.refs_6_), channel_id=1, source_target_pairs={{0,4},{1,5},{2,6},{3,7},{4,8},{5,9},{6,10},{7,11},{8,12},{9,13},{1... | collective-permute-start | bytes 98312 | tf_op jit(solution)/shard_map/ppermute | solution.py:25
  225.8 5.9 %copy-start.4 = (bf16[256,2048]{1,0:T(8,128)(2,1)}, bf16[256,2048]{1,0:T(8,128)(2,1)S(1)}, u32[]{:S(2)}) copy-start(bf16[256,2048]{1,0:T(8,128)(2,1)S(1)} %collective-permute-done.20.refs_17_) | copy-start | bytes 3145732
  225.8 5.9 %copy-start.15 = (f32[16,2,256]{2,1,0:T(2,128)}, f32[16,2,256]{2,1,0:T(2,128)S(1)}, u32[]{:S(2)}) copy-start(f32[16,2,256]{2,1,0:T(2,128)S(1)} %collective-permute-done.12.refs_9_) | copy-start | bytes 98308
  (12 other events, 28.8 us)
where the time goes:
time: 256 us; the launch traced here: 255 us
  waiting for transfers between devices  131 us (51%)
  starting transfers between devices  74.4 us (29%)
  Pallas kernels  44.8 us (18%)
  local copies, waits for them, and re-layouts  4.82 us (2%)
    ppermute x22, waiting for transfers between devices, shifted(): return lax.ppermute(tree, axis, route)  131 us
    ppermute x22, starting transfers between devices, shifted(): return lax.ppermute(tree, axis, route)  74.4 us
    pallas_call x1, Pallas kernels, body(): pl.pallas_call(lambda *refs: key_kernel(*refs, scale=scale), grid_spec=pl...  23.1 us
    pallas_call x1, Pallas kernels, body(): pl.pallas_call(lambda *refs: query_kernel(*refs, scale=scale), grid_spec=...  21.7 us
  transfers between devices with their start and end apart: 22, of which 8 were waited for; matrix products, arithmetic and copies ran while one was open for 0% of the time, Pallas kernels for 8%

commit v1 on v0

v1 whole, which is shorter than its diff:
```python
import math

import jax
import jax.numpy as jnp
from jax import lax
from jax.experimental import pallas as pl
from jax.experimental.pallas import tpu as pltpu
from jax.sharding import PartitionSpec as P

BLK = 128
LOCAL_HEADS = 16
HEAD_SIZE = 128
FRAME_DEV = 4
BLK_DEV = 2

NT = (((1,), (1,)), ((), ()))
TN = (((0,), (0,)), ((), ()))
F32 = jnp.float32
BF16 = jnp.bfloat16


def shifted(tree, axis, distance):
    count = lax.axis_size(axis)
    route = [(i, (i + distance) % count) for i in range(count)]
    return lax.ppermute(tree, axis, route)


def row_block(ref, index):
    start = pl.multiple_of(index * BLK, BLK)
    return ref[pl.ds(start, BLK), :]


def query_kernel(kl_ref, qd_ref, kv_ref, left_ref, right_ref, early_ref, late_ref,
                 dq_ref, st_ref, *, scale):
    for i in range(BLK_DEV):
        rows = slice(i * BLK, (i + 1) * BLK)
        q = qd_ref[0, rows, :]
        do = qd_ref[1, rows, :]
        side = left_ref if i == 0 else right_ref
        early = lax.rem(kl_ref[i, 2], BLK_DEV)
        late = lax.rem(kl_ref[i, 3], BLK_DEV)
        parts = []
        for n in range(2):
            parts.append(jnp.concatenate(
                [kv_ref[n, rows, :], side[n], row_block(early_ref.at[n], early),
                 row_block(late_ref.at[n], late)], axis=0
            ))
        keys, vals = parts
        s = lax.dot_general(keys, q, NT, preferred_element_type=F32) * scale
        top = jnp.max(s, axis=0, keepdims=True)
        lse = top + jnp.log(jnp.sum(jnp.exp(s - top), axis=0, keepdims=True))
        p = jnp.exp(s - lse)
        p_low = p.astype(BF16)
        dp = lax.dot_general(vals, do, NT, preferred_element_type=F32)
        delta = jnp.sum(p_low.astype(F32) * dp, axis=0, keepdims=True)
        ds = (p * (dp - delta)).astype(BF16)
        dq = lax.dot_general(ds, keys, TN, preferred_element_type=F32) * scale
        dq_ref[rows, :] = dq.astype(BF16)
        st_ref[0, 0:1, rows] = lse
        st_ref[0, 1:2, rows] = delta


def key_terms(keys, vals, q, do, lse, delta, scale):
    s = lax.dot_general(keys, q, NT, preferred_element_type=F32) * scale
    p = jnp.exp(s - lse)
    p_low = p.astype(BF16)
    dp = lax.dot_general(vals, do, NT, preferred_element_type=F32)
    ds = (p * (dp - delta)).astype(BF16)
    d_value = jnp.dot(p_low, do, preferred_element_type=F32)
    d_key = jnp.dot(ds, q, preferred_element_type=F32)
    return d_key, d_value


def near_kernel(kv_ref, qd_ref, st_ref, left_ref, lst_ref, right_ref, rst_ref, acc_ref, *, scale):
    sides = ((left_ref, lst_ref, 1), (right_ref, rst_ref, 0))
    for j in range(BLK_DEV):
        rows = slice(j * BLK, (j + 1) * BLK)
        side, side_st, side_blk = sides[j]
        far = slice(side_blk * BLK, (side_blk + 1) * BLK)
        q = jnp.concatenate([qd_ref[0, rows, :], side[0]], axis=0)
        do = jnp.concatenate([qd_ref[1, rows, :], side[1]], axis=0)
        lse = jnp.concatenate([st_ref[0, 0:1, rows], side_st[0, 0:1, far]], axis=1)
        delta = jnp.concatenate([st_ref[0, 1:2, rows], side_st[0, 1:2, far]], axis=1)
        d_key, d_value = key_terms(kv_ref[0, rows, :], kv_ref[1, rows, :], q, do, lse, delta, scale)
        acc_ref[0, rows, :] = d_key
        acc_ref[1, rows, :] = d_value


def far_kernel(klp_ref, klm_ref, kv_ref, acc_in, pqd_ref, pst_ref, mqd_ref, mst_ref,
               dk_ref, dv_ref, acc_k, acc_v, *, scale):
    acc_k[...] = acc_in[0]
    acc_v[...] = acc_in[1]
    for kl_ref, column, rqd, rst in ((klp_ref, 2, pqd_ref, pst_ref), (klm_ref, 3, mqd_ref, mst_ref)):
        for r in range(BLK_DEV):
            rows = slice(r * BLK, (r + 1) * BLK)
            pick = lax.rem(kl_ref[r, column], BLK_DEV)
            start = pl.multiple_of(pick * BLK, BLK)
            mine = pl.ds(start, BLK)
            d_key, d_value = key_terms(
                kv_ref[0, mine, :], kv_ref[1, mine, :], rqd[0, rows, :], rqd[1, rows, :],
                rst[0, 0:1, rows], rst[0, 1:2, rows], scale,
            )
            acc_k[mine, :] += d_key
            acc_v[mine, :] += d_value
    dk_ref[...] = (acc_k[...] * scale).astype(BF16)
    dv_ref[...] = acc_v[...].astype(BF16)


def body(queries, keys, values, d_out, key_lists):
    rows, width = queries.shape
    heads = width // HEAD_SIZE
    assert rows == BLK_DEV * BLK and key_lists.shape[0] == BLK_DEV
    scale = 1.0 / math.sqrt(HEAD_SIZE)

    kv = jnp.stack([keys, values])
    qd = jnp.stack([queries, d_out])
    tail = slice(rows - BLK, rows)
    head = slice(0, BLK)
    left_kv, left_qd = shifted((kv[:, tail], qd[:, tail]), "seq", 1)
    right_kv, right_qd = shifted((kv[:, head], qd[:, head]), "seq", -1)
    early_kv, early_kl = shifted((kv, key_lists), "seq", FRAME_DEV)
    late_kv, late_kl = shifted((kv, key_lists), "seq", -FRAME_DEV)
    first_phase = (qd, left_kv, left_qd, right_kv, right_qd, early_kv, early_kl, late_kv, late_kl)
    (qd_send, left_kv, left_qd, right_kv, right_qd, early_kv, early_kl, late_kv,
     late_kl) = lax.optimization_barrier(first_phase)
    early_qd = shifted(qd_send, "seq", FRAME_DEV)
    late_qd = shifted(qd_send, "seq", -FRAME_DEV)

    full = pl.BlockSpec((2, rows, HEAD_SIZE), lambda h, *_: (0, 0, h))
    edge = pl.BlockSpec((2, BLK, HEAD_SIZE), lambda h, *_: (0, 0, h))
    stat = pl.BlockSpec((1, 2, rows), lambda h, *_: (h, 0, 0))
    out = pl.BlockSpec((rows, HEAD_SIZE), lambda h, *_: (0, h))

    d_queries, stats = pl.pallas_call(
        lambda *refs: query_kernel(*refs, scale=scale),
        grid_spec=pltpu.PrefetchScalarGridSpec(
            num_scalar_prefetch=1,
            grid=(heads,),
            in_specs=[full, full, edge, edge, full, full],
            out_specs=[out, stat],
        ),
        out_shape=[
            jax.ShapeDtypeStruct((rows, width), BF16),
            jax.ShapeDtypeStruct((heads, 2, rows), F32),
        ],
    )(key_lists, qd, kv, left_kv, right_kv, early_kv, late_kv)

    stats_left = shifted(stats, "seq", 1)
    stats_right = shifted(stats, "seq", -1)
    stats_early = shifted(stats, "seq", FRAME_DEV)
    stats_late = shifted(stats, "seq", -FRAME_DEV)

    near = pl.pallas_call(
        lambda *refs: near_kernel(*refs, scale=scale),
        grid=(heads,),
        in_specs=[full, full, stat, edge, stat, edge, stat],
        out_specs=full,
        out_shape=jax.ShapeDtypeStruct((2, rows, width), F32),
    )(kv, qd, stats, left_qd, stats_left, right_qd, stats_right)

    d_keys, d_values = pl.pallas_call(
        lambda *refs: far_kernel(*refs, scale=scale),
        grid_spec=pltpu.PrefetchScalarGridSpec(
            num_scalar_prefetch=2,
            grid=(heads,),
            in_specs=[full, full, full, stat, full, stat],
            out_specs=[out, out],
            scratch_shapes=[pltpu.VMEM((rows, HEAD_SIZE), F32), pltpu.VMEM((rows, HEAD_SIZE), F32)],
        ),
        out_shape=[
            jax.ShapeDtypeStruct((rows, width), BF16),
            jax.ShapeDtypeStruct((rows, width), BF16),
        ],
    )(late_kl, early_kl, kv, near, late_qd, stats_late, early_qd, stats_early)
    return (d_queries, d_keys, d_values)


def solution(mesh):
    spec = P(("groups", "seq"), None)
    return jax.shard_map(
        body,
        mesh=mesh,
        in_specs=(spec, spec, spec, spec, spec),
        out_specs=(spec, spec, spec),
        check_vma=False,
    )
```

time: 256 us -> 271 us (1.059); the launches traced: 255 us -> 267 us
  starting transfers between devices: 74.4 us -> 28.9 us
  waiting for transfers between devices: 131 us -> 174 us
  Pallas kernels: 44.8 us -> 54.5 us
  other arithmetic: 0 us -> 3.91 us
    ppermute x22 -> x14, starting transfers between devices: 74.4 us -> 28.9 us  [shifted(): return lax.ppermute(tree, axis, route)]
    ppermute x22 -> x14, waiting for transfers between devices: 131 us -> 174 us  [shifted(): return lax.ppermute(tree, axis, route)]
    pallas_call x1 -> x2, Pallas kernels: 23.1 us -> 33.1 us  [the longest x1 18.5 us: body(): pl.pallas_call(lambda *refs: far_kernel(*refs, scale=scale), grid_spec=pl...]
    another operation x0 -> x4, other arithmetic: none -> 3.91 us  [the longest x2 3.54 us: body(): qd = jnp.stack([queries, d_out])]
  transfers between devices with their start and end apart: 22 -> 14, of which waited for: 8 -> 4; matrix products, arithmetic and copies ran while one was open for 0% -> 1% of each run, Pallas kernels for 8% -> 14%
where the time goes in v1:
time: 271 us; the launch traced here: 267 us
  waiting for transfers between devices  174 us (64%)
  Pallas kernels  54.5 us (20%)
  starting transfers between devices  28.9 us (11%)
  local copies, waits for them, and re-layouts  4.69 us (2%)
  other arithmetic  3.91 us (1%)
    ppermute x14, waiting for transfers between devices, shifted(): return lax.ppermute(tree, axis, route)  174 us
    ppermute x14, starting transfers between devices, shifted(): return lax.ppermute(tree, axis, route)  28.9 us
    pallas_call x1, Pallas kernels, body(): pl.pallas_call(lambda *refs: query_kernel(*refs, scale=scale), grid_spec=...  21.4 us
    pallas_call x1, Pallas kernels, body(): pl.pallas_call(lambda *refs: far_kernel(*refs, scale=scale), grid_spec=pl...  18.5 us
    pallas_call x1, Pallas kernels, body(): pl.pallas_call(lambda *refs: near_kernel(*refs, scale=scale), grid=(heads...  14.7 us
  transfers between devices with their start and end apart: 14, of which 4 were waited for; matrix products, arithmetic and copies ran while one was open for 1% of the time, Pallas kernels for 14%

profile of v1, /device:TPU:0, one launch (start us, length us, event | category | flops | bytes accessed | tf_op | source)
XLA Modules:
  0.0 266.5 jit_solution(17730040026011996276)
XLA Ops:
  0.7 1.8 fusion.3
  2.5 5.5 %collective-permute-start.3 = (bf16[2,128,2048]{2,1,0:T(8,128)(2,1)S(1)}, bf16[2,128,2048]{2,1,0:T(8,128)(2,1)S(1)}, u32[]{:S(2)}, u32[]{:S(2)}) collective-permute-start(bf16[2,128,2048]{2,1,0:T(8,128)(2,1)S(1)} %get-tuple-element.29), channel_id=1, source_target_pairs={{0,15},{1,0},{2,1},{3,2},{4,3},{5,4},{6,5},{7,6},{8,7},{9,8},{10,9... | collective-permute-start | bytes 3145736 | tf_op jit(solution)/shard_map/ppermute | solution.py:25
  8.0 0.2 pad_maximum_fusion.1.refs_2_.refs_0_
  8.2 0.0 copy-start.3
  8.2 0.0 copy-start.4
  8.2 0.5 collective-permute-start.6
  8.7 1.6 collective-permute-start.4
  10.3 0.0 collective-permute-start.5
  10.3 3.8 %collective-permute-start.7 = (s32[2,4]{1,0:T(2,128)S(1)}, s32[2,4]{1,0:T(2,128)S(1)}, u32[]{:S(2)}, u32[]{:S(2)}) collective-permute-start(s32[2,4]{1,0:T(2,128)S(1)} %copy-done.18), channel_id=1, source_target_pairs={{0,12},{1,13},{2,14},{3,15},{4,0},{5,1},{6,2},{7,3},{8,4},{9,5},{1... | collective-permute-start | bytes 104 | tf_op jit(solution)/shard_map/ppermute | solution.py:25
  14.1 0.2 fusion.1
  14.3 96.3 %collective-permute-done.5.refs_1_ = s32[2,4]{1,0:T(2,128)S(1)} collective-permute-done((s32[2,4]{1,0:T(2,128)S(1)}, s32[2,4]{1,0:T(2,128)S(1)}, u32[]{:S(2)}, u32[]{:S(2)}) %collective-permute-start.5) | collective-permute-done | bytes 64 | tf_op jit(solution)/shard_map/ppermute | solution.py:25
  110.6 0.0 collective-permute-start.1
  110.6 0.0 collective-permute-done.7.refs_0_
  110.6 4.4 %collective-permute-start.2 = (bf16[2,128,2048]{2,1,0:T(8,128)(2,1)S(1)}, bf16[2,128,2048]{2,1,0:T(8,128)(2,1)S(1)}, u32[]{:S(2)}, u32[]{:S(2)}) collective-permute-start(bf16[2,128,2048]{2,1,0:T(8,128)(2,1)S(1)} %get-tuple-element.31), channel_id=1, source_target_pairs={{0,15},{1,0},{2,1},{3,2},{4,3},{5,4},{6,5},{7,6},{8,7},{9,8},{10,9... | collective-permute-start | bytes 3145736 | tf_op jit(solution)/shard_map/ppermute | solution.py:25
  115.1 0.0 collective-permute-done.3.refs_5_
  115.1 1.7 pad_maximum_fusion.refs_1_
  116.8 10.7 %collective-permute-done.1.refs_3_ = bf16[2,128,2048]{2,1,0:T(8,128)(2,1)S(1)} collective-permute-done((bf16[2,128,2048]{2,1,0:T(8,128)(2,1)S(1)}, bf16[2,128,2048]{2,1,0:T(8,128)(2,1)S(1)}, u32[]{:S(2)}, u32[]{:S(2)}) %collective-permute-start.1) | collective-permute-done | bytes 1048608 | tf_op jit(solution)/shard_map/ppermute | solution.py:25
  127.5 11.2 %collective-permute-done.refs_3_ = bf16[2,128,2048]{2,1,0:T(8,128)(2,1)S(1)} collective-permute-done((bf16[2,128,2048]{2,1,0:T(8,128)(2,1)S(1)}, bf16[2,128,2048]{2,1,0:T(8,128)(2,1)S(1)}, u32[]{:S(2)}, u32[]{:S(2)}) %collective-permute-start) | collective-permute-done | bytes 1048608 | tf_op jit(solution)/shard_map/ppermute | solution.py:25
  138.8 1.3 copy-done.5
  140.1 0.3 copy-done.11
  140.4 1.0 copy-done.6
  141.5 2.6 collective-permute-start.10
  144.0 21.4 %shard_map.76 = (bf16[256,2048]{1,0:T(8,128)(2,1)}, f32[16,2,256]{2,1,0:T(2,128)}) custom-call(s32[2,4]{1,0:T(2,128)} %refs_0_.1, bf16[2,256,2048]{2,1,0:T(8,128)(2,1)} %pad_maximum_fusion.refs_1_, bf16[2,256,2048]{2,1,0:T(8,128)(2,1)} %copy-done, bf16[2,128,2048]{2,1,0:T(8,128)(2,1)} %copy-done.11, bf16[2,128,2048]{2,1,0:T(8,128)(2,1)} %copy-done.10, ...), custom_call_target="tpu_custom_call" | custom-call | tf_op jit(solution)/shard_map/pallas_call | solution.py:134
  165.4 6.4 %collective-permute-start.8 = (f32[16,2,256]{2,1,0:T(2,128)}, f32[16,2,256]{2,1,0:T(2,128)S(1)}, u32[]{:S(2)}, u32[]{:S(2)}) collective-permute-start(f32[16,2,256]{2,1,0:T(2,128)} %get-tuple-element.23.refs_2_), channel_id=1, source_target_pairs={{0,1},{1,2},{2,3},{3,4},{4,5},{5,6},{6,7},{7,8},{8,9},{9,10},{10,1... | collective-permute-start | bytes 98312 | tf_op jit(solution)/shard_map/ppermute | solution.py:25
  171.8 55.3 %collective-permute-done.9.refs_6_ = f32[16,2,256]{2,1,0:T(2,128)S(1)} collective-permute-done((f32[16,2,256]{2,1,0:T(2,128)}, f32[16,2,256]{2,1,0:T(2,128)S(1)}, u32[]{:S(2)}, u32[]{:S(2)}) %collective-permute-start.9) | collective-permute-done | bytes 32800 | tf_op jit(solution)/shard_map/ppermute | solution.py:25
  227.1 4.2 %collective-permute-start.11 = (f32[16,2,256]{2,1,0:T(2,128)}, f32[16,2,256]{2,1,0:T(2,128)S(1)}, u32[]{:S(2)}, u32[]{:S(2)}) collective-permute-start(f32[16,2,256]{2,1,0:T(2,128)} %get-tuple-element.23.refs_2_), channel_id=1, source_target_pairs={{0,12},{1,13},{2,14},{3,15},{4,0},{5,1},{6,2},{7,3},{8,4},{9,5},{1... | collective-permute-start | bytes 98312 | tf_op jit(solution)/shard_map/ppermute | solution.py:25
  231.4 0.6 copy-done.15
  232.0 14.7 %shard_map.77.refs_3_ = f32[2,256,2048]{2,1,0:T(8,128)} custom-call(bf16[2,256,2048]{2,1,0:T(8,128)(2,1)} %copy-done, bf16[2,256,2048]{2,1,0:T(8,128)(2,1)} %pad_maximum_fusion.refs_1_, f32[16,2,256]{2,1,0:T(2,128)} %get-tuple-element.23.refs_2_, bf16[2,128,2048]{2,1,0:T(8,128)(2,1)} %copy-done.9, f32[16,2,256]{2,1,0:T(2,128)} %copy-done.15, ...), custom_call_target="tpu_custom_call" | custom-call | tf_op jit(solution)/shard_map/pallas_call | solution.py:153
  246.7 0.6 copy-done.12
  247.3 0.0 copy-done.13
  247.3 0.8 copy-done.7
  248.0 18.5 %shard_map.78 = (bf16[256,2048]{1,0:T(8,128)(2,1)}, bf16[256,2048]{1,0:T(8,128)(2,1)}) custom-call(s32[2,4]{1,0:T(2,128)} %copy-done.17, s32[2,4]{1,0:T(2,128)} %copy-done.16, bf16[2,256,2048]{2,1,0:T(8,128)(2,1)} %copy-done, f32[2,256,2048]{2,1,0:T(8,128)} %shard_map.77.refs_3_, bf16[2,256,2048]{2,1,0:T(8,128)(2,1)} %collective-permute-done.10.refs_4_, ...), custom_call_target="tpu_custom_call" | custom-call | tf_op jit(solution)/shard_map/pallas_call | solution.py:161
  (41 shorter events, 0.1 us)
Async XLA Ops:
  0.6 7.3 %copy-start.1 = (bf16[256,2048]{1,0:T(8,128)(2,1)S(1)}, bf16[256,2048]{1,0:T(8,128)(2,1)}, u32[]{:S(2)}) copy-start(bf16[256,2048]{1,0:T(8,128)(2,1)} %param.7) | copy-start | bytes 3145732
  0.6 7.3 %copy-start.2 = (bf16[256,2048]{1,0:T(8,128)(2,1)S(1)}, bf16[256,2048]{1,0:T(8,128)(2,1)}, u32[]{:S(2)}) copy-start(bf16[256,2048]{1,0:T(8,128)(2,1)} %param.6) | copy-start | bytes 3145732
  2.5 112.6 %collective-permute-start.3 = (bf16[2,128,2048]{2,1,0:T(8,128)(2,1)S(1)}, bf16[2,128,2048]{2,1,0:T(8,128)(2,1)S(1)}, u32[]{:S(2)}, u32[]{:S(2)}) collective-permute-start(bf16[2,128,2048]{2,1,0:T(8,128)(2,1)S(1)} %get-tuple-element.29), channel_id=1, source_target_pairs={{0,15},{1,0},{2,1},{3,2},{4,3},{5,4},{6,5},{7,6},{8,7},{9,8},{10,9... | collective-permute-start | bytes 3145736 | tf_op jit(solution)/shard_map/ppermute | solution.py:25
  8.0 2.3 copy-start.18
  8.2 102.4 %copy-start = (bf16[2,256,2048]{2,1,0:T(8,128)(2,1)}, bf16[2,256,2048]{2,1,0:T(8,128)(2,1)S(1)}, u32[]{:S(2)}) copy-start(bf16[2,256,2048]{2,1,0:T(8,128)(2,1)S(1)} %pad_maximum_fusion.1.refs_2_.refs_0_) | copy-start | bytes 6291460
  8.2 106.9 %copy-start.3 = (bf16[256,2048]{1,0:T(8,128)(2,1)S(1)}, bf16[256,2048]{1,0:T(8,128)(2,1)}, u32[]{:S(2)}) copy-start(bf16[256,2048]{1,0:T(8,128)(2,1)} %param.8) | copy-start | bytes 3145732
  8.2 106.9 %copy-start.4 = (bf16[256,2048]{1,0:T(8,128)(2,1)S(1)}, bf16[256,2048]{1,0:T(8,128)(2,1)}, u32[]{:S(2)}) copy-start(bf16[256,2048]{1,0:T(8,128)(2,1)} %param.5) | copy-start | bytes 3145732
  8.2 130.6 %collective-permute-start.6 = (bf16[2,256,2048]{2,1,0:T(8,128)(2,1)S(1)}, bf16[2,256,2048]{2,1,0:T(8,128)(2,1)S(1)}, u32[]{:S(2)}, u32[]{:S(2)}) collective-permute-start(bf16[2,256,2048]{2,1,0:T(8,128)(2,1)S(1)} %pad_maximum_fusion.1.refs_2_.refs_0_), channel_id=1, source_target_pairs={{0,12},{1,13},{2,14},{3,15},{4,0},{5,1},{6,2},{7,3},{8,4},{9,5},{1... | collective-permute-start | bytes 6291464 | tf_op jit(solution)/shard_map/ppermute | solution.py:25
  8.7 130.1 %collective-permute-start.4 = (bf16[2,256,2048]{2,1,0:T(8,128)(2,1)S(1)}, bf16[2,256,2048]{2,1,0:T(8,128)(2,1)S(1)}, u32[]{:S(2)}, u32[]{:S(2)}) collective-permute-start(bf16[2,256,2048]{2,1,0:T(8,128)(2,1)S(1)} %pad_maximum_fusion.1.refs_2_.refs_0_), channel_id=1, source_target_pairs={{0,4},{1,5},{2,6},{3,7},{4,8},{5,9},{6,10},{7,11},{8,12},{9,13},{1... | collective-permute-start | bytes 6291464 | tf_op jit(solution)/shard_map/ppermute | solution.py:25
  10.3 100.3 %collective-permute-start.5 = (s32[2,4]{1,0:T(2,128)S(1)}, s32[2,4]{1,0:T(2,128)S(1)}, u32[]{:S(2)}, u32[]{:S(2)}) collective-permute-start(s32[2,4]{1,0:T(2,128)S(1)} %copy-done.18), channel_id=1, source_target_pairs={{0,4},{1,5},{2,6},{3,7},{4,8},{5,9},{6,10},{7,11},{8,12},{9,13},{1... | collective-permute-start | bytes 104 | tf_op jit(solution)/shard_map/ppermute | solution.py:25
  10.3 100.3 %collective-permute-start.7 = (s32[2,4]{1,0:T(2,128)S(1)}, s32[2,4]{1,0:T(2,128)S(1)}, u32[]{:S(2)}, u32[]{:S(2)}) collective-permute-start(s32[2,4]{1,0:T(2,128)S(1)} %copy-done.18), channel_id=1, source_target_pairs={{0,12},{1,13},{2,14},{3,15},{4,0},{5,1},{6,2},{7,3},{8,4},{9,5},{1... | collective-permute-start | bytes 104 | tf_op jit(solution)/shard_map/ppermute | solution.py:25
  110.6 6.2 %copy-start.16 = (s32[2,4]{1,0:T(2,128)}, s32[2,4]{1,0:T(2,128)S(1)}, u32[]{:S(2)}) copy-start(s32[2,4]{1,0:T(2,128)S(1)} %collective-permute-done.5.refs_1_) | copy-start | bytes 100
  110.6 16.9 %collective-permute-start.1 = (bf16[2,128,2048]{2,1,0:T(8,128)(2,1)S(1)}, bf16[2,128,2048]{2,1,0:T(8,128)(2,1)S(1)}, u32[]{:S(2)}, u32[]{:S(2)}) collective-permute-start(bf16[2,128,2048]{2,1,0:T(8,128)(2,1)S(1)} %get-tuple-element.30), channel_id=1, source_target_pairs={{0,1},{1,2},{2,3},{3,4},{4,5},{5,6},{6,7},{7,8},{8,9},{9,10},{10,1... | collective-permute-start | bytes 3145736 | tf_op jit(solution)/shard_map/ppermute | solution.py:25
  110.6 6.2 %copy-start.17 = (s32[2,4]{1,0:T(2,128)}, s32[2,4]{1,0:T(2,128)S(1)}, u32[]{:S(2)}) copy-start(s32[2,4]{1,0:T(2,128)S(1)} %collective-permute-done.7.refs_0_) | copy-start | bytes 100
  110.6 16.9 %collective-permute-start.2 = (bf16[2,128,2048]{2,1,0:T(8,128)(2,1)S(1)}, bf16[2,128,2048]{2,1,0:T(8,128)(2,1)S(1)}, u32[]{:S(2)}, u32[]{:S(2)}) collective-permute-start(bf16[2,128,2048]{2,1,0:T(8,128)(2,1)S(1)} %get-tuple-element.31), channel_id=1, source_target_pairs={{0,15},{1,0},{2,1},{3,2},{4,3},{5,4},{6,5},{7,6},{8,7},{9,8},{10,9... | collective-permute-start | bytes 3145736 | tf_op jit(solution)/shard_map/ppermute | solution.py:25
  115.1 1.7 copy-start.8
  115.1 23.7 %collective-permute-start = (bf16[2,128,2048]{2,1,0:T(8,128)(2,1)S(1)}, bf16[2,128,2048]{2,1,0:T(8,128)(2,1)S(1)}, u32[]{:S(2)}, u32[]{:S(2)}) collective-permute-start(bf16[2,128,2048]{2,1,0:T(8,128)(2,1)S(1)} %get-tuple-element.32), channel_id=1, source_target_pairs={{0,1},{1,2},{2,3},{3,4},{4,5},{5,6},{6,7},{7,8},{8,9},{9,10},{10,1... | collective-permute-start | bytes 3145736 | tf_op jit(solution)/shard_map/ppermute | solution.py:25
  127.5 12.6 %copy-start.9 = (bf16[2,128,2048]{2,1,0:T(8,128)(2,1)}, bf16[2,128,2048]{2,1,0:T(8,128)(2,1)S(1)}, u32[]{:S(2)}) copy-start(bf16[2,128,2048]{2,1,0:T(8,128)(2,1)S(1)} %collective-permute-done.1.refs_3_) | copy-start | bytes 3145732
  127.5 12.6 %copy-start.10 = (bf16[2,128,2048]{2,1,0:T(8,128)(2,1)}, bf16[2,128,2048]{2,1,0:T(8,128)(2,1)S(1)}, u32[]{:S(2)}) copy-start(bf16[2,128,2048]{2,1,0:T(8,128)(2,1)S(1)} %collective-permute-done.2.refs_4_) | copy-start | bytes 3145732
  138.8 1.7 copy-start.11
  138.8 1.3 copy-start.5
  140.1 1.3 copy-start.6
  140.1 106.5 %collective-permute-start.12 = (bf16[2,256,2048]{2,1,0:T(8,128)(2,1)}, bf16[2,256,2048]{2,1,0:T(8,128)(2,1)S(1)}, u32[]{:S(2)}, u32[]{:S(2)}) collective-permute-start(bf16[2,256,2048]{2,1,0:T(8,128)(2,1)} %pad_maximum_fusion.refs_1_), channel_id=1, source_target_pairs={{0,4},{1,5},{2,6},{3,7},{4,8},{5,9},{6,10},{7,11},{8,12},{9,13},{1... | collective-permute-start | bytes 6291464 | tf_op jit(solution)/shard_map/ppermute | solution.py:25
  141.5 105.2 %collective-permute-start.10 = (bf16[2,256,2048]{2,1,0:T(8,128)(2,1)}, bf16[2,256,2048]{2,1,0:T(8,128)(2,1)}, u32[]{:S(2)}, u32[]{:S(2)}) collective-permute-start(bf16[2,256,2048]{2,1,0:T(8,128)(2,1)} %pad_maximum_fusion.refs_1_), channel_id=1, source_target_pairs={{0,12},{1,13},{2,14},{3,15},{4,0},{5,1},{6,2},{7,3},{8,4},{9,5},{1... | collective-permute-start | bytes 6291464 | tf_op jit(solution)/shard_map/ppermute | solution.py:25
  165.4 61.7 %collective-permute-start.9 = (f32[16,2,256]{2,1,0:T(2,128)}, f32[16,2,256]{2,1,0:T(2,128)S(1)}, u32[]{:S(2)}, u32[]{:S(2)}) collective-permute-start(f32[16,2,256]{2,1,0:T(2,128)} %get-tuple-element.23.refs_2_), channel_id=1, source_target_pairs={{0,15},{1,0},{2,1},{3,2},{4,3},{5,4},{6,5},{7,6},{8,7},{9,8},{10,9... | collective-permute-start | bytes 98312 | tf_op jit(solution)/shard_map/ppermute | solution.py:25
  165.4 65.9 %collective-permute-start.8 = (f32[16,2,256]{2,1,0:T(2,128)}, f32[16,2,256]{2,1,0:T(2,128)S(1)}, u32[]{:S(2)}, u32[]{:S(2)}) collective-permute-start(f32[16,2,256]{2,1,0:T(2,128)} %get-tuple-element.23.refs_2_), channel_id=1, source_target_pairs={{0,1},{1,2},{2,3},{3,4},{4,5},{5,6},{6,7},{7,8},{8,9},{9,10},{10,1... | collective-permute-start | bytes 98312 | tf_op jit(solution)/shard_map/ppermute | solution.py:25
  171.8 74.8 %collective-permute-start.13 = (f32[16,2,256]{2,1,0:T(2,128)}, f32[16,2,256]{2,1,0:T(2,128)S(1)}, u32[]{:S(2)}, u32[]{:S(2)}) collective-permute-start(f32[16,2,256]{2,1,0:T(2,128)} %get-tuple-element.23.refs_2_), channel_id=1, source_target_pairs={{0,4},{1,5},{2,6},{3,7},{4,8},{5,9},{6,10},{7,11},{8,12},{9,13},{1... | collective-permute-start | bytes 98312 | tf_op jit(solution)/shard_map/ppermute | solution.py:25
  227.1 4.2 %copy-start.14 = (f32[16,2,256]{2,1,0:T(2,128)}, f32[16,2,256]{2,1,0:T(2,128)S(1)}, u32[]{:S(2)}) copy-start(f32[16,2,256]{2,1,0:T(2,128)S(1)} %collective-permute-done.9.refs_6_) | copy-start | bytes 98308
  227.1 19.5 %collective-permute-start.11 = (f32[16,2,256]{2,1,0:T(2,128)}, f32[16,2,256]{2,1,0:T(2,128)S(1)}, u32[]{:S(2)}, u32[]{:S(2)}) collective-permute-start(f32[16,2,256]{2,1,0:T(2,128)} %get-tuple-element.23.refs_2_), channel_id=1, source_target_pairs={{0,12},{1,13},{2,14},{3,15},{4,0},{5,1},{6,2},{7,3},{8,4},{9,5},{1... | collective-permute-start | bytes 98312 | tf_op jit(solution)/shard_map/ppermute | solution.py:25
  231.4 0.6 copy-start.15
  246.7 0.6 copy-start.13
  246.7 1.4 copy-start.7
  (1 other events, 0.6 us)

commit v2 on v1

--- a/solution.py
+++ b/solution.py
@@ -58,6 +58,8 @@
         dq_ref[rows, :] = dq.astype(BF16)
         st_ref[0, 0:1, rows] = lse
         st_ref[0, 1:2, rows] = delta
+        st_ref[0, 2:3, rows] = jnp.full((1, BLK), early.astype(F32), F32)
+        st_ref[0, 3:4, rows] = jnp.full((1, BLK), late.astype(F32), F32)
 
 
 def key_terms(keys, vals, q, do, lse, delta, scale):
@@ -86,24 +88,39 @@
         acc_ref[1, rows, :] = d_value
 
 
-def far_kernel(klp_ref, klm_ref, kv_ref, acc_in, pqd_ref, pst_ref, mqd_ref, mst_ref,
-               dk_ref, dv_ref, acc_k, acc_v, *, scale):
-    acc_k[...] = acc_in[0]
-    acc_v[...] = acc_in[1]
-    for kl_ref, column, rqd, rst in ((klp_ref, 2, pqd_ref, pst_ref), (klm_ref, 3, mqd_ref, mst_ref)):
-        for r in range(BLK_DEV):
-            rows = slice(r * BLK, (r + 1) * BLK)
-            pick = lax.rem(kl_ref[r, column], BLK_DEV)
-            start = pl.multiple_of(pick * BLK, BLK)
-            mine = pl.ds(start, BLK)
-            d_key, d_value = key_terms(
-                kv_ref[0, mine, :], kv_ref[1, mine, :], rqd[0, rows, :], rqd[1, rows, :],
-                rst[0, 0:1, rows], rst[0, 1:2, rows], scale,
-            )
-            acc_k[mine, :] += d_key
-            acc_v[mine, :] += d_value
-    dk_ref[...] = (acc_k[...] * scale).astype(BF16)
-    dv_ref[...] = acc_v[...].astype(BF16)
+def far_kernel(kv_ref, acc_in, rqd_ref, rst_ref, *outs, scale, column, last):
+    acc = [[acc_in[n, j * BLK:(j + 1) * BLK, :] for j in range(BLK_DEV)] for n in range(2)]
+    for r in range(BLK_DEV):
+        rows = slice(r * BLK, (r + 1) * BLK)
+        pick = rst_ref[0, column:column + 1, rows]
+        first = pick == 0.0
+        keys = jnp.where(first, kv_ref[0, 0:BLK, :], kv_ref[0, BLK:2 * BLK, :])
+        vals = jnp.where(first, kv_ref[1, 0:BLK, :], kv_ref[1, BLK:2 * BLK, :])
+        terms = key_terms(
+            keys, vals, rqd_ref[0, rows, :], rqd_ref[1, rows, :],
+            rst_ref[0, 0:1, rows], rst_ref[0, 1:2, rows], scale,
+        )
+        for n in range(2):
+            acc[n][0] = acc[n][0] + jnp.where(first, terms[n], 0.0)
+            acc[n][1] = acc[n][1] + jnp.where(first, 0.0, terms[n])
+    if last:
+        dk_ref, dv_ref = outs
+        for j in range(BLK_DEV):
+            rows = slice(j * BLK, (j + 1) * BLK)
+            dk_ref[rows, :] = (acc[0][j] * scale).astype(BF16)
+            dv_ref[rows, :] = acc[1][j].astype(BF16)
+    else:
+        (acc_out,) = outs
+        for n in range(2):
+            for j in range(BLK_DEV):
+                acc_out[n, j * BLK:(j + 1) * BLK, :] = acc[n][j]
+
+
+def cost(heads, block_products, exp_blocks, bytes_accessed):
+    flops = 2 * BLK * BLK * HEAD_SIZE * block_products * heads
+    return pl.CostEstimate(
+        flops=flops, transcendentals=BLK * BLK * exp_blocks * heads, bytes_accessed=bytes_accessed
+    )
 
 
 def body(queries, keys, values, d_out, key_lists):
@@ -118,17 +135,16 @@
     head = slice(0, BLK)
     left_kv, left_qd = shifted((kv[:, tail], qd[:, tail]), "seq", 1)
     right_kv, right_qd = shifted((kv[:, head], qd[:, head]), "seq", -1)
-    early_kv, early_kl = shifted((kv, key_lists), "seq", FRAME_DEV)
-    late_kv, late_kl = shifted((kv, key_lists), "seq", -FRAME_DEV)
-    first_phase = (qd, left_kv, left_qd, right_kv, right_qd, early_kv, early_kl, late_kv, late_kl)
-    (qd_send, left_kv, left_qd, right_kv, right_qd, early_kv, early_kl, late_kv,
-     late_kl) = lax.optimization_barrier(first_phase)
-    early_qd = shifted(qd_send, "seq", FRAME_DEV)
+    kv_send, qd_send, left_kv, left_qd, right_kv, right_qd = lax.optimization_barrier(
+        (kv, qd, left_kv, left_qd, right_kv, right_qd)
+    )
+    early_kv = shifted(kv_send, "seq", FRAME_DEV)
+    late_kv = shifted(kv_send, "seq", -FRAME_DEV)
     late_qd = shifted(qd_send, "seq", -FRAME_DEV)
 
     full = pl.BlockSpec((2, rows, HEAD_SIZE), lambda h, *_: (0, 0, h))
     edge = pl.BlockSpec((2, BLK, HEAD_SIZE), lambda h, *_: (0, 0, h))
-    stat = pl.BlockSpec((1, 2, rows), lambda h, *_: (h, 0, 0))
+    stat = pl.BlockSpec((1, 4, rows), lambda h, *_: (h, 0, 0))
     out = pl.BlockSpec((rows, HEAD_SIZE), lambda h, *_: (0, h))
 
     d_queries, stats = pl.pallas_call(
@@ -141,14 +157,19 @@
         ),
         out_shape=[
             jax.ShapeDtypeStruct((rows, width), BF16),
-            jax.ShapeDtypeStruct((heads, 2, rows), F32),
+            jax.ShapeDtypeStruct((heads, 4, rows), F32),
         ],
+        cost_estimate=cost(heads, 24, 8, 14 * rows * width),
     )(key_lists, qd, kv, left_kv, right_kv, early_kv, late_kv)
 
     stats_left = shifted(stats, "seq", 1)
     stats_right = shifted(stats, "seq", -1)
     stats_early = shifted(stats, "seq", FRAME_DEV)
     stats_late = shifted(stats, "seq", -FRAME_DEV)
+    qd_send, stats_left, stats_right, stats_early, stats_late = lax.optimization_barrier(
+        (qd, stats_left, stats_right, stats_early, stats_late)
+    )
+    early_qd = shifted(qd_send, "seq", FRAME_DEV)
 
     near = pl.pallas_call(
         lambda *refs: near_kernel(*refs, scale=scale),
@@ -156,22 +177,30 @@
         in_specs=[full, full, stat, edge, stat, edge, stat],
         out_specs=full,
         out_shape=jax.ShapeDtypeStruct((2, rows, width), F32),
+        cost_estimate=cost(heads, 16, 4, 14 * rows * width),
     )(kv, qd, stats, left_qd, stats_left, right_qd, stats_right)
 
+    near = pl.pallas_call(
+        lambda *refs: far_kernel(*refs, scale=scale, column=2, last=False),
+        grid=(heads,),
+        in_specs=[full, full, full, stat],
+        out_specs=full,
+        out_shape=jax.ShapeDtypeStruct((2, rows, width), F32),
+        input_output_aliases={1: 0},
+        cost_estimate=cost(heads, 8, 2, 16 * rows * width),
+    )(kv, near, late_qd, stats_late)
+
     d_keys, d_values = pl.pallas_call(
-        lambda *refs: far_kernel(*refs, scale=scale),
-        grid_spec=pltpu.PrefetchScalarGridSpec(
-            num_scalar_prefetch=2,
-            grid=(heads,),
-            in_specs=[full, full, full, stat, full, stat],
-            out_specs=[out, out],
-            scratch_shapes=[pltpu.VMEM((rows, HEAD_SIZE), F32), pltpu.VMEM((rows, HEAD_SIZE), F32)],
-        ),
+        lambda *refs: far_kernel(*refs, scale=scale, column=3, last=True),
+        grid=(heads,),
+        in_specs=[full, full, full, stat],
+        out_specs=[out, out],
         out_shape=[
             jax.ShapeDtypeStruct((rows, width), BF16),
             jax.ShapeDtypeStruct((rows, width), BF16),
         ],
-    )(late_kl, early_kl, kv, near, late_qd, stats_late, early_qd, stats_early)
+        cost_estimate=cost(heads, 8, 2, 16 * rows * width),
+    )(kv, near, early_qd, stats_early)
     return (d_queries, d_keys, d_values)
 
 

time: 271 us -> 263 us (0.970); the launches traced: 267 us -> 262 us
  waiting for transfers between devices: 174 us -> 150 us
  Pallas kernels: 54.5 us -> 64.7 us
  starting transfers between devices: 28.9 us -> 37.7 us
    ppermute x14 -> x12, waiting for transfers between devices: 174 us -> 150 us  [shifted(): return lax.ppermute(tree, axis, route)]
    pallas_call x1 -> x2, Pallas kernels: 18.5 us -> 28.7 us  [the longest x1 14.5 us: body(): pl.pallas_call(lambda *refs: far_kernel(*refs, scale=scale, column=2, las...]
    ppermute x14 -> x12, starting transfers between devices: 28.9 us -> 37.7 us  [shifted(): return lax.ppermute(tree, axis, route)]
  transfers between devices with their start and end apart: 14 -> 12, of which waited for: 4 -> 10; matrix products, arithmetic and copies ran while one was open for 1% -> 1% of each run, Pallas kernels for 14% -> 11%
where the time goes in v2:
time: 263 us; the launch traced here: 262 us
  waiting for transfers between devices  150 us (57%)
  Pallas kernels  64.7 us (25%)
  starting transfers between devices  37.7 us (14%)
  local copies, waits for them, and re-layouts  4.63 us (2%)
  other arithmetic  3.92 us (1%)
    ppermute x12, waiting for transfers between devices, shifted(): return lax.ppermute(tree, axis, route)  150 us
    ppermute x12, starting transfers between devices, shifted(): return lax.ppermute(tree, axis, route)  37.7 us
    pallas_call x1, Pallas kernels, body(): pl.pallas_call(lambda *refs: query_kernel(*refs, scale=scale), grid_spec=...  21.4 us
    pallas_call x1, Pallas kernels, body(): pl.pallas_call(lambda *refs: near_kernel(*refs, scale=scale), grid=(heads...  14.6 us
    pallas_call x1, Pallas kernels, body(): pl.pallas_call(lambda *refs: far_kernel(*refs, scale=scale, column=2, las...  14.5 us
    pallas_call x1, Pallas kernels, body(): pl.pallas_call(lambda *refs: far_kernel(*refs, scale=scale, column=3, las...  14.2 us
  transfers between devices with their start and end apart: 12, of which 10 were waited for; matrix products, arithmetic and copies ran while one was open for 1% of the time, Pallas kernels for 11%

profile of v2, /device:TPU:0, one launch (start us, length us, event | category | flops | bytes accessed | tf_op | source)
XLA Modules:
  0.0 261.7 jit_solution(11748485914814850506)
XLA Ops:
  0.7 1.8 fusion.3
  2.5 5.5 %collective-permute-start.3 = (bf16[2,128,2048]{2,1,0:T(8,128)(2,1)S(1)}, bf16[2,128,2048]{2,1,0:T(8,128)(2,1)S(1)}, u32[]{:S(2)}, u32[]{:S(2)}) collective-permute-start(bf16[2,128,2048]{2,1,0:T(8,128)(2,1)S(1)} %get-tuple-element.33), channel_id=1, source_target_pairs={{0,15},{1,0},{2,1},{3,2},{4,3},{5,4},{6,5},{7,6},{8,7},{9,8},{10,9... | collective-permute-start | bytes 3145736 | tf_op jit(solution)/shard_map/ppermute | solution.py:25
  8.0 0.2 fusion.1
  8.2 4.5 %collective-permute-start.2 = (bf16[2,128,2048]{2,1,0:T(8,128)(2,1)S(1)}, bf16[2,128,2048]{2,1,0:T(8,128)(2,1)S(1)}, u32[]{:S(2)}, u32[]{:S(2)}) collective-permute-start(bf16[2,128,2048]{2,1,0:T(8,128)(2,1)S(1)} %get-tuple-element.35), channel_id=1, source_target_pairs={{0,15},{1,0},{2,1},{3,2},{4,3},{5,4},{6,5},{7,6},{8,7},{9,8},{10,9... | collective-permute-start | bytes 3145736 | tf_op jit(solution)/shard_map/ppermute | solution.py:25
  12.7 0.0 collective-permute-start
  12.7 0.2 pad_maximum_fusion.1.refs_2_.refs_0_
  12.9 1.0 copy-done.3
  13.9 0.3 copy-done.4
  14.2 1.7 pad_maximum_fusion.refs_1_
  15.9 4.4 %collective-permute-done.3.refs_5_ = bf16[2,128,2048]{2,1,0:T(8,128)(2,1)S(1)} collective-permute-done((bf16[2,128,2048]{2,1,0:T(8,128)(2,1)S(1)}, bf16[2,128,2048]{2,1,0:T(8,128)(2,1)S(1)}, u32[]{:S(2)}, u32[]{:S(2)}) %collective-permute-start.3) | collective-permute-done | bytes 1048608 | tf_op jit(solution)/shard_map/ppermute | solution.py:25
  20.3 4.7 %collective-permute-done.1.refs_3_ = bf16[2,128,2048]{2,1,0:T(8,128)(2,1)S(1)} collective-permute-done((bf16[2,128,2048]{2,1,0:T(8,128)(2,1)S(1)}, bf16[2,128,2048]{2,1,0:T(8,128)(2,1)S(1)}, u32[]{:S(2)}, u32[]{:S(2)}) %collective-permute-start.1) | collective-permute-done | bytes 1048608 | tf_op jit(solution)/shard_map/ppermute | solution.py:25
  25.0 6.5 %collective-permute-done.2.refs_4_ = bf16[2,128,2048]{2,1,0:T(8,128)(2,1)S(1)} collective-permute-done((bf16[2,128,2048]{2,1,0:T(8,128)(2,1)S(1)}, bf16[2,128,2048]{2,1,0:T(8,128)(2,1)S(1)}, u32[]{:S(2)}, u32[]{:S(2)}) %collective-permute-start.2) | collective-permute-done | bytes 1048608 | tf_op jit(solution)/shard_map/ppermute | solution.py:25
  31.5 4.8 %collective-permute-done.refs_3_ = bf16[2,128,2048]{2,1,0:T(8,128)(2,1)S(1)} collective-permute-done((bf16[2,128,2048]{2,1,0:T(8,128)(2,1)S(1)}, bf16[2,128,2048]{2,1,0:T(8,128)(2,1)S(1)}, u32[]{:S(2)}, u32[]{:S(2)}) %collective-permute-start) | collective-permute-done | bytes 1048608 | tf_op jit(solution)/shard_map/ppermute | solution.py:25
  36.3 2.0 collective-permute-start.4
  38.4 39.7 %collective-permute-done.5.refs_6_ = bf16[2,256,2048]{2,1,0:T(8,128)(2,1)S(1)} collective-permute-done((bf16[2,256,2048]{2,1,0:T(8,128)(2,1)S(1)}, bf16[2,256,2048]{2,1,0:T(8,128)(2,1)S(1)}, u32[]{:S(2)}, u32[]{:S(2)}) %collective-permute-start.5) | collective-permute-done | bytes 2097184 | tf_op jit(solution)/shard_map/ppermute | solution.py:25
  78.1 1.3 copy-done.6
  79.4 29.4 %collective-permute-done.4.refs_5_ = bf16[2,256,2048]{2,1,0:T(8,128)(2,1)} collective-permute-done((bf16[2,256,2048]{2,1,0:T(8,128)(2,1)S(1)}, bf16[2,256,2048]{2,1,0:T(8,128)(2,1)}, u32[]{:S(2)}, u32[]{:S(2)}) %collective-permute-start.4) | collective-permute-done | bytes 2097184 | tf_op jit(solution)/shard_map/ppermute | solution.py:25
  108.8 21.4 %shard_map.76 = (bf16[256,2048]{1,0:T(8,128)(2,1)}, f32[16,4,256]{2,1,0:T(4,128)}) custom-call(s32[2,4]{1,0:T(2,128)} %refs_0_.1, bf16[2,256,2048]{2,1,0:T(8,128)(2,1)} %pad_maximum_fusion.refs_1_, bf16[2,256,2048]{2,1,0:T(8,128)(2,1)} %copy-done, bf16[2,128,2048]{2,1,0:T(8,128)(2,1)} %copy-done.10, bf16[2,128,2048]{2,1,0:T(8,128)(2,1)} %copy-done.9, ...), custom_call_target="tpu_custom_call" | custom-call | flops 1610612736 | bytes 7340032 | tf_op jit(solution)/shard_map/pallas_call | solution.py:150
  130.2 17.1 %collective-permute-start.9 = (f32[16,4,256]{2,1,0:T(4,128)}, f32[16,4,256]{2,1,0:T(4,128)S(1)}, u32[]{:S(2)}, u32[]{:S(2)}) collective-permute-start(f32[16,4,256]{2,1,0:T(4,128)} %get-tuple-element.22.refs_2_), channel_id=1, source_target_pairs={{0,12},{1,13},{2,14},{3,15},{4,0},{5,1},{6,2},{7,3},{8,4},{9,5},{1... | collective-permute-start | bytes 196616 | tf_op jit(solution)/shard_map/ppermute | solution.py:25
  147.3 2.8 %collective-permute-start.8 = (f32[16,4,256]{2,1,0:T(4,128)}, f32[16,4,256]{2,1,0:T(4,128)S(1)}, u32[]{:S(2)}, u32[]{:S(2)}) collective-permute-start(f32[16,4,256]{2,1,0:T(4,128)} %get-tuple-element.22.refs_2_), channel_id=1, source_target_pairs={{0,4},{1,5},{2,6},{3,7},{4,8},{5,9},{6,10},{7,11},{8,12},{9,13},{1... | collective-permute-start | bytes 196616 | tf_op jit(solution)/shard_map/ppermute | solution.py:25
  150.1 1.6 collective-permute-start.7
  151.8 2.0 collective-permute-start.6
  153.8 2.1 collective-permute-start.10
  155.9 0.9 collective-permute-done.8.refs_3_
  156.8 1.7 collective-permute-done.6.refs_4_
  158.6 0.6 copy-done.14
  159.2 14.6 %shard_map.77.refs_1_ = f32[2,256,2048]{2,1,0:T(8,128)} custom-call(bf16[2,256,2048]{2,1,0:T(8,128)(2,1)} %copy-done, bf16[2,256,2048]{2,1,0:T(8,128)(2,1)} %pad_maximum_fusion.refs_1_, f32[16,4,256]{2,1,0:T(4,128)} %get-tuple-element.22.refs_2_, bf16[2,128,2048]{2,1,0:T(8,128)(2,1)} %copy-done.8, f32[16,4,256]{2,1,0:T(4,128)} %copy-done.14, ...), custom_call_target="tpu_custom_call" | custom-call | flops 1073741824 | bytes 7340032 | tf_op jit(solution)/shard_map/pallas_call | solution.py:174
  173.8 29.0 %collective-permute-done.10.refs_2_ = bf16[2,256,2048]{2,1,0:T(8,128)(2,1)S(1)} collective-permute-done((bf16[2,256,2048]{2,1,0:T(8,128)(2,1)}, bf16[2,256,2048]{2,1,0:T(8,128)(2,1)S(1)}, u32[]{:S(2)}, u32[]{:S(2)}) %collective-permute-start.10) | collective-permute-done | bytes 2097184 | tf_op jit(solution)/shard_map/ppermute | solution.py:25
  202.8 1.4 copy-done.5
  204.2 14.5 %shard_map.78.refs_1_ = f32[2,256,2048]{2,1,0:T(8,128)} custom-call(bf16[2,256,2048]{2,1,0:T(8,128)(2,1)} %copy-done, f32[2,256,2048]{2,1,0:T(8,128)} %shard_map.77.refs_1_, bf16[2,256,2048]{2,1,0:T(8,128)(2,1)} %copy-done.5, f32[16,4,256]{2,1,0:T(4,128)} %copy-done.12), custom_call_target="tpu_custom_call", output_to_operand_aliasing={{}: (1, {})} | custom-call | flops 536870912 | bytes 8388608 | tf_op jit(solution)/shard_map/pallas_call | solution.py:183
  218.7 28.8 %collective-permute-done.11.refs_2_ = bf16[2,256,2048]{2,1,0:T(8,128)(2,1)} collective-permute-done((bf16[2,256,2048]{2,1,0:T(8,128)(2,1)}, bf16[2,256,2048]{2,1,0:T(8,128)(2,1)}, u32[]{:S(2)}, u32[]{:S(2)}) %collective-permute-start.11) | collective-permute-done | bytes 2097184 | tf_op jit(solution)/shard_map/ppermute | solution.py:25
  247.5 14.2 %shard_map.79 = (bf16[256,2048]{1,0:T(8,128)(2,1)}, bf16[256,2048]{1,0:T(8,128)(2,1)}) custom-call(bf16[2,256,2048]{2,1,0:T(8,128)(2,1)} %copy-done, f32[2,256,2048]{2,1,0:T(8,128)} %shard_map.78.refs_1_, bf16[2,256,2048]{2,1,0:T(8,128)(2,1)} %collective-permute-done.11.refs_2_, f32[16,4,256]{2,1,0:T(4,128)} %copy-done.11), custom_call_target="tpu_custom_call" | custom-call | flops 536870912 | bytes 8388608 | tf_op jit(solution)/shard_map/pallas_call | solution.py:193
  (30 shorter events, 0.1 us)
Async XLA Ops:
  0.6 7.3 %copy-start.1 = (bf16[256,2048]{1,0:T(8,128)(2,1)S(1)}, bf16[256,2048]{1,0:T(8,128)(2,1)}, u32[]{:S(2)}) copy-start(bf16[256,2048]{1,0:T(8,128)(2,1)} %param.7) | copy-start | bytes 3145732
  0.6 7.3 %copy-start.2 = (bf16[256,2048]{1,0:T(8,128)(2,1)S(1)}, bf16[256,2048]{1,0:T(8,128)(2,1)}, u32[]{:S(2)}) copy-start(bf16[256,2048]{1,0:T(8,128)(2,1)} %param.6) | copy-start | bytes 3145732
  2.5 17.8 %collective-permute-start.3 = (bf16[2,128,2048]{2,1,0:T(8,128)(2,1)S(1)}, bf16[2,128,2048]{2,1,0:T(8,128)(2,1)S(1)}, u32[]{:S(2)}, u32[]{:S(2)}) collective-permute-start(bf16[2,128,2048]{2,1,0:T(8,128)(2,1)S(1)} %get-tuple-element.33), channel_id=1, source_target_pairs={{0,15},{1,0},{2,1},{3,2},{4,3},{5,4},{6,5},{7,6},{8,7},{9,8},{10,9... | collective-permute-start | bytes 3145736 | tf_op jit(solution)/shard_map/ppermute | solution.py:25
  8.0 17.0 %collective-permute-start.1 = (bf16[2,128,2048]{2,1,0:T(8,128)(2,1)S(1)}, bf16[2,128,2048]{2,1,0:T(8,128)(2,1)S(1)}, u32[]{:S(2)}, u32[]{:S(2)}) collective-permute-start(bf16[2,128,2048]{2,1,0:T(8,128)(2,1)S(1)} %get-tuple-element.34), channel_id=1, source_target_pairs={{0,1},{1,2},{2,3},{3,4},{4,5},{5,6},{6,7},{7,8},{8,9},{9,10},{10,1... | collective-permute-start | bytes 3145736 | tf_op jit(solution)/shard_map/ppermute | solution.py:25
  8.2 23.4 %collective-permute-start.2 = (bf16[2,128,2048]{2,1,0:T(8,128)(2,1)S(1)}, bf16[2,128,2048]{2,1,0:T(8,128)(2,1)S(1)}, u32[]{:S(2)}, u32[]{:S(2)}) collective-permute-start(bf16[2,128,2048]{2,1,0:T(8,128)(2,1)S(1)} %get-tuple-element.35), channel_id=1, source_target_pairs={{0,15},{1,0},{2,1},{3,2},{4,3},{5,4},{6,5},{7,6},{8,7},{9,8},{10,9... | collective-permute-start | bytes 3145736 | tf_op jit(solution)/shard_map/ppermute | solution.py:25
  12.7 1.2 copy-start.3
  12.7 1.5 copy-start.4
  12.7 23.7 %collective-permute-start = (bf16[2,128,2048]{2,1,0:T(8,128)(2,1)S(1)}, bf16[2,128,2048]{2,1,0:T(8,128)(2,1)S(1)}, u32[]{:S(2)}, u32[]{:S(2)}) collective-permute-start(bf16[2,128,2048]{2,1,0:T(8,128)(2,1)S(1)} %get-tuple-element.36), channel_id=1, source_target_pairs={{0,1},{1,2},{2,3},{3,4},{4,5},{5,6},{6,7},{7,8},{8,9},{9,10},{10,1... | collective-permute-start | bytes 3145736 | tf_op jit(solution)/shard_map/ppermute | solution.py:25
  14.2 94.6 %copy-start = (bf16[2,256,2048]{2,1,0:T(8,128)(2,1)}, bf16[2,256,2048]{2,1,0:T(8,128)(2,1)S(1)}, u32[]{:S(2)}) copy-start(bf16[2,256,2048]{2,1,0:T(8,128)(2,1)S(1)} %pad_maximum_fusion.1.refs_2_.refs_0_) | copy-start | bytes 6291460
  20.3 138.3 %copy-start.7 = (bf16[2,128,2048]{2,1,0:T(8,128)(2,1)}, bf16[2,128,2048]{2,1,0:T(8,128)(2,1)S(1)}, u32[]{:S(2)}) copy-start(bf16[2,128,2048]{2,1,0:T(8,128)(2,1)S(1)} %collective-permute-done.3.refs_5_) | copy-start | bytes 3145732
  25.0 53.1 %copy-start.8 = (bf16[2,128,2048]{2,1,0:T(8,128)(2,1)}, bf16[2,128,2048]{2,1,0:T(8,128)(2,1)S(1)}, u32[]{:S(2)}) copy-start(bf16[2,128,2048]{2,1,0:T(8,128)(2,1)S(1)} %collective-permute-done.1.refs_3_) | copy-start | bytes 3145732
  31.5 46.6 %copy-start.9 = (bf16[2,128,2048]{2,1,0:T(8,128)(2,1)}, bf16[2,128,2048]{2,1,0:T(8,128)(2,1)S(1)}, u32[]{:S(2)}) copy-start(bf16[2,128,2048]{2,1,0:T(8,128)(2,1)S(1)} %collective-permute-done.2.refs_4_) | copy-start | bytes 3145732
  36.3 41.8 %copy-start.10 = (bf16[2,128,2048]{2,1,0:T(8,128)(2,1)}, bf16[2,128,2048]{2,1,0:T(8,128)(2,1)S(1)}, u32[]{:S(2)}) copy-start(bf16[2,128,2048]{2,1,0:T(8,128)(2,1)S(1)} %collective-permute-done.refs_3_) | copy-start | bytes 3145732
  36.3 41.8 %collective-permute-start.5 = (bf16[2,256,2048]{2,1,0:T(8,128)(2,1)S(1)}, bf16[2,256,2048]{2,1,0:T(8,128)(2,1)S(1)}, u32[]{:S(2)}, u32[]{:S(2)}) collective-permute-start(bf16[2,256,2048]{2,1,0:T(8,128)(2,1)S(1)} %pad_maximum_fusion.1.refs_2_.refs_0_), channel_id=1, source_target_pairs={{0,12},{1,13},{2,14},{3,15},{4,0},{5,1},{6,2},{7,3},{8,4},{9,5},{1... | collective-permute-start | bytes 6291464 | tf_op jit(solution)/shard_map/ppermute | solution.py:25
  36.3 72.4 %collective-permute-start.4 = (bf16[2,256,2048]{2,1,0:T(8,128)(2,1)S(1)}, bf16[2,256,2048]{2,1,0:T(8,128)(2,1)}, u32[]{:S(2)}, u32[]{:S(2)}) collective-permute-start(bf16[2,256,2048]{2,1,0:T(8,128)(2,1)S(1)} %pad_maximum_fusion.1.refs_2_.refs_0_), channel_id=1, source_target_pairs={{0,4},{1,5},{2,6},{3,7},{4,8},{5,9},{6,10},{7,11},{8,12},{9,13},{1... | collective-permute-start | bytes 6291464 | tf_op jit(solution)/shard_map/ppermute | solution.py:25
  78.1 1.3 copy-start.6
  130.2 25.8 %collective-permute-start.9 = (f32[16,4,256]{2,1,0:T(4,128)}, f32[16,4,256]{2,1,0:T(4,128)S(1)}, u32[]{:S(2)}, u32[]{:S(2)}) collective-permute-start(f32[16,4,256]{2,1,0:T(4,128)} %get-tuple-element.22.refs_2_), channel_id=1, source_target_pairs={{0,12},{1,13},{2,14},{3,15},{4,0},{5,1},{6,2},{7,3},{8,4},{9,5},{1... | collective-permute-start | bytes 196616 | tf_op jit(solution)/shard_map/ppermute | solution.py:25
  147.3 9.5 %collective-permute-start.8 = (f32[16,4,256]{2,1,0:T(4,128)}, f32[16,4,256]{2,1,0:T(4,128)S(1)}, u32[]{:S(2)}, u32[]{:S(2)}) collective-permute-start(f32[16,4,256]{2,1,0:T(4,128)} %get-tuple-element.22.refs_2_), channel_id=1, source_target_pairs={{0,4},{1,5},{2,6},{3,7},{4,8},{5,9},{6,10},{7,11},{8,12},{9,13},{1... | collective-permute-start | bytes 196616 | tf_op jit(solution)/shard_map/ppermute | solution.py:25
  150.1 6.7 %collective-permute-start.7 = (f32[16,4,256]{2,1,0:T(4,128)}, f32[16,4,256]{2,1,0:T(4,128)S(1)}, u32[]{:S(2)}, u32[]{:S(2)}) collective-permute-start(f32[16,4,256]{2,1,0:T(4,128)} %get-tuple-element.22.refs_2_), channel_id=1, source_target_pairs={{0,15},{1,0},{2,1},{3,2},{4,3},{5,4},{6,5},{7,6},{8,7},{9,8},{10,9... | collective-permute-start | bytes 196616 | tf_op jit(solution)/shard_map/ppermute | solution.py:25
  151.8 6.8 %collective-permute-start.6 = (f32[16,4,256]{2,1,0:T(4,128)}, f32[16,4,256]{2,1,0:T(4,128)S(1)}, u32[]{:S(2)}, u32[]{:S(2)}) collective-permute-start(f32[16,4,256]{2,1,0:T(4,128)} %get-tuple-element.22.refs_2_), channel_id=1, source_target_pairs={{0,1},{1,2},{2,3},{3,4},{4,5},{5,6},{6,7},{7,8},{8,9},{9,10},{10,1... | collective-permute-start | bytes 196616 | tf_op jit(solution)/shard_map/ppermute | solution.py:25
  153.8 49.0 %collective-permute-start.10 = (bf16[2,256,2048]{2,1,0:T(8,128)(2,1)}, bf16[2,256,2048]{2,1,0:T(8,128)(2,1)S(1)}, u32[]{:S(2)}, u32[]{:S(2)}) collective-permute-start(bf16[2,256,2048]{2,1,0:T(8,128)(2,1)} %pad_maximum_fusion.refs_1_), channel_id=1, source_target_pairs={{0,12},{1,13},{2,14},{3,15},{4,0},{5,1},{6,2},{7,3},{8,4},{9,5},{1... | collective-permute-start | bytes 6291464 | tf_op jit(solution)/shard_map/ppermute | solution.py:25
  155.9 17.8 %copy-start.12 = (f32[16,4,256]{2,1,0:T(4,128)}, f32[16,4,256]{2,1,0:T(4,128)S(1)}, u32[]{:S(2)}) copy-start(f32[16,4,256]{2,1,0:T(4,128)S(1)} %collective-permute-done.9.refs_3_) | copy-start | bytes 196612
  156.8 17.0 %copy-start.11 = (f32[16,4,256]{2,1,0:T(4,128)}, f32[16,4,256]{2,1,0:T(4,128)S(1)}, u32[]{:S(2)}) copy-start(f32[16,4,256]{2,1,0:T(4,128)S(1)} %collective-permute-done.8.refs_3_) | copy-start | bytes 196612
  156.8 1.7 copy-start.13
  158.5 0.6 copy-start.14
  158.5 89.0 %collective-permute-start.11 = (bf16[2,256,2048]{2,1,0:T(8,128)(2,1)}, bf16[2,256,2048]{2,1,0:T(8,128)(2,1)}, u32[]{:S(2)}, u32[]{:S(2)}) collective-permute-start(bf16[2,256,2048]{2,1,0:T(8,128)(2,1)} %pad_maximum_fusion.refs_1_), channel_id=1, source_target_pairs={{0,4},{1,5},{2,6},{3,7},{4,8},{5,9},{6,10},{7,11},{8,12},{9,13},{1... | collective-permute-start | bytes 6291464 | tf_op jit(solution)/shard_map/ppermute | solution.py:25
  202.8 1.4 copy-start.5

commit v3 on v2

v3 whole, which is shorter than its diff:
```python
import math

import jax
import jax.numpy as jnp
from jax import lax
from jax.experimental import pallas as pl
from jax.experimental.pallas import tpu as pltpu
from jax.sharding import PartitionSpec as P

BLK = 128
LOCAL_HEADS = 16
HEAD_SIZE = 128
FRAME_DEV = 4
BLK_DEV = 2
STEP_HEADS = 4

NT = (((1,), (1,)), ((), ()))
TN = (((0,), (0,)), ((), ()))
F32 = jnp.float32
BF16 = jnp.bfloat16


def shifted(tree, axis, distance):
    count = lax.axis_size(axis)
    route = [(i, (i + distance) % count) for i in range(count)]
    return lax.ppermute(tree, axis, route)


def cols(hh):
    return slice(hh * HEAD_SIZE, (hh + 1) * HEAD_SIZE)


def row_block(ref, index, hh):
    start = pl.multiple_of(index * BLK, BLK)
    return ref[pl.ds(start, BLK), cols(hh)]


def query_kernel(kl_ref, qd_ref, kv_ref, left_ref, right_ref, early_ref, late_ref,
                 dq_ref, st_ref, *, scale):
    for i in range(BLK_DEV):
        rows = slice(i * BLK, (i + 1) * BLK)
        side = left_ref if i == 0 else right_ref
        early = lax.rem(kl_ref[i, 2], BLK_DEV)
        late = lax.rem(kl_ref[i, 3], BLK_DEV)
        for hh in range(STEP_HEADS):
            c = cols(hh)
            q = qd_ref[0, rows, c]
            do = qd_ref[1, rows, c]
            parts = []
            for n in range(2):
                parts.append(jnp.concatenate(
                    [kv_ref[n, rows, c], side[n, :, c], row_block(early_ref.at[n], early, hh),
                     row_block(late_ref.at[n], late, hh)], axis=0
                ))
            keys, vals = parts
            s = lax.dot_general(keys, q, NT, preferred_element_type=F32) * scale
            top = jnp.max(s, axis=0, keepdims=True)
            lse = top + jnp.log(jnp.sum(jnp.exp(s - top), axis=0, keepdims=True))
            p = jnp.exp(s - lse)
            p_low = p.astype(BF16)
            dp = lax.dot_general(vals, do, NT, preferred_element_type=F32)
            delta = jnp.sum(p_low.astype(F32) * dp, axis=0, keepdims=True)
            ds = (p * (dp - delta)).astype(BF16)
            dq = lax.dot_general(ds, keys, TN, preferred_element_type=F32) * scale
            dq_ref[rows, c] = dq.astype(BF16)
            st_ref[hh, 0:1, rows] = lse
            st_ref[hh, 1:2, rows] = delta
            st_ref[hh, 2:3, rows] = jnp.full((1, BLK), early.astype(F32), F32)
            st_ref[hh, 3:4, rows] = jnp.full((1, BLK), late.astype(F32), F32)


def key_terms(keys, vals, q, do, lse, delta, scale):
    s = lax.dot_general(keys, q, NT, preferred_element_type=F32) * scale
    p = jnp.exp(s - lse)
    p_low = p.astype(BF16)
    dp = lax.dot_general(vals, do, NT, preferred_element_type=F32)
    ds = (p * (dp - delta)).astype(BF16)
    d_value = jnp.dot(p_low, do, preferred_element_type=F32)
    d_key = jnp.dot(ds, q, preferred_element_type=F32)
    return d_key, d_value


def near_kernel(kv_ref, qd_ref, st_ref, left_ref, lst_ref, right_ref, rst_ref, acc_ref, *, scale):
    sides = ((left_ref, lst_ref, 1), (right_ref, rst_ref, 0))
    for j in range(BLK_DEV):
        rows = slice(j * BLK, (j + 1) * BLK)
        side, side_st, side_blk = sides[j]
        far = slice(side_blk * BLK, (side_blk + 1) * BLK)
        for hh in range(STEP_HEADS):
            c = cols(hh)
            q = jnp.concatenate([qd_ref[0, rows, c], side[0, :, c]], axis=0)
            do = jnp.concatenate([qd_ref[1, rows, c], side[1, :, c]], axis=0)
            lse = jnp.concatenate([st_ref[hh, 0:1, rows], side_st[hh, 0:1, far]], axis=1)
            delta = jnp.concatenate([st_ref[hh, 1:2, rows], side_st[hh, 1:2, far]], axis=1)
            d_key, d_value = key_terms(kv_ref[0, rows, c], kv_ref[1, rows, c], q, do, lse, delta, scale)
            acc_ref[0, rows, c] = d_key
            acc_ref[1, rows, c] = d_value


def far_kernel(kv_ref, acc_in, rqd_ref, rst_ref, *outs, scale, column, last):
    for hh in range(STEP_HEADS):
        c = cols(hh)
        acc = [[acc_in[n, j * BLK:(j + 1) * BLK, c] for j in range(BLK_DEV)] for n in range(2)]
        for r in range(BLK_DEV):
            rows = slice(r * BLK, (r + 1) * BLK)
            first = rst_ref[hh, column:column + 1, rows] == 0.0
            keys = jnp.where(first, kv_ref[0, 0:BLK, c], kv_ref[0, BLK:2 * BLK, c])
            vals = jnp.where(first, kv_ref[1, 0:BLK, c], kv_ref[1, BLK:2 * BLK, c])
            terms = key_terms(
                keys, vals, rqd_ref[0, rows, c], rqd_ref[1, rows, c],
                rst_ref[hh, 0:1, rows], rst_ref[hh, 1:2, rows], scale,
            )
            for n in range(2):
                acc[n][0] = acc[n][0] + jnp.where(first, terms[n], 0.0)
                acc[n][1] = acc[n][1] + jnp.where(first, 0.0, terms[n])
        for j in range(BLK_DEV):
            rows = slice(j * BLK, (j + 1) * BLK)
            if last:
                dk_ref, dv_ref = outs
                dk_ref[rows, c] = (acc[0][j] * scale).astype(BF16)
                dv_ref[rows, c] = acc[1][j].astype(BF16)
            else:
                (acc_out,) = outs
                acc_out[0, rows, c] = acc[0][j]
                acc_out[1, rows, c] = acc[1][j]


def cost(steps, block_products, exp_blocks, bytes_accessed):
    heads = steps * STEP_HEADS
    flops = 2 * BLK * BLK * HEAD_SIZE * block_products * heads
    return pl.CostEstimate(
        flops=flops, transcendentals=BLK * BLK * exp_blocks * heads, bytes_accessed=bytes_accessed
    )


def body(queries, keys, values, d_out, key_lists):
    rows, width = queries.shape
    steps = width // (HEAD_SIZE * STEP_HEADS)
    assert rows == BLK_DEV * BLK and key_lists.shape[0] == BLK_DEV
    assert steps * HEAD_SIZE * STEP_HEADS == width
    scale = 1.0 / math.sqrt(HEAD_SIZE)

    kvqd = jnp.stack([keys, values, queries, d_out])
    left = shifted(kvqd[:, rows - BLK:], "seq", 1)
    right = shifted(kvqd[:, :BLK], "seq", -1)
    kvqd_send, left, right = lax.optimization_barrier((kvqd, left, right))
    early_kv = shifted(kvqd_send[:2], "seq", FRAME_DEV)
    late = shifted(kvqd_send, "seq", -FRAME_DEV)
    qd_send, early_kv, late = lax.optimization_barrier((kvqd[2:], early_kv, late))

    width_step = HEAD_SIZE * STEP_HEADS
    first = pl.BlockSpec((2, rows, width_step), lambda h, *_: (0, 0, h))
    second = pl.BlockSpec((2, rows, width_step), lambda h, *_: (1, 0, h))
    edge_first = pl.BlockSpec((2, BLK, width_step), lambda h, *_: (0, 0, h))
    edge_second = pl.BlockSpec((2, BLK, width_step), lambda h, *_: (1, 0, h))
    stat = pl.BlockSpec((STEP_HEADS, 4, rows), lambda h, *_: (h, 0, 0))
    out = pl.BlockSpec((rows, width_step), lambda h, *_: (0, h))
    heads = steps * STEP_HEADS
    array_bytes = rows * width * 2

    d_queries, stats = pl.pallas_call(
        lambda *refs: query_kernel(*refs, scale=scale),
        grid_spec=pltpu.PrefetchScalarGridSpec(
            num_scalar_prefetch=1,
            grid=(steps,),
            in_specs=[second, first, edge_first, edge_first, first, first],
            out_specs=[out, stat],
        ),
        out_shape=[
            jax.ShapeDtypeStruct((rows, width), BF16),
            jax.ShapeDtypeStruct((heads, 4, rows), F32),
        ],
        cost_estimate=cost(steps, 24, 8, 11 * array_bytes),
    )(key_lists, kvqd, kvqd, left, right, early_kv, late)

    stats_left = shifted(stats, "seq", 1)
    stats_right = shifted(stats, "seq", -1)
    stats_early = shifted(stats, "seq", FRAME_DEV)
    stats_late = shifted(stats, "seq", -FRAME_DEV)
    qd_send, stats_left, stats_right, stats_early, stats_late = lax.optimization_barrier(
        (qd_send, stats_left, stats_right, stats_early, stats_late)
    )
    early_qd = shifted(qd_send, "seq", FRAME_DEV)

    near = pl.pallas_call(
        lambda *refs: near_kernel(*refs, scale=scale),
        grid=(steps,),
        in_specs=[first, second, stat, edge_second, stat, edge_second, stat],
        out_specs=first,
        out_shape=jax.ShapeDtypeStruct((2, rows, width), F32),
        cost_estimate=cost(steps, 16, 4, 10 * array_bytes),
    )(kvqd, kvqd, stats, left, stats_left, right, stats_right)

    near = pl.pallas_call(
        lambda *refs: far_kernel(*refs, scale=scale, column=2, last=False),
        grid=(steps,),
        in_specs=[first, first, second, stat],
        out_specs=first,
        out_shape=jax.ShapeDtypeStruct((2, rows, width), F32),
        input_output_aliases={1: 0},
        cost_estimate=cost(steps, 8, 2, 12 * array_bytes),
    )(kvqd, near, late, stats_late)

    d_keys, d_values = pl.pallas_call(
        lambda *refs: far_kernel(*refs, scale=scale, column=3, last=True),
        grid=(steps,),
        in_specs=[first, first, first, stat],
        out_specs=[out, out],
        out_shape=[
            jax.ShapeDtypeStruct((rows, width), BF16),
            jax.ShapeDtypeStruct((rows, width), BF16),
        ],
        cost_estimate=cost(steps, 8, 2, 10 * array_bytes),
    )(kvqd, near, early_qd, stats_early)
    return (d_queries, d_keys, d_values)


def solution(mesh):
    spec = P(("groups", "seq"), None)
    return jax.shard_map(
        body,
        mesh=mesh,
        in_specs=(spec, spec, spec, spec, spec),
        out_specs=(spec, spec, spec),
        check_vma=False,
    )
```

time: 263 us -> 262 us (level)
  waiting for transfers between devices: 150 us -> 177 us
  Pallas kernels: 64.7 us -> 45.9 us
  starting transfers between devices: 37.7 us -> 29.5 us
    ppermute x12 -> x9, waiting for transfers between devices: 150 us -> 177 us  [shifted(): return lax.ppermute(tree, axis, route)]
    ppermute x12 -> x9, starting transfers between devices: 37.7 us -> 29.5 us  [shifted(): return lax.ppermute(tree, axis, route)]
    pallas_call x1, Pallas kernels: 14.6 us -> 8.94 us  [body(): pl.pallas_call(lambda *refs: near_kernel(*refs, scale=scale), grid=(steps...]
    pallas_call x1, Pallas kernels: 14.2 us -> 8.7 us  [body(): pl.pallas_call(lambda *refs: far_kernel(*refs, scale=scale, column=3, las...]
    pallas_call x1, Pallas kernels: 14.5 us -> 9.12 us  [body(): pl.pallas_call(lambda *refs: far_kernel(*refs, scale=scale, column=2, las...]
  transfers between devices with their start and end apart: 12 -> 9, of which waited for: 10 -> 7; matrix products, arithmetic and copies ran while one was open for 1% -> 1% of each run, Pallas kernels for 11% -> 7%
where the time goes in v3:
time: 262 us; the launch traced here: 261 us
  waiting for transfers between devices  177 us (68%)
  Pallas kernels  45.9 us (18%)
  starting transfers between devices  29.5 us (11%)
  local copies, waits for them, and re-layouts  4.2 us (2%)
  other arithmetic  3.94 us (2%)
    ppermute x9, waiting for transfers between devices, shifted(): return lax.ppermute(tree, axis, route)  177 us
    ppermute x9, starting transfers between devices, shifted(): return lax.ppermute(tree, axis, route)  29.5 us
    pallas_call x1, Pallas kernels, body(): pl.pallas_call(lambda *refs: query_kernel(*refs, scale=scale), grid_spec=...  19.2 us
    pallas_call x1, Pallas kernels, body(): pl.pallas_call(lambda *refs: far_kernel(*refs, scale=scale, column=2, las...  9.12 us
    pallas_call x1, Pallas kernels, body(): pl.pallas_call(lambda *refs: near_kernel(*refs, scale=scale), grid=(steps...  8.94 us
    pallas_call x1, Pallas kernels, body(): pl.pallas_call(lambda *refs: far_kernel(*refs, scale=scale, column=3, las...  8.7 us
  transfers between devices with their start and end apart: 9, of which 7 were waited for; matrix products, arithmetic and copies ran while one was open for 1% of the time, Pallas kernels for 7%

profile of v3, /device:TPU:0, one launch (start us, length us, event | category | flops | bytes accessed | tf_op | source)
XLA Modules:
  0.0 261.1 jit_solution(16008076636884077021)
XLA Ops:
  0.6 2.4 pad_maximum_fusion.refs_1_.refs_2_.refs_0_
  3.1 0.0 copy-start
  3.1 0.6 fusion
  3.7 5.5 %collective-permute-start.1 = (bf16[4,128,2048]{2,1,0:T(8,128)(2,1)S(1)}, bf16[4,128,2048]{2,1,0:T(8,128)(2,1)S(1)}, u32[]{:S(2)}, u32[]{:S(2)}) collective-permute-start(bf16[4,128,2048]{2,1,0:T(8,128)(2,1)S(1)} %get-tuple-element.33), channel_id=1, source_target_pairs={{0,15},{1,0},{2,1},{3,2},{4,3},{5,4},{6,5},{7,6},{8,7},{9,8},{10,9... | collective-permute-start | bytes 6291464 | tf_op jit(solution)/shard_map/ppermute | solution.py:26
  9.1 0.0 collective-permute-start
  9.1 23.5 %collective-permute-done.1.refs_4_.refs_5_ = bf16[4,128,2048]{2,1,0:T(8,128)(2,1)S(1)} collective-permute-done((bf16[4,128,2048]{2,1,0:T(8,128)(2,1)S(1)}, bf16[4,128,2048]{2,1,0:T(8,128)(2,1)S(1)}, u32[]{:S(2)}, u32[]{:S(2)}) %collective-permute-start.1) | collective-permute-done | bytes 2097184 | tf_op jit(solution)/shard_map/ppermute | solution.py:26
  32.7 4.8 %collective-permute-done.refs_3_ = bf16[4,128,2048]{2,1,0:T(8,128)(2,1)S(1)} collective-permute-done((bf16[4,128,2048]{2,1,0:T(8,128)(2,1)S(1)}, bf16[4,128,2048]{2,1,0:T(8,128)(2,1)S(1)}, u32[]{:S(2)}, u32[]{:S(2)}) %collective-permute-start) | collective-permute-done | bytes 2097184 | tf_op jit(solution)/shard_map/ppermute | solution.py:26
  37.5 0.0 collective-permute-start.3
  37.5 0.2 slice.13
  37.8 2.1 collective-permute-start.2
  39.8 0.0 copy-done.3
  39.8 1.5 pad_maximum_fusion.1
  41.4 0.0 copy-done.1
  41.4 113.5 %collective-permute-done.2.refs_5_ = bf16[2,256,2048]{2,1,0:T(8,128)(2,1)S(1)} collective-permute-done((bf16[2,256,2048]{2,1,0:T(8,128)(2,1)S(1)}, bf16[2,256,2048]{2,1,0:T(8,128)(2,1)S(1)}, u32[]{:S(2)}, u32[]{:S(2)}) %collective-permute-start.2) | collective-permute-done | bytes 2097184 | tf_op jit(solution)/shard_map/ppermute | solution.py:26
  154.9 1.4 copy-done.6
  156.3 0.0 collective-permute-done.3.refs_6_.refs_2_
  156.3 19.2 %shard_map.76 = (bf16[256,2048]{1,0:T(8,128)(2,1)}, f32[16,4,256]{2,1,0:T(4,128)}) custom-call(s32[2,4]{1,0:T(2,128)} %refs_0_.1, bf16[4,256,2048]{2,1,0:T(8,128)(2,1)} %copy-done, bf16[4,256,2048]{2,1,0:T(8,128)(2,1)} %copy-done, bf16[4,128,2048]{2,1,0:T(8,128)(2,1)} %copy-done.2, bf16[4,128,2048]{2,1,0:T(8,128)(2,1)} %copy-done.1, ...), custom_call_target="tpu_custom_call" | custom-call | flops 1610612736 | bytes 11534336 | tf_op jit(solution)/shard_map/pallas_call | solution.py:161
  175.5 17.6 %collective-permute-start.7 = (f32[16,4,256]{2,1,0:T(4,128)}, f32[16,4,256]{2,1,0:T(4,128)S(1)}, u32[]{:S(2)}, u32[]{:S(2)}) collective-permute-start(f32[16,4,256]{2,1,0:T(4,128)} %get-tuple-element.24.refs_2_), channel_id=1, source_target_pairs={{0,12},{1,13},{2,14},{3,15},{4,0},{5,1},{6,2},{7,3},{8,4},{9,5},{1... | collective-permute-start | bytes 196616 | tf_op jit(solution)/shard_map/ppermute | solution.py:26
  193.1 2.4 collective-permute-start.6
  195.4 2.0 collective-permute-start.5
  197.5 0.0 collective-permute-start.4
  197.5 0.4 collective-permute-done.7.refs_3_
  197.8 4.7 %collective-permute-done.6.refs_3_ = f32[16,4,256]{2,1,0:T(4,128)S(1)} collective-permute-done((f32[16,4,256]{2,1,0:T(4,128)}, f32[16,4,256]{2,1,0:T(4,128)S(1)}, u32[]{:S(2)}, u32[]{:S(2)}) %collective-permute-start.6) | collective-permute-done | bytes 65568 | tf_op jit(solution)/shard_map/ppermute | solution.py:26
  202.5 0.0 collective-permute-done.5.refs_6_
  202.6 1.5 collective-permute-done.4.refs_4_
  204.1 0.0 collective-permute-start.8
  204.1 0.6 copy-done.10
  204.7 8.9 %shard_map.77.refs_1_ = f32[2,256,2048]{2,1,0:T(8,128)} custom-call(bf16[4,256,2048]{2,1,0:T(8,128)(2,1)} %copy-done, bf16[4,256,2048]{2,1,0:T(8,128)(2,1)} %copy-done, f32[16,4,256]{2,1,0:T(4,128)} %get-tuple-element.24.refs_2_, bf16[4,128,2048]{2,1,0:T(8,128)(2,1)} %copy-done.2, f32[16,4,256]{2,1,0:T(4,128)} %copy-done.10, ...), custom_call_target="tpu_custom_call" | custom-call | flops 1073741824 | bytes 10485760 | tf_op jit(solution)/shard_map/pallas_call | solution.py:185
  213.6 9.1 %shard_map.78.refs_1_ = f32[2,256,2048]{2,1,0:T(8,128)} custom-call(bf16[4,256,2048]{2,1,0:T(8,128)(2,1)} %copy-done, f32[2,256,2048]{2,1,0:T(8,128)} %shard_map.77.refs_1_, bf16[4,256,2048]{2,1,0:T(8,128)(2,1)} %collective-permute-done.3.refs_6_.refs_2_, f32[16,4,256]{2,1,0:T(4,128)} %copy-done.8), custom_call_target="tpu_custom_call", output_to_operand_aliasing={{}: (1, {})} | custom-call | flops 536870912 | bytes 12582912 | tf_op jit(solution)/shard_map/pallas_call | solution.py:194
  222.8 28.3 %collective-permute-done.8.refs_2_ = bf16[2,256,2048]{2,1,0:T(8,128)(2,1)S(1)} collective-permute-done((bf16[2,256,2048]{2,1,0:T(8,128)(2,1)}, bf16[2,256,2048]{2,1,0:T(8,128)(2,1)S(1)}, u32[]{:S(2)}, u32[]{:S(2)}) %collective-permute-start.8) | collective-permute-done | bytes 2097184 | tf_op jit(solution)/shard_map/ppermute | solution.py:26
  251.1 1.3 copy-done.5
  252.4 8.7 %shard_map.79 = (bf16[256,2048]{1,0:T(8,128)(2,1)}, bf16[256,2048]{1,0:T(8,128)(2,1)}) custom-call(bf16[4,256,2048]{2,1,0:T(8,128)(2,1)} %copy-done, f32[2,256,2048]{2,1,0:T(8,128)} %shard_map.78.refs_1_, bf16[2,256,2048]{2,1,0:T(8,128)(2,1)} %copy-done.5, f32[16,4,256]{2,1,0:T(4,128)} %copy-done.7), custom_call_target="tpu_custom_call" | custom-call | flops 536870912 | bytes 10485760 | tf_op jit(solution)/shard_map/pallas_call | solution.py:204
  (16 shorter events, 0.0 us)
Async XLA Ops:
  3.1 34.4 %copy-start = (bf16[4,256,2048]{2,1,0:T(8,128)(2,1)}, bf16[4,256,2048]{2,1,0:T(8,128)(2,1)S(1)}, u32[]{:S(2)}) copy-start(bf16[4,256,2048]{2,1,0:T(8,128)(2,1)S(1)} %pad_maximum_fusion.refs_1_.refs_2_.refs_0_) | copy-start | bytes 12582916
  3.7 29.0 %collective-permute-start.1 = (bf16[4,128,2048]{2,1,0:T(8,128)(2,1)S(1)}, bf16[4,128,2048]{2,1,0:T(8,128)(2,1)S(1)}, u32[]{:S(2)}, u32[]{:S(2)}) collective-permute-start(bf16[4,128,2048]{2,1,0:T(8,128)(2,1)S(1)} %get-tuple-element.33), channel_id=1, source_target_pairs={{0,15},{1,0},{2,1},{3,2},{4,3},{5,4},{6,5},{7,6},{8,7},{9,8},{10,9... | collective-permute-start | bytes 6291464 | tf_op jit(solution)/shard_map/ppermute | solution.py:26
  9.1 30.7 %copy-start.3 = (bf16[256,2048]{1,0:T(8,128)(2,1)S(1)}, bf16[256,2048]{1,0:T(8,128)(2,1)}, u32[]{:S(2)}) copy-start(bf16[256,2048]{1,0:T(8,128)(2,1)} %param.8) | copy-start | bytes 3145732
  9.1 30.7 %copy-start.4 = (bf16[256,2048]{1,0:T(8,128)(2,1)S(1)}, bf16[256,2048]{1,0:T(8,128)(2,1)}, u32[]{:S(2)}) copy-start(bf16[256,2048]{1,0:T(8,128)(2,1)} %param.5) | copy-start | bytes 3145732
  9.1 28.4 %collective-permute-start = (bf16[4,128,2048]{2,1,0:T(8,128)(2,1)S(1)}, bf16[4,128,2048]{2,1,0:T(8,128)(2,1)S(1)}, u32[]{:S(2)}, u32[]{:S(2)}) collective-permute-start(bf16[4,128,2048]{2,1,0:T(8,128)(2,1)S(1)} %get-tuple-element.34), channel_id=1, source_target_pairs={{0,1},{1,2},{2,3},{3,4},{4,5},{5,6},{6,7},{7,8},{8,9},{9,10},{10,1... | collective-permute-start | bytes 6291464 | tf_op jit(solution)/shard_map/ppermute | solution.py:26
  32.7 8.7 %copy-start.1 = (bf16[4,128,2048]{2,1,0:T(8,128)(2,1)}, bf16[4,128,2048]{2,1,0:T(8,128)(2,1)S(1)}, u32[]{:S(2)}) copy-start(bf16[4,128,2048]{2,1,0:T(8,128)(2,1)S(1)} %collective-permute-done.1.refs_4_.refs_5_) | copy-start | bytes 6291460
  37.5 3.8 %copy-start.2 = (bf16[4,128,2048]{2,1,0:T(8,128)(2,1)}, bf16[4,128,2048]{2,1,0:T(8,128)(2,1)S(1)}, u32[]{:S(2)}) copy-start(bf16[4,128,2048]{2,1,0:T(8,128)(2,1)S(1)} %collective-permute-done.refs_3_) | copy-start | bytes 6291460
  37.5 118.8 %collective-permute-start.3 = (bf16[4,256,2048]{2,1,0:T(8,128)(2,1)S(1)}, bf16[4,256,2048]{2,1,0:T(8,128)(2,1)}, u32[]{:S(2)}, u32[]{:S(2)}) collective-permute-start(bf16[4,256,2048]{2,1,0:T(8,128)(2,1)S(1)} %pad_maximum_fusion.refs_1_.refs_2_.refs_0_), channel_id=1, source_target_pairs={{0,12},{1,13},{2,14},{3,15},{4,0},{5,1},{6,2},{7,3},{8,4},{9,5},{1... | collective-permute-start | bytes 12582920 | tf_op jit(solution)/shard_map/ppermute | solution.py:26
  37.8 117.1 %collective-permute-start.2 = (bf16[2,256,2048]{2,1,0:T(8,128)(2,1)S(1)}, bf16[2,256,2048]{2,1,0:T(8,128)(2,1)S(1)}, u32[]{:S(2)}, u32[]{:S(2)}) collective-permute-start(bf16[2,256,2048]{2,1,0:T(8,128)(2,1)S(1)} %slice.13), channel_id=1, source_target_pairs={{0,4},{1,5},{2,6},{3,7},{4,8},{5,9},{6,10},{7,11},{8,12},{9,13},{1... | collective-permute-start | bytes 6291464 | tf_op jit(solution)/shard_map/ppermute | solution.py:26
  154.9 1.4 copy-start.6
  175.5 22.3 %collective-permute-start.7 = (f32[16,4,256]{2,1,0:T(4,128)}, f32[16,4,256]{2,1,0:T(4,128)S(1)}, u32[]{:S(2)}, u32[]{:S(2)}) collective-permute-start(f32[16,4,256]{2,1,0:T(4,128)} %get-tuple-element.24.refs_2_), channel_id=1, source_target_pairs={{0,12},{1,13},{2,14},{3,15},{4,0},{5,1},{6,2},{7,3},{8,4},{9,5},{1... | collective-permute-start | bytes 196616 | tf_op jit(solution)/shard_map/ppermute | solution.py:26
  193.1 9.5 %collective-permute-start.6 = (f32[16,4,256]{2,1,0:T(4,128)}, f32[16,4,256]{2,1,0:T(4,128)S(1)}, u32[]{:S(2)}, u32[]{:S(2)}) collective-permute-start(f32[16,4,256]{2,1,0:T(4,128)} %get-tuple-element.24.refs_2_), channel_id=1, source_target_pairs={{0,4},{1,5},{2,6},{3,7},{4,8},{5,9},{6,10},{7,11},{8,12},{9,13},{1... | collective-permute-start | bytes 196616 | tf_op jit(solution)/shard_map/ppermute | solution.py:26
  195.4 7.1 %collective-permute-start.5 = (f32[16,4,256]{2,1,0:T(4,128)}, f32[16,4,256]{2,1,0:T(4,128)S(1)}, u32[]{:S(2)}, u32[]{:S(2)}) collective-permute-start(f32[16,4,256]{2,1,0:T(4,128)} %get-tuple-element.24.refs_2_), channel_id=1, source_target_pairs={{0,15},{1,0},{2,1},{3,2},{4,3},{5,4},{6,5},{7,6},{8,7},{9,8},{10,9... | collective-permute-start | bytes 196616 | tf_op jit(solution)/shard_map/ppermute | solution.py:26
  197.5 6.6 %collective-permute-start.4 = (f32[16,4,256]{2,1,0:T(4,128)}, f32[16,4,256]{2,1,0:T(4,128)S(1)}, u32[]{:S(2)}, u32[]{:S(2)}) collective-permute-start(f32[16,4,256]{2,1,0:T(4,128)} %get-tuple-element.24.refs_2_), channel_id=1, source_target_pairs={{0,1},{1,2},{2,3},{3,4},{4,5},{5,6},{6,7},{7,8},{8,9},{9,10},{10,1... | collective-permute-start | bytes 196616 | tf_op jit(solution)/shard_map/ppermute | solution.py:26
  197.8 15.8 %copy-start.8 = (f32[16,4,256]{2,1,0:T(4,128)}, f32[16,4,256]{2,1,0:T(4,128)S(1)}, u32[]{:S(2)}) copy-start(f32[16,4,256]{2,1,0:T(4,128)S(1)} %collective-permute-done.7.refs_3_) | copy-start | bytes 196612
  202.5 11.1 %copy-start.7 = (f32[16,4,256]{2,1,0:T(4,128)}, f32[16,4,256]{2,1,0:T(4,128)S(1)}, u32[]{:S(2)}) copy-start(f32[16,4,256]{2,1,0:T(4,128)S(1)} %collective-permute-done.6.refs_3_) | copy-start | bytes 196612
  202.6 1.5 copy-start.9
  204.1 0.6 copy-start.10
  204.1 47.0 %collective-permute-start.8 = (bf16[2,256,2048]{2,1,0:T(8,128)(2,1)}, bf16[2,256,2048]{2,1,0:T(8,128)(2,1)S(1)}, u32[]{:S(2)}, u32[]{:S(2)}) collective-permute-start(bf16[2,256,2048]{2,1,0:T(8,128)(2,1)} %pad_maximum_fusion.1), channel_id=1, source_target_pairs={{0,4},{1,5},{2,6},{3,7},{4,8},{5,9},{6,10},{7,11},{8,12},{9,13},{1... | collective-permute-start | bytes 6291464 | tf_op jit(solution)/shard_map/ppermute | solution.py:26
  251.1 1.3 copy-start.5

commit v4 on v3

v4 whole, which is shorter than its diff:
```python
import math

import jax
import jax.numpy as jnp
from jax import lax
from jax.experimental import pallas as pl
from jax.experimental.pallas import tpu as pltpu
from jax.sharding import PartitionSpec as P

BLK = 128
LOCAL_HEADS = 16
HEAD_SIZE = 128
FRAME_DEV = 4
BLK_DEV = 2
STEP_HEADS = 4

NT = (((1,), (1,)), ((), ()))
TN = (((0,), (0,)), ((), ()))
F32 = jnp.float32
BF16 = jnp.bfloat16


def shifted(tree, axis, distance):
    count = lax.axis_size(axis)
    route = [(i, (i + distance) % count) for i in range(count)]
    return lax.ppermute(tree, axis, route)


def cols(hh):
    return slice(hh * HEAD_SIZE, (hh + 1) * HEAD_SIZE)


def picked(index):
    return pl.ds(pl.multiple_of(index * BLK, BLK), BLK)


def attend_kernel(kl_ref, qd_ref, kv_ref, left_ref, right_ref, early_ref, late_ref,
                  dq_ref, own_ref, to_left, to_right, to_early, to_late, acc_early, acc_late,
                  *, scale):
    acc_early[...] = jnp.zeros_like(acc_early)
    acc_late[...] = jnp.zeros_like(acc_late)
    for i in range(BLK_DEV):
        rows = slice(i * BLK, (i + 1) * BLK)
        side = left_ref if i == 0 else right_ref
        to_side = to_left if i == 0 else to_right
        early = lax.rem(kl_ref[i, 2], BLK_DEV)
        late = lax.rem(kl_ref[i, 3], BLK_DEV)
        for hh in range(STEP_HEADS):
            c = cols(hh)
            q = qd_ref[0, rows, c]
            do = qd_ref[1, rows, c]
            parts = []
            for n in range(2):
                parts.append(jnp.concatenate(
                    [kv_ref[n, rows, c], side[n, :, c], early_ref[n, picked(early), c],
                     late_ref[n, picked(late), c]], axis=0
                ))
            keys, vals = parts
            s = lax.dot_general(keys, q, NT, preferred_element_type=F32) * scale
            top = jnp.max(s, axis=0, keepdims=True)
            lse = top + jnp.log(jnp.sum(jnp.exp(s - top), axis=0, keepdims=True))
            p = jnp.exp(s - lse)
            p_low = p.astype(BF16)
            dp = lax.dot_general(vals, do, NT, preferred_element_type=F32)
            delta = jnp.sum(p_low.astype(F32) * dp, axis=0, keepdims=True)
            ds = (p * (dp - delta)).astype(BF16)
            dq = lax.dot_general(ds, keys, TN, preferred_element_type=F32) * scale
            dq_ref[rows, c] = dq.astype(BF16)
            d_key = jnp.dot(ds, q, preferred_element_type=F32) * scale
            d_value = jnp.dot(p_low, do, preferred_element_type=F32)
            for n, term in ((0, d_key), (1, d_value)):
                own_ref[n, rows, c] = term[0:BLK]
                to_side[n, :, c] = term[BLK:2 * BLK].astype(BF16)
                acc_early[n, picked(early), c] += term[2 * BLK:3 * BLK]
                acc_late[n, picked(late), c] += term[3 * BLK:4 * BLK]
    to_early[...] = acc_early[...].astype(BF16)
    to_late[...] = acc_late[...].astype(BF16)


def body(queries, keys, values, d_out, key_lists):
    rows, width = queries.shape
    steps = width // (HEAD_SIZE * STEP_HEADS)
    assert rows == BLK_DEV * BLK and key_lists.shape[0] == BLK_DEV
    assert steps * HEAD_SIZE * STEP_HEADS == width
    scale = 1.0 / math.sqrt(HEAD_SIZE)

    kv = jnp.stack([keys, values])
    qd = jnp.stack([queries, d_out])
    left = shifted(kv[:, rows - BLK:], "seq", 1)
    right = shifted(kv[:, :BLK], "seq", -1)
    kv_send, left, right = lax.optimization_barrier((kv, left, right))
    early = shifted(kv_send, "seq", FRAME_DEV)
    late = shifted(kv_send, "seq", -FRAME_DEV)

    width_step = HEAD_SIZE * STEP_HEADS
    pair = pl.BlockSpec((2, rows, width_step), lambda h, *_: (0, 0, h))
    edge = pl.BlockSpec((2, BLK, width_step), lambda h, *_: (0, 0, h))
    out = pl.BlockSpec((rows, width_step), lambda h, *_: (0, h))
    heads = steps * STEP_HEADS
    flops = 2 * BLK * 4 * BLK * HEAD_SIZE * 5 * BLK_DEV * heads
    cost = pl.CostEstimate(
        flops=flops, transcendentals=2 * BLK * 4 * BLK * BLK_DEV * heads,
        bytes_accessed=14 * rows * width * 2,
    )

    d_queries, own, to_left, to_right, to_early, to_late = pl.pallas_call(
        lambda *refs: attend_kernel(*refs, scale=scale),
        grid_spec=pltpu.PrefetchScalarGridSpec(
            num_scalar_prefetch=1,
            grid=(steps,),
            in_specs=[pair, pair, edge, edge, pair, pair],
            out_specs=[out, pair, edge, edge, pair, pair],
            scratch_shapes=[pltpu.VMEM((2, rows, width_step), F32)] * 2,
        ),
        out_shape=[
            jax.ShapeDtypeStruct((rows, width), BF16),
            jax.ShapeDtypeStruct((2, rows, width), F32),
            jax.ShapeDtypeStruct((2, BLK, width), BF16),
            jax.ShapeDtypeStruct((2, BLK, width), BF16),
            jax.ShapeDtypeStruct((2, rows, width), BF16),
            jax.ShapeDtypeStruct((2, rows, width), BF16),
        ],
        cost_estimate=cost,
    )(key_lists, qd, kv, left, right, early, late)

    from_right = shifted(to_left, "seq", -1)
    from_left = shifted(to_right, "seq", 1)
    from_late = shifted(to_early, "seq", -FRAME_DEV)
    from_early = shifted(to_late, "seq", FRAME_DEV)
    side = jnp.concatenate([from_left, from_right], axis=1).astype(F32)
    total = own + side + from_late.astype(F32) + from_early.astype(F32)
    grads = total.astype(BF16)
    return (d_queries, grads[0], grads[1])


def solution(mesh):
    spec = P(("groups", "seq"), None)
    return jax.shard_map(
        body,
        mesh=mesh,
        in_specs=(spec, spec, spec, spec, spec),
        out_specs=(spec, spec, spec),
        check_vma=False,
    )
```

time: 262 us -> 248 us (0.947)
  Pallas kernels: 45.9 us -> 22.9 us
  waiting for transfers between devices: 177 us -> 192 us
  starting transfers between devices: 29.5 us -> 20.7 us
  other arithmetic: 3.94 us -> 7.42 us
    pallas_call x4 -> x1, Pallas kernels: 45.9 us -> 22.9 us  [body(): pl.pallas_call(lambda *refs: attend_kernel(*refs, scale=scale), grid_spec...]
    ppermute x9 -> x8, waiting for transfers between devices: 177 us -> 192 us  [shifted(): return lax.ppermute(tree, axis, route)]
    ppermute x9 -> x8, starting transfers between devices: 29.5 us -> 20.7 us  [shifted(): return lax.ppermute(tree, axis, route)]
    convert_element_type x0 -> x1, other arithmetic: none -> 3.83 us  [body(): grads = total.astype(BF16)]
  transfers between devices with their start and end apart: 9 -> 8, of which waited for: 7 -> 5; matrix products, arithmetic and copies ran while one was open for 1% -> 1% of each run, Pallas kernels for 7% -> 0%
where the time goes in v4:
time: 248 us; the launch traced here: 247 us
  waiting for transfers between devices  192 us (77%)
  Pallas kernels  22.9 us (9%)
  starting transfers between devices  20.7 us (8%)
  other arithmetic  7.42 us (3%)
  local copies, waits for them, and re-layouts  2.81 us (1%)
    ppermute x8, waiting for transfers between devices, shifted(): return lax.ppermute(tree, axis, route)  192 us
    pallas_call x1, Pallas kernels, body(): pl.pallas_call(lambda *refs: attend_kernel(*refs, scale=scale), grid_spec...  22.9 us
    ppermute x8, starting transfers between devices, shifted(): return lax.ppermute(tree, axis, route)  20.7 us
  transfers between devices with their start and end apart: 8, of which 5 were waited for; matrix products, arithmetic and copies ran while one was open for 1% of the time, Pallas kernels for 0%

profile of v4, /device:TPU:0, one launch (start us, length us, event | category | flops | bytes accessed | tf_op | source)
XLA Modules:
  0.0 246.7 jit_solution(3470015063210906694)
XLA Ops:
  0.6 0.0 copy-start.1
  0.6 0.0 copy-start.2
  0.7 1.8 fusion.1
  2.5 5.5 %collective-permute-start.1 = (bf16[2,128,2048]{2,1,0:T(8,128)(2,1)S(1)}, bf16[2,128,2048]{2,1,0:T(8,128)(2,1)S(1)}, u32[]{:S(2)}, u32[]{:S(2)}) collective-permute-start(bf16[2,128,2048]{2,1,0:T(8,128)(2,1)S(1)} %get-tuple-element.23), channel_id=1, source_target_pairs={{0,15},{1,0},{2,1},{3,2},{4,3},{5,4},{6,5},{7,6},{8,7},{9,8},{10,9... | collective-permute-start | bytes 3145736 | tf_op jit(solution)/shard_map/ppermute | solution.py:26
  8.0 0.0 collective-permute-start
  8.0 0.0 copy-done.1
  8.0 0.0 copy-done.2
  8.0 0.2 pad_maximum_fusion.refs_2_
  8.2 0.0 copy-start
  8.2 12.1 %collective-permute-done.1.refs_4_ = bf16[2,128,2048]{2,1,0:T(8,128)(2,1)S(1)} collective-permute-done((bf16[2,128,2048]{2,1,0:T(8,128)(2,1)S(1)}, bf16[2,128,2048]{2,1,0:T(8,128)(2,1)S(1)}, u32[]{:S(2)}, u32[]{:S(2)}) %collective-permute-start.1) | collective-permute-done | bytes 1048608 | tf_op jit(solution)/shard_map/ppermute | solution.py:26
  20.3 4.8 %collective-permute-done.refs_3_ = bf16[2,128,2048]{2,1,0:T(8,128)(2,1)S(1)} collective-permute-done((bf16[2,128,2048]{2,1,0:T(8,128)(2,1)S(1)}, bf16[2,128,2048]{2,1,0:T(8,128)(2,1)S(1)}, u32[]{:S(2)}, u32[]{:S(2)}) %collective-permute-start) | collective-permute-done | bytes 1048608 | tf_op jit(solution)/shard_map/ppermute | solution.py:26
  25.1 0.0 collective-permute-start.3
  25.1 2.0 collective-permute-start.2
  27.1 0.0 copy-done.4
  27.1 0.0 copy-done.5
  27.1 1.5 pad_maximum_fusion.1.refs_1_
  28.7 0.0 copy-done
  28.7 0.0 copy-done.6
  28.7 49.4 %collective-permute-done.3.refs_6_ = bf16[2,256,2048]{2,1,0:T(8,128)(2,1)S(1)} collective-permute-done((bf16[2,256,2048]{2,1,0:T(8,128)(2,1)S(1)}, bf16[2,256,2048]{2,1,0:T(8,128)(2,1)S(1)}, u32[]{:S(2)}, u32[]{:S(2)}) %collective-permute-start.3) | collective-permute-done | bytes 2097184 | tf_op jit(solution)/shard_map/ppermute | solution.py:26
  78.1 1.3 copy-done.3
  79.5 29.3 %collective-permute-done.2.refs_5_ = bf16[2,256,2048]{2,1,0:T(8,128)(2,1)} collective-permute-done((bf16[2,256,2048]{2,1,0:T(8,128)(2,1)S(1)}, bf16[2,256,2048]{2,1,0:T(8,128)(2,1)}, u32[]{:S(2)}, u32[]{:S(2)}) %collective-permute-start.2) | collective-permute-done | bytes 2097184 | tf_op jit(solution)/shard_map/ppermute | solution.py:26
  108.8 22.9 %shard_map.76 = (bf16[256,2048]{1,0:T(8,128)(2,1)}, f32[2,256,2048]{2,1,0:T(8,128)}, bf16[2,128,2048]{2,1,0:T(8,128)(2,1)}, bf16[2,128,2048]{2,1,0:T(8,128)(2,1)...) custom-call(s32[2,4]{1,0:T(2,128)} %refs_0_.1, bf16[2,256,2048]{2,1,0:T(8,128)(2,1)} %pad_maximum_fusion.1.refs_1_, ...), custom_call_target="tpu_custom_call" | custom-call | flops 2684354560 | bytes 14680064 | tf_op jit(solution)/shard_map/pallas_call | solution.py:106
  131.7 5.9 %collective-permute-start.6 = (bf16[2,256,2048]{2,1,0:T(8,128)(2,1)}, bf16[2,256,2048]{2,1,0:T(8,128)(2,1)S(1)}, u32[]{:S(2)}, u32[]{:S(2)}) collective-permute-start(bf16[2,256,2048]{2,1,0:T(8,128)(2,1)} %get-tuple-element.19), channel_id=1, source_target_pairs={{0,12},{1,13},{2,14},{3,15},{4,0},{5,1},{6,2},{7,3},{8,4},{9,5},{1... | collective-permute-start | bytes 6291464 | tf_op jit(solution)/shard_map/ppermute | solution.py:26
  137.6 2.9 %collective-permute-start.7 = (bf16[2,256,2048]{2,1,0:T(8,128)(2,1)}, bf16[2,256,2048]{2,1,0:T(8,128)(2,1)S(1)}, u32[]{:S(2)}, u32[]{:S(2)}) collective-permute-start(bf16[2,256,2048]{2,1,0:T(8,128)(2,1)} %get-tuple-element.20), channel_id=1, source_target_pairs={{0,4},{1,5},{2,6},{3,7},{4,8},{5,9},{6,10},{7,11},{8,12},{9,13},{1... | collective-permute-start | bytes 6291464 | tf_op jit(solution)/shard_map/ppermute | solution.py:26
  140.5 3.6 %collective-permute-start.4 = (bf16[2,128,2048]{2,1,0:T(8,128)(2,1)}, bf16[2,128,2048]{2,1,0:T(8,128)(2,1)S(1)}, u32[]{:S(2)}, u32[]{:S(2)}) collective-permute-start(bf16[2,128,2048]{2,1,0:T(8,128)(2,1)} %get-tuple-element.17), channel_id=1, source_target_pairs={{0,1},{1,2},{2,3},{3,4},{4,5},{5,6},{6,7},{7,8},{8,9},{9,10},{10,1... | collective-permute-start | bytes 3145736 | tf_op jit(solution)/shard_map/ppermute | solution.py:26
  144.1 0.8 collective-permute-start.5
  144.9 96.5 %collective-permute-done.4 = bf16[2,128,2048]{2,1,0:T(8,128)(2,1)S(1)} collective-permute-done((bf16[2,128,2048]{2,1,0:T(8,128)(2,1)}, bf16[2,128,2048]{2,1,0:T(8,128)(2,1)S(1)}, u32[]{:S(2)}, u32[]{:S(2)}) %collective-permute-start.4) | collective-permute-done | bytes 1048608 | tf_op jit(solution)/shard_map/ppermute | solution.py:26
  241.4 0.0 collective-permute-done.5
  241.4 0.0 collective-permute-done.6
  241.4 0.0 collective-permute-done.7
  241.4 3.8 %add_convert_fusion = bf16[2,256,2048]{2,1,0:T(8,128)(2,1)S(1)} fusion(bf16[2,256,2048]{2,1,0:T(8,128)(2,1)S(1)} %collective-permute-done.7, bf16[2,256,2048]{2,1,0:T(8,128)(2,1)S(1)} %collective-permute-done.6, f32[2,256,2048]{2,1,0:T(8,128)} %get-tuple-element.16, bf16[2,128,2048]{2,1,0:T(8,128)(2,1)S(1)} %collective-permute-done.5, ...), kind=kLoop, calls=%fused_computation | loop fusion | flops 10485760 | bytes 12582912 | tf_op jit(solution)/shard_map/convert_element_type | solution.py:132
  245.3 1.5 slice_bitcast_fusion
  (6 shorter events, 0.0 us)
Async XLA Ops:
  0.6 7.3 %copy-start.1 = (bf16[256,2048]{1,0:T(8,128)(2,1)S(1)}, bf16[256,2048]{1,0:T(8,128)(2,1)}, u32[]{:S(2)}) copy-start(bf16[256,2048]{1,0:T(8,128)(2,1)} %param.7) | copy-start | bytes 3145732
  0.6 7.3 %copy-start.2 = (bf16[256,2048]{1,0:T(8,128)(2,1)S(1)}, bf16[256,2048]{1,0:T(8,128)(2,1)}, u32[]{:S(2)}) copy-start(bf16[256,2048]{1,0:T(8,128)(2,1)} %param.6) | copy-start | bytes 3145732
  2.5 17.8 %collective-permute-start.1 = (bf16[2,128,2048]{2,1,0:T(8,128)(2,1)S(1)}, bf16[2,128,2048]{2,1,0:T(8,128)(2,1)S(1)}, u32[]{:S(2)}, u32[]{:S(2)}) collective-permute-start(bf16[2,128,2048]{2,1,0:T(8,128)(2,1)S(1)} %get-tuple-element.23), channel_id=1, source_target_pairs={{0,15},{1,0},{2,1},{3,2},{4,3},{5,4},{6,5},{7,6},{8,7},{9,8},{10,9... | collective-permute-start | bytes 3145736 | tf_op jit(solution)/shard_map/ppermute | solution.py:26
  8.0 19.2 %copy-start.4 = (bf16[256,2048]{1,0:T(8,128)(2,1)S(1)}, bf16[256,2048]{1,0:T(8,128)(2,1)}, u32[]{:S(2)}) copy-start(bf16[256,2048]{1,0:T(8,128)(2,1)} %param.8) | copy-start | bytes 3145732
  8.0 19.2 %copy-start.5 = (bf16[256,2048]{1,0:T(8,128)(2,1)S(1)}, bf16[256,2048]{1,0:T(8,128)(2,1)}, u32[]{:S(2)}) copy-start(bf16[256,2048]{1,0:T(8,128)(2,1)} %param.5) | copy-start | bytes 3145732
  8.0 17.1 %collective-permute-start = (bf16[2,128,2048]{2,1,0:T(8,128)(2,1)S(1)}, bf16[2,128,2048]{2,1,0:T(8,128)(2,1)S(1)}, u32[]{:S(2)}, u32[]{:S(2)}) collective-permute-start(bf16[2,128,2048]{2,1,0:T(8,128)(2,1)S(1)} %get-tuple-element.24), channel_id=1, source_target_pairs={{0,1},{1,2},{2,3},{3,4},{4,5},{5,6},{6,7},{7,8},{8,9},{9,10},{10,1... | collective-permute-start | bytes 3145736 | tf_op jit(solution)/shard_map/ppermute | solution.py:26
  8.2 20.5 %copy-start = (bf16[2,256,2048]{2,1,0:T(8,128)(2,1)}, bf16[2,256,2048]{2,1,0:T(8,128)(2,1)S(1)}, u32[]{:S(2)}) copy-start(bf16[2,256,2048]{2,1,0:T(8,128)(2,1)S(1)} %pad_maximum_fusion.refs_2_) | copy-start | bytes 6291460
  20.3 8.4 %copy-start.6 = (bf16[2,128,2048]{2,1,0:T(8,128)(2,1)}, bf16[2,128,2048]{2,1,0:T(8,128)(2,1)S(1)}, u32[]{:S(2)}) copy-start(bf16[2,128,2048]{2,1,0:T(8,128)(2,1)S(1)} %collective-permute-done.1.refs_4_) | copy-start | bytes 3145732
  25.1 3.6 %copy-start.7 = (bf16[2,128,2048]{2,1,0:T(8,128)(2,1)}, bf16[2,128,2048]{2,1,0:T(8,128)(2,1)S(1)}, u32[]{:S(2)}) copy-start(bf16[2,128,2048]{2,1,0:T(8,128)(2,1)S(1)} %collective-permute-done.refs_3_) | copy-start | bytes 3145732
  25.1 53.0 %collective-permute-start.3 = (bf16[2,256,2048]{2,1,0:T(8,128)(2,1)S(1)}, bf16[2,256,2048]{2,1,0:T(8,128)(2,1)S(1)}, u32[]{:S(2)}, u32[]{:S(2)}) collective-permute-start(bf16[2,256,2048]{2,1,0:T(8,128)(2,1)S(1)} %pad_maximum_fusion.refs_2_), channel_id=1, source_target_pairs={{0,12},{1,13},{2,14},{3,15},{4,0},{5,1},{6,2},{7,3},{8,4},{9,5},{1... | collective-permute-start | bytes 6291464 | tf_op jit(solution)/shard_map/ppermute | solution.py:26
  25.1 83.7 %collective-permute-start.2 = (bf16[2,256,2048]{2,1,0:T(8,128)(2,1)S(1)}, bf16[2,256,2048]{2,1,0:T(8,128)(2,1)}, u32[]{:S(2)}, u32[]{:S(2)}) collective-permute-start(bf16[2,256,2048]{2,1,0:T(8,128)(2,1)S(1)} %pad_maximum_fusion.refs_2_), channel_id=1, source_target_pairs={{0,4},{1,5},{2,6},{3,7},{4,8},{5,9},{6,10},{7,11},{8,12},{9,13},{1... | collective-permute-start | bytes 6291464 | tf_op jit(solution)/shard_map/ppermute | solution.py:26
  78.1 1.3 copy-start.3
  131.7 109.7 %collective-permute-start.6 = (bf16[2,256,2048]{2,1,0:T(8,128)(2,1)}, bf16[2,256,2048]{2,1,0:T(8,128)(2,1)S(1)}, u32[]{:S(2)}, u32[]{:S(2)}) collective-permute-start(bf16[2,256,2048]{2,1,0:T(8,128)(2,1)} %get-tuple-element.19), channel_id=1, source_target_pairs={{0,12},{1,13},{2,14},{3,15},{4,0},{5,1},{6,2},{7,3},{8,4},{9,5},{1... | collective-permute-start | bytes 6291464 | tf_op jit(solution)/shard_map/ppermute | solution.py:26
  137.6 103.8 %collective-permute-start.7 = (bf16[2,256,2048]{2,1,0:T(8,128)(2,1)}, bf16[2,256,2048]{2,1,0:T(8,128)(2,1)S(1)}, u32[]{:S(2)}, u32[]{:S(2)}) collective-permute-start(bf16[2,256,2048]{2,1,0:T(8,128)(2,1)} %get-tuple-element.20), channel_id=1, source_target_pairs={{0,4},{1,5},{2,6},{3,7},{4,8},{5,9},{6,10},{7,11},{8,12},{9,13},{1... | collective-permute-start | bytes 6291464 | tf_op jit(solution)/shard_map/ppermute | solution.py:26
  140.5 100.9 %collective-permute-start.4 = (bf16[2,128,2048]{2,1,0:T(8,128)(2,1)}, bf16[2,128,2048]{2,1,0:T(8,128)(2,1)S(1)}, u32[]{:S(2)}, u32[]{:S(2)}) collective-permute-start(bf16[2,128,2048]{2,1,0:T(8,128)(2,1)} %get-tuple-element.17), channel_id=1, source_target_pairs={{0,1},{1,2},{2,3},{3,4},{4,5},{5,6},{6,7},{7,8},{8,9},{9,10},{10,1... | collective-permute-start | bytes 3145736 | tf_op jit(solution)/shard_map/ppermute | solution.py:26
  144.1 97.3 %collective-permute-start.5 = (bf16[2,128,2048]{2,1,0:T(8,128)(2,1)}, bf16[2,128,2048]{2,1,0:T(8,128)(2,1)S(1)}, u32[]{:S(2)}, u32[]{:S(2)}) collective-permute-start(bf16[2,128,2048]{2,1,0:T(8,128)(2,1)} %get-tuple-element.18), channel_id=1, source_target_pairs={{0,15},{1,0},{2,1},{3,2},{4,3},{5,4},{6,5},{7,6},{8,7},{9,8},{10,9... | collective-permute-start | bytes 3145736 | tf_op jit(solution)/shard_map/ppermute | solution.py:26

commit v5 on v4

--- a/solution.py
+++ b/solution.py
@@ -13,6 +13,7 @@
 FRAME_DEV = 4
 BLK_DEV = 2
 STEP_HEADS = 4
+CHUNK_STEPS = (3, 1)
 
 NT = (((1,), (1,)), ((), ()))
 TN = (((0,), (0,)), ((), ()))
@@ -34,9 +35,11 @@
     return pl.ds(pl.multiple_of(index * BLK, BLK), BLK)
 
 
-def attend_kernel(kl_ref, qd_ref, kv_ref, left_ref, right_ref, early_ref, late_ref,
-                  dq_ref, own_ref, to_left, to_right, to_early, to_late, acc_early, acc_late,
-                  *, scale):
+def attend_kernel(kl_ref, qd_ref, kv_ref, left_ref, right_ref, early_ref, late_ref, *rest,
+                  scale, aliased):
+    if aliased:
+        rest = rest[2:]
+    dq_ref, own_ref, to_left, to_right, to_early, to_late, acc_early, acc_late = rest
     acc_early[...] = jnp.zeros_like(acc_early)
     acc_late[...] = jnp.zeros_like(acc_late)
     for i in range(BLK_DEV):
@@ -86,47 +89,63 @@
 
     kv = jnp.stack([keys, values])
     qd = jnp.stack([queries, d_out])
+    width_step = HEAD_SIZE * STEP_HEADS
+    assert sum(CHUNK_STEPS) == steps
+    bases = [sum(CHUNK_STEPS[:c]) for c in range(len(CHUNK_STEPS))]
+    chunked = [kv[:, :, b * width_step:(b + n) * width_step] for b, n in zip(bases, CHUNK_STEPS)]
     left = shifted(kv[:, rows - BLK:], "seq", 1)
     right = shifted(kv[:, :BLK], "seq", -1)
-    kv_send, left, right = lax.optimization_barrier((kv, left, right))
-    early = shifted(kv_send, "seq", FRAME_DEV)
-    late = shifted(kv_send, "seq", -FRAME_DEV)
+    chunked, left, right = lax.optimization_barrier((chunked, left, right))
+    far = []
+    for part in chunked:
+        far.append((shifted(part, "seq", FRAME_DEV), shifted(part, "seq", -FRAME_DEV)))
 
-    width_step = HEAD_SIZE * STEP_HEADS
-    pair = pl.BlockSpec((2, rows, width_step), lambda h, *_: (0, 0, h))
-    edge = pl.BlockSpec((2, BLK, width_step), lambda h, *_: (0, 0, h))
-    out = pl.BlockSpec((rows, width_step), lambda h, *_: (0, h))
-    heads = steps * STEP_HEADS
-    flops = 2 * BLK * 4 * BLK * HEAD_SIZE * 5 * BLK_DEV * heads
-    cost = pl.CostEstimate(
-        flops=flops, transcendentals=2 * BLK * 4 * BLK * BLK_DEV * heads,
-        bytes_accessed=14 * rows * width * 2,
+    d_queries = own = None
+    received = []
+    for c, (base, chunk_steps) in enumerate(zip(bases, CHUNK_STEPS)):
+        chunk_width = chunk_steps * width_step
+        heads = chunk_steps * STEP_HEADS
+        cost = pl.CostEstimate(
+            flops=2 * BLK * 4 * BLK * HEAD_SIZE * 5 * BLK_DEV * heads,
+            transcendentals=2 * BLK * 4 * BLK * BLK_DEV * heads,
+            bytes_accessed=14 * rows * chunk_width * 2,
+        )
+        pair = pl.BlockSpec((2, rows, width_step), lambda h, *_, b=base: (0, 0, b + h))
+        edge = pl.BlockSpec((2, BLK, width_step), lambda h, *_, b=base: (0, 0, b + h))
+        out = pl.BlockSpec((rows, width_step), lambda h, *_, b=base: (0, b + h))
+        local_pair = pl.BlockSpec((2, rows, width_step), lambda h, *_: (0, 0, h))
+        local_edge = pl.BlockSpec((2, BLK, width_step), lambda h, *_: (0, 0, h))
+        aliased = c > 0
+        extra_specs = [pl.BlockSpec(memory_space=pl.ANY)] * 2 if aliased else []
+        extra_args = [d_queries, own] if aliased else []
+        aliases = {7: 0, 8: 1} if aliased else {}
+        d_queries, own, to_left, to_right, to_early, to_late = pl.pallas_call(
+            lambda *refs, a=aliased: attend_kernel(*refs, scale=scale, aliased=a),
+            grid_spec=pltpu.PrefetchScalarGridSpec(
+                num_scalar_prefetch=1,
+                grid=(chunk_steps,),
+                in_specs=[pair, pair, edge, edge, local_pair, local_pair] + extra_specs,
+                out_specs=[out, pair, local_edge, local_edge, local_pair, local_pair],
+                scratch_shapes=[pltpu.VMEM((2, rows, width_step), F32)] * 2,
+            ),
+            out_shape=[
+                jax.ShapeDtypeStruct((rows, width), BF16),
+                jax.ShapeDtypeStruct((2, rows, width), F32),
+                jax.ShapeDtypeStruct((2, BLK, chunk_width), BF16),
+                jax.ShapeDtypeStruct((2, BLK, chunk_width), BF16),
+                jax.ShapeDtypeStruct((2, rows, chunk_width), BF16),
+                jax.ShapeDtypeStruct((2, rows, chunk_width), BF16),
+            ],
+            input_output_aliases=aliases,
+            cost_estimate=cost,
+        )(key_lists, qd, kv, left, right, far[c][0], far[c][1], *extra_args)
+        received.append((
+            shifted(to_right, "seq", 1), shifted(to_left, "seq", -1),
+            shifted(to_late, "seq", FRAME_DEV), shifted(to_early, "seq", -FRAME_DEV),
+        ))
+    from_left, from_right, from_early, from_late = (
+        jnp.concatenate([r[k] for r in received], axis=-1) for k in range(4)
     )
-
-    d_queries, own, to_left, to_right, to_early, to_late = pl.pallas_call(
-        lambda *refs: attend_kernel(*refs, scale=scale),
-        grid_spec=pltpu.PrefetchScalarGridSpec(
-            num_scalar_prefetch=1,
-            grid=(steps,),
-            in_specs=[pair, pair, edge, edge, pair, pair],
-            out_specs=[out, pair, edge, edge, pair, pair],
-            scratch_shapes=[pltpu.VMEM((2, rows, width_step), F32)] * 2,
-        ),
-        out_shape=[
-            jax.ShapeDtypeStruct((rows, width), BF16),
-            jax.ShapeDtypeStruct((2, rows, width), F32),
-            jax.ShapeDtypeStruct((2, BLK, width), BF16),
-            jax.ShapeDtypeStruct((2, BLK, width), BF16),
-            jax.ShapeDtypeStruct((2, rows, width), BF16),
-            jax.ShapeDtypeStruct((2, rows, width), BF16),
-        ],
-        cost_estimate=cost,
-    )(key_lists, qd, kv, left, right, early, late)
-
-    from_right = shifted(to_left, "seq", -1)
-    from_left = shifted(to_right, "seq", 1)
-    from_late = shifted(to_early, "seq", -FRAME_DEV)
-    from_early = shifted(to_late, "seq", FRAME_DEV)
     side = jnp.concatenate([from_left, from_right], axis=1).astype(F32)
     total = own + side + from_late.astype(F32) + from_early.astype(F32)
     grads = total.astype(BF16)

time: 248 us -> 231 us (0.931)
  waiting for transfers between devices: 192 us -> 151 us
  starting transfers between devices: 20.7 us -> 40.9 us
  Pallas kernels: 22.9 us -> 26.6 us
    ppermute x8 -> x14, waiting for transfers between devices: 192 us -> 151 us  [shifted(): return lax.ppermute(tree, axis, route)]
    ppermute x8 -> x14, starting transfers between devices: 20.7 us -> 40.9 us  [shifted(): return lax.ppermute(tree, axis, route)]
    pallas_call x1 -> x2, Pallas kernels: 22.9 us -> 26.6 us  [body(): pl.pallas_call(lambda *refs, a=aliased: attend_kernel(*refs, scale=scale,...]
  transfers between devices with their start and end apart: 8 -> 14, of which waited for: 5 -> 7; matrix products, arithmetic and copies ran while one was open for 1% -> 2% of each run, Pallas kernels for 0% -> 12%
where the time goes in v5:
time: 231 us
  waiting for transfers between devices  151 us (65%)
  starting transfers between devices  40.9 us (18%)
  Pallas kernels  26.6 us (12%)
  other arithmetic  8.75 us (4%)
  local copies, waits for them, and re-layouts  2.74 us (1%)
    ppermute x14, waiting for transfers between devices, shifted(): return lax.ppermute(tree, axis, route)  151 us
    ppermute x14, starting transfers between devices, shifted(): return lax.ppermute(tree, axis, route)  40.9 us
    pallas_call x2, Pallas kernels, body(): pl.pallas_call(lambda *refs, a=aliased: attend_kernel(*refs, scale=scale,...  26.6 us
  transfers between devices with their start and end apart: 14, of which 7 were waited for; matrix products, arithmetic and copies ran while one was open for 2% of the time, Pallas kernels for 12%

profile of v5, /device:TPU:0, one launch (start us, length us, event | category | flops | bytes accessed | tf_op | source)
XLA Modules:
  0.0 230.8 jit_solution(6294705827851648862)
XLA Ops:
  0.7 1.8 fusion.2
  2.5 5.5 %collective-permute-start.1 = (bf16[2,128,2048]{2,1,0:T(8,128)(2,1)S(1)}, bf16[2,128,2048]{2,1,0:T(8,128)(2,1)S(1)}, u32[]{:S(2)}, u32[]{:S(2)}) collective-permute-start(bf16[2,128,2048]{2,1,0:T(8,128)(2,1)S(1)} %get-tuple-element.37), channel_id=1, source_target_pairs={{0,15},{1,0},{2,1},{3,2},{4,3},{5,4},{6,5},{7,6},{8,7},{9,8},{10,9... | collective-permute-start | bytes 3145736 | tf_op jit(solution)/shard_map/ppermute | solution.py:27
  8.0 0.0 collective-permute-start
  8.0 0.9 fusion.3
  8.8 0.1 fusion
  9.0 0.0 copy-start.5
  9.0 0.0 copy-start.6
  9.0 11.3 %collective-permute-done.1.refs_4_ = bf16[2,128,2048]{2,1,0:T(8,128)(2,1)S(1)} collective-permute-done((bf16[2,128,2048]{2,1,0:T(8,128)(2,1)S(1)}, bf16[2,128,2048]{2,1,0:T(8,128)(2,1)S(1)}, u32[]{:S(2)}, u32[]{:S(2)}) %collective-permute-start.1) | collective-permute-done | bytes 1048608 | tf_op jit(solution)/shard_map/ppermute | solution.py:27
  20.3 4.8 %collective-permute-done.refs_3_ = bf16[2,128,2048]{2,1,0:T(8,128)(2,1)S(1)} collective-permute-done((bf16[2,128,2048]{2,1,0:T(8,128)(2,1)S(1)}, bf16[2,128,2048]{2,1,0:T(8,128)(2,1)S(1)}, u32[]{:S(2)}, u32[]{:S(2)}) %collective-permute-start) | collective-permute-done | bytes 1048608 | tf_op jit(solution)/shard_map/ppermute | solution.py:27
  25.1 0.0 collective-permute-start.5
  25.1 2.0 collective-permute-start.4
  27.1 1.6 pad_maximum_fusion.refs_2_
  28.7 1.5 pad_maximum_fusion.1.refs_1_
  30.2 1.8 collective-permute-start.3
  32.0 0.2 collective-permute-start.2
  32.2 34.6 %collective-permute-done.5.refs_6_ = bf16[2,256,1536]{2,1,0:T(8,128)(2,1)S(1)} collective-permute-done((bf16[2,256,1536]{2,1,0:T(8,128)(2,1)S(1)}, bf16[2,256,1536]{2,1,0:T(8,128)(2,1)S(1)}, u32[]{:S(2)}, u32[]{:S(2)}) %collective-permute-start.5) | collective-permute-done | bytes 1572896 | tf_op jit(solution)/shard_map/ppermute | solution.py:27
  66.9 1.1 copy-done.4
  68.0 18.3 %collective-permute-done.4.refs_5_ = bf16[2,256,1536]{2,1,0:T(8,128)(2,1)} collective-permute-done((bf16[2,256,1536]{2,1,0:T(8,128)(2,1)S(1)}, bf16[2,256,1536]{2,1,0:T(8,128)(2,1)}, u32[]{:S(2)}, u32[]{:S(2)}) %collective-permute-start.4) | collective-permute-done | bytes 1572896 | tf_op jit(solution)/shard_map/ppermute | solution.py:27
  86.3 18.1 %shard_map.76 = (bf16[256,2048]{1,0:T(8,128)(2,1)}, f32[2,256,2048]{2,1,0:T(8,128)}, bf16[2,128,1536]{2,1,0:T(8,128)(2,1)}, bf16[2,128,1536]{2,1,0:T(8,128)(2,1)...) custom-call(s32[2,4]{1,0:T(2,128)} %refs_0_.3, bf16[2,256,2048]{2,1,0:T(8,128)(2,1)} %pad_maximum_fusion.1.refs_1_, ...), custom_call_target="tpu_custom_call" | custom-call | flops 2013265920 | bytes 11010048 | tf_op jit(solution)/shard_map/pallas_call | solution.py:122
  104.4 7.4 %collective-permute-start.10 = (bf16[2,256,1536]{2,1,0:T(8,128)(2,1)}, bf16[2,256,1536]{2,1,0:T(8,128)(2,1)S(1)}, u32[]{:S(2)}, u32[]{:S(2)}) collective-permute-start(bf16[2,256,1536]{2,1,0:T(8,128)(2,1)} %get-tuple-element.31), channel_id=1, source_target_pairs={{0,12},{1,13},{2,14},{3,15},{4,0},{5,1},{6,2},{7,3},{8,4},{9,5},{1... | collective-permute-start | bytes 4718600 | tf_op jit(solution)/shard_map/ppermute | solution.py:27
  111.8 7.0 %collective-permute-start.12 = (bf16[2,256,1536]{2,1,0:T(8,128)(2,1)}, bf16[2,256,1536]{2,1,0:T(8,128)(2,1)S(1)}, u32[]{:S(2)}, u32[]{:S(2)}) collective-permute-start(bf16[2,256,1536]{2,1,0:T(8,128)(2,1)} %get-tuple-element.33), channel_id=1, source_target_pairs={{0,4},{1,5},{2,6},{3,7},{4,8},{5,9},{6,10},{7,11},{8,12},{9,13},{1... | collective-permute-start | bytes 4718600 | tf_op jit(solution)/shard_map/ppermute | solution.py:27
  118.8 0.0 collective-permute-done.3.refs_6_
  118.8 8.5 %shard_map.77 = (bf16[256,2048]{1,0:T(8,128)(2,1)}, f32[2,256,2048]{2,1,0:T(8,128)}, bf16[2,128,512]{2,1,0:T(8,128)(2,1)}, bf16[2,128,512]{2,1,0:T(8,128)(2,1)},...) custom-call(s32[2,4]{1,0:T(2,128)} %refs_0_.3, ...), custom_call_target="tpu_custom_call", output_to_operand_aliasing={{0}: (7, {}), {1}: (8, {})} | custom-call | flops 671088640 | bytes 3670016 | tf_op jit(solution)/shard_map/pallas_call | solution.py:122
  127.4 6.2 %collective-permute-start.7 = (bf16[2,128,512]{2,1,0:T(8,128)(2,1)}, bf16[2,128,512]{2,1,0:T(8,128)(2,1)S(1)}, u32[]{:S(2)}, u32[]{:S(2)}) collective-permute-start(bf16[2,128,512]{2,1,0:T(8,128)(2,1)} %get-tuple-element.28), channel_id=1, source_target_pairs={{0,1},{1,2},{2,3},{3,4},{4,5},{5,6},{6,7},{7,8},{8,9},{9,10},{10,1... | collective-permute-start | bytes 786440 | tf_op jit(solution)/shard_map/ppermute | solution.py:27
  133.5 2.1 collective-permute-start.11
  135.7 51.1 %collective-permute-done.7 = bf16[2,128,512]{2,1,0:T(8,128)(2,1)S(1)} collective-permute-done((bf16[2,128,512]{2,1,0:T(8,128)(2,1)}, bf16[2,128,512]{2,1,0:T(8,128)(2,1)S(1)}, u32[]{:S(2)}, u32[]{:S(2)}) %collective-permute-start.7) | collective-permute-done | bytes 262176 | tf_op jit(solution)/shard_map/ppermute | solution.py:27
  186.8 5.8 %collective-permute-done.9 = bf16[2,128,512]{2,1,0:T(8,128)(2,1)S(1)} collective-permute-done((bf16[2,128,512]{2,1,0:T(8,128)(2,1)}, bf16[2,128,512]{2,1,0:T(8,128)(2,1)S(1)}, u32[]{:S(2)}, u32[]{:S(2)}) %collective-permute-start.9) | collective-permute-done | bytes 262176 | tf_op jit(solution)/shard_map/ppermute | solution.py:27
  192.5 4.5 %collective-permute-start.8 = (bf16[2,128,1536]{2,1,0:T(8,128)(2,1)}, bf16[2,128,1536]{2,1,0:T(8,128)(2,1)S(1)}, u32[]{:S(2)}, u32[]{:S(2)}) collective-permute-start(bf16[2,128,1536]{2,1,0:T(8,128)(2,1)} %get-tuple-element.29), channel_id=1, source_target_pairs={{0,15},{1,0},{2,1},{3,2},{4,3},{5,4},{6,5},{7,6},{8,7},{9,8},{10,9... | collective-permute-start | bytes 2359304 | tf_op jit(solution)/shard_map/ppermute | solution.py:27
  197.1 4.2 %collective-permute-start.13 = (bf16[2,256,512]{2,1,0:T(8,128)(2,1)}, bf16[2,256,512]{2,1,0:T(8,128)(2,1)S(1)}, u32[]{:S(2)}, u32[]{:S(2)}) collective-permute-start(bf16[2,256,512]{2,1,0:T(8,128)(2,1)} %get-tuple-element.34), channel_id=1, source_target_pairs={{0,4},{1,5},{2,6},{3,7},{4,8},{5,9},{6,10},{7,11},{8,12},{9,13},{1... | collective-permute-start | bytes 1572872 | tf_op jit(solution)/shard_map/ppermute | solution.py:27
  201.2 25.2 %collective-permute-done.13 = bf16[2,256,512]{2,1,0:T(8,128)(2,1)S(1)} collective-permute-done((bf16[2,256,512]{2,1,0:T(8,128)(2,1)}, bf16[2,256,512]{2,1,0:T(8,128)(2,1)S(1)}, u32[]{:S(2)}, u32[]{:S(2)}) %collective-permute-start.13) | collective-permute-done | bytes 524320 | tf_op jit(solution)/shard_map/ppermute | solution.py:27
  226.4 2.8 %add_convert_fusion = bf16[2,256,2048]{2,1,0:T(8,128)(2,1)S(1)} fusion(f32[2,256,2048]{2,1,0:T(8,128)} %get-tuple-element.26, bf16[2,128,512]{2,1,0:T(8,128)(2,1)S(1)} %collective-permute-done.9, bf16[2,128,1536]{2,1,0:T(8,128)(2,1)S(1)} %collective-permute-done.8, bf16[2,128,512]{2,1,0:T(8,128)(2,1)S(1)} %collective-permute-done.7, ...), kind=kLoop, calls=%fused_computation | loop fusion | flops 20971520 | bytes 12582912 | tf_op jit(solution)/shard_map/convert_element_type | solution.py:151
  229.2 1.6 slice_bitcast_fusion
  (19 shorter events, 0.0 us)
Async XLA Ops:
  0.6 7.3 %copy-start = (bf16[256,2048]{1,0:T(8,128)(2,1)S(1)}, bf16[256,2048]{1,0:T(8,128)(2,1)}, u32[]{:S(2)}) copy-start(bf16[256,2048]{1,0:T(8,128)(2,1)} %param.7) | copy-start | bytes 3145732
  0.6 7.3 %copy-start.1 = (bf16[256,2048]{1,0:T(8,128)(2,1)S(1)}, bf16[256,2048]{1,0:T(8,128)(2,1)}, u32[]{:S(2)}) copy-start(bf16[256,2048]{1,0:T(8,128)(2,1)} %param.6) | copy-start | bytes 3145732
  2.5 17.8 %collective-permute-start.1 = (bf16[2,128,2048]{2,1,0:T(8,128)(2,1)S(1)}, bf16[2,128,2048]{2,1,0:T(8,128)(2,1)S(1)}, u32[]{:S(2)}, u32[]{:S(2)}) collective-permute-start(bf16[2,128,2048]{2,1,0:T(8,128)(2,1)S(1)} %get-tuple-element.37), channel_id=1, source_target_pairs={{0,15},{1,0},{2,1},{3,2},{4,3},{5,4},{6,5},{7,6},{8,7},{9,8},{10,9... | collective-permute-start | bytes 3145736 | tf_op jit(solution)/shard_map/ppermute | solution.py:27
  8.0 17.1 %collective-permute-start = (bf16[2,128,2048]{2,1,0:T(8,128)(2,1)S(1)}, bf16[2,128,2048]{2,1,0:T(8,128)(2,1)S(1)}, u32[]{:S(2)}, u32[]{:S(2)}) collective-permute-start(bf16[2,128,2048]{2,1,0:T(8,128)(2,1)S(1)} %get-tuple-element.38), channel_id=1, source_target_pairs={{0,1},{1,2},{2,3},{3,4},{4,5},{5,6},{6,7},{7,8},{8,9},{9,10},{10,1... | collective-permute-start | bytes 3145736 | tf_op jit(solution)/shard_map/ppermute | solution.py:27
  9.0 19.7 %copy-start.5 = (bf16[256,2048]{1,0:T(8,128)(2,1)S(1)}, bf16[256,2048]{1,0:T(8,128)(2,1)}, u32[]{:S(2)}) copy-start(bf16[256,2048]{1,0:T(8,128)(2,1)} %param.8) | copy-start | bytes 3145732
  9.0 19.7 %copy-start.6 = (bf16[256,2048]{1,0:T(8,128)(2,1)S(1)}, bf16[256,2048]{1,0:T(8,128)(2,1)}, u32[]{:S(2)}) copy-start(bf16[256,2048]{1,0:T(8,128)(2,1)} %param.5) | copy-start | bytes 3145732
  20.3 8.4 %copy-start.2 = (bf16[2,128,2048]{2,1,0:T(8,128)(2,1)}, bf16[2,128,2048]{2,1,0:T(8,128)(2,1)S(1)}, u32[]{:S(2)}) copy-start(bf16[2,128,2048]{2,1,0:T(8,128)(2,1)S(1)} %collective-permute-done.1.refs_4_) | copy-start | bytes 3145732
  25.1 3.6 %copy-start.3 = (bf16[2,128,2048]{2,1,0:T(8,128)(2,1)}, bf16[2,128,2048]{2,1,0:T(8,128)(2,1)S(1)}, u32[]{:S(2)}) copy-start(bf16[2,128,2048]{2,1,0:T(8,128)(2,1)S(1)} %collective-permute-done.refs_3_) | copy-start | bytes 3145732
  25.1 41.8 %collective-permute-start.5 = (bf16[2,256,1536]{2,1,0:T(8,128)(2,1)S(1)}, bf16[2,256,1536]{2,1,0:T(8,128)(2,1)S(1)}, u32[]{:S(2)}, u32[]{:S(2)}) collective-permute-start(bf16[2,256,1536]{2,1,0:T(8,128)(2,1)S(1)} %fusion), channel_id=1, source_target_pairs={{0,12},{1,13},{2,14},{3,15},{4,0},{5,1},{6,2},{7,3},{8,4},{9,5},{1... | collective-permute-start | bytes 4718600 | tf_op jit(solution)/shard_map/ppermute | solution.py:27
  25.1 61.2 %collective-permute-start.4 = (bf16[2,256,1536]{2,1,0:T(8,128)(2,1)S(1)}, bf16[2,256,1536]{2,1,0:T(8,128)(2,1)}, u32[]{:S(2)}, u32[]{:S(2)}) collective-permute-start(bf16[2,256,1536]{2,1,0:T(8,128)(2,1)S(1)} %fusion), channel_id=1, source_target_pairs={{0,4},{1,5},{2,6},{3,7},{4,8},{5,9},{6,10},{7,11},{8,12},{9,13},{1... | collective-permute-start | bytes 4718600 | tf_op jit(solution)/shard_map/ppermute | solution.py:27
  30.2 88.6 %collective-permute-start.3 = (bf16[2,256,512]{2,1,0:T(8,128)(2,1)}, bf16[2,256,512]{2,1,0:T(8,128)(2,1)}, u32[]{:S(2)}, u32[]{:S(2)}) collective-permute-start(bf16[2,256,512]{2,1,0:T(8,128)(2,1)} %fusion.3), channel_id=1, source_target_pairs={{0,12},{1,13},{2,14},{3,15},{4,0},{5,1},{6,2},{7,3},{8,4},{9,5},{1... | collective-permute-start | bytes 1572872 | tf_op jit(solution)/shard_map/ppermute | solution.py:27
  32.0 86.8 %collective-permute-start.2 = (bf16[2,256,512]{2,1,0:T(8,128)(2,1)}, bf16[2,256,512]{2,1,0:T(8,128)(2,1)}, u32[]{:S(2)}, u32[]{:S(2)}) collective-permute-start(bf16[2,256,512]{2,1,0:T(8,128)(2,1)} %fusion.3), channel_id=1, source_target_pairs={{0,4},{1,5},{2,6},{3,7},{4,8},{5,9},{6,10},{7,11},{8,12},{9,13},{1... | collective-permute-start | bytes 1572872 | tf_op jit(solution)/shard_map/ppermute | solution.py:27
  66.9 1.1 copy-start.4
  104.4 122.0 %collective-permute-start.10 = (bf16[2,256,1536]{2,1,0:T(8,128)(2,1)}, bf16[2,256,1536]{2,1,0:T(8,128)(2,1)S(1)}, u32[]{:S(2)}, u32[]{:S(2)}) collective-permute-start(bf16[2,256,1536]{2,1,0:T(8,128)(2,1)} %get-tuple-element.31), channel_id=1, source_target_pairs={{0,12},{1,13},{2,14},{3,15},{4,0},{5,1},{6,2},{7,3},{8,4},{9,5},{1... | collective-permute-start | bytes 4718600 | tf_op jit(solution)/shard_map/ppermute | solution.py:27
  111.8 114.6 %collective-permute-start.12 = (bf16[2,256,1536]{2,1,0:T(8,128)(2,1)}, bf16[2,256,1536]{2,1,0:T(8,128)(2,1)S(1)}, u32[]{:S(2)}, u32[]{:S(2)}) collective-permute-start(bf16[2,256,1536]{2,1,0:T(8,128)(2,1)} %get-tuple-element.33), channel_id=1, source_target_pairs={{0,4},{1,5},{2,6},{3,7},{4,8},{5,9},{6,10},{7,11},{8,12},{9,13},{1... | collective-permute-start | bytes 4718600 | tf_op jit(solution)/shard_map/ppermute | solution.py:27
  127.4 59.4 %collective-permute-start.7 = (bf16[2,128,512]{2,1,0:T(8,128)(2,1)}, bf16[2,128,512]{2,1,0:T(8,128)(2,1)S(1)}, u32[]{:S(2)}, u32[]{:S(2)}) collective-permute-start(bf16[2,128,512]{2,1,0:T(8,128)(2,1)} %get-tuple-element.28), channel_id=1, source_target_pairs={{0,1},{1,2},{2,3},{3,4},{4,5},{5,6},{6,7},{7,8},{8,9},{9,10},{10,1... | collective-permute-start | bytes 786440 | tf_op jit(solution)/shard_map/ppermute | solution.py:27
  133.5 63.5 %collective-permute-start.11 = (bf16[2,256,512]{2,1,0:T(8,128)(2,1)}, bf16[2,256,512]{2,1,0:T(8,128)(2,1)S(1)}, u32[]{:S(2)}, u32[]{:S(2)}) collective-permute-start(bf16[2,256,512]{2,1,0:T(8,128)(2,1)} %get-tuple-element.32), channel_id=1, source_target_pairs={{0,12},{1,13},{2,14},{3,15},{4,0},{5,1},{6,2},{7,3},{8,4},{9,5},{1... | collective-permute-start | bytes 1572872 | tf_op jit(solution)/shard_map/ppermute | solution.py:27
  135.7 56.9 %collective-permute-start.9 = (bf16[2,128,512]{2,1,0:T(8,128)(2,1)}, bf16[2,128,512]{2,1,0:T(8,128)(2,1)S(1)}, u32[]{:S(2)}, u32[]{:S(2)}) collective-permute-start(bf16[2,128,512]{2,1,0:T(8,128)(2,1)} %get-tuple-element.30), channel_id=1, source_target_pairs={{0,15},{1,0},{2,1},{3,2},{4,3},{5,4},{6,5},{7,6},{8,7},{9,8},{10,9... | collective-permute-start | bytes 786440 | tf_op jit(solution)/shard_map/ppermute | solution.py:27
  186.8 39.6 %collective-permute-start.6 = (bf16[2,128,1536]{2,1,0:T(8,128)(2,1)}, bf16[2,128,1536]{2,1,0:T(8,128)(2,1)S(1)}, u32[]{:S(2)}, u32[]{:S(2)}) collective-permute-start(bf16[2,128,1536]{2,1,0:T(8,128)(2,1)} %get-tuple-element.27), channel_id=1, source_target_pairs={{0,1},{1,2},{2,3},{3,4},{4,5},{5,6},{6,7},{7,8},{8,9},{9,10},{10,1... | collective-permute-start | bytes 2359304 | tf_op jit(solution)/shard_map/ppermute | solution.py:27
  192.5 33.8 %collective-permute-start.8 = (bf16[2,128,1536]{2,1,0:T(8,128)(2,1)}, bf16[2,128,1536]{2,1,0:T(8,128)(2,1)S(1)}, u32[]{:S(2)}, u32[]{:S(2)}) collective-permute-start(bf16[2,128,1536]{2,1,0:T(8,128)(2,1)} %get-tuple-element.29), channel_id=1, source_target_pairs={{0,15},{1,0},{2,1},{3,2},{4,3},{5,4},{6,5},{7,6},{8,7},{9,8},{10,9... | collective-permute-start | bytes 2359304 | tf_op jit(solution)/shard_map/ppermute | solution.py:27
  197.1 29.3 %collective-permute-start.13 = (bf16[2,256,512]{2,1,0:T(8,128)(2,1)}, bf16[2,256,512]{2,1,0:T(8,128)(2,1)S(1)}, u32[]{:S(2)}, u32[]{:S(2)}) collective-permute-start(bf16[2,256,512]{2,1,0:T(8,128)(2,1)} %get-tuple-element.34), channel_id=1, source_target_pairs={{0,4},{1,5},{2,6},{3,7},{4,8},{5,9},{6,10},{7,11},{8,12},{9,13},{1... | collective-permute-start | bytes 1572872 | tf_op jit(solution)/shard_map/ppermute | solution.py:27

commit v6 on v5

--- a/solution.py
+++ b/solution.py
@@ -93,12 +93,11 @@
     assert sum(CHUNK_STEPS) == steps
     bases = [sum(CHUNK_STEPS[:c]) for c in range(len(CHUNK_STEPS))]
     chunked = [kv[:, :, b * width_step:(b + n) * width_step] for b, n in zip(bases, CHUNK_STEPS)]
-    left = shifted(kv[:, rows - BLK:], "seq", 1)
-    right = shifted(kv[:, :BLK], "seq", -1)
-    chunked, left, right = lax.optimization_barrier((chunked, left, right))
     far = []
     for part in chunked:
         far.append((shifted(part, "seq", FRAME_DEV), shifted(part, "seq", -FRAME_DEV)))
+    left = shifted(kv[:, rows - BLK:], "seq", 1)
+    right = shifted(kv[:, :BLK], "seq", -1)
 
     d_queries = own = None
     received = []

time: 231 us -> 219 us (0.948)
  waiting for transfers between devices: 151 us -> 139 us
    ppermute x14, waiting for transfers between devices: 151 us -> 139 us  [shifted(): return lax.ppermute(tree, axis, route)]
  transfers between devices with their start and end apart: 14 -> 14, of which waited for: 7 -> 5; matrix products, arithmetic and copies ran while one was open for 2% -> 2% of each run, Pallas kernels for 12% -> 12%
where the time goes in v6:
time: 219 us
  waiting for transfers between devices  139 us (63%)
  starting transfers between devices  42 us (19%)
  Pallas kernels  26.6 us (12%)
  other arithmetic  7.9 us (4%)
  local copies, waits for them, and re-layouts  2.87 us (1%)
    ppermute x14, waiting for transfers between devices, shifted(): return lax.ppermute(tree, axis, route)  139 us
    ppermute x14, starting transfers between devices, shifted(): return lax.ppermute(tree, axis, route)  42 us
    pallas_call x2, Pallas kernels, body(): pl.pallas_call(lambda *refs, a=aliased: attend_kernel(*refs, scale=scale,...  26.6 us
    another operation x4, other arithmetic, body(): kv = jnp.stack([keys, values])  5.07 us
  transfers between devices with their start and end apart: 14, of which 5 were waited for; matrix products, arithmetic and copies ran while one was open for 2% of the time, Pallas kernels for 12%

profile of v6, /device:TPU:0, one launch (start us, length us, event | category | flops | bytes accessed | tf_op | source)
XLA Modules:
  0.0 219.1 jit_solution(8547164267817136924)
XLA Ops:
  0.7 1.7 fusion
  2.3 5.1 %collective-permute-start.5 = (bf16[2,256,1536]{2,1,0:T(8,128)(2,1)S(1)}, bf16[2,256,1536]{2,1,0:T(8,128)(2,1)}, u32[]{:S(2)}, u32[]{:S(2)}) collective-permute-start(bf16[2,256,1536]{2,1,0:T(8,128)(2,1)S(1)} %fusion), channel_id=1, source_target_pairs={{0,12},{1,13},{2,14},{3,15},{4,0},{5,1},{6,2},{7,3},{8,4},{9,5},{1... | collective-permute-start | bytes 4718600 | tf_op jit(solution)/shard_map/ppermute | solution.py:27
  7.4 0.0 collective-permute-start.4
  7.4 0.2 fusion.2
  7.6 0.0 copy-start.4
  7.6 0.0 copy-start.5
  7.6 3.7 %collective-permute-start.1 = (bf16[2,128,2048]{2,1,0:T(8,128)(2,1)S(1)}, bf16[2,128,2048]{2,1,0:T(8,128)(2,1)S(1)}, u32[]{:S(2)}, u32[]{:S(2)}) collective-permute-start(bf16[2,128,2048]{2,1,0:T(8,128)(2,1)S(1)} %get-tuple-element.29), channel_id=1, source_target_pairs={{0,15},{1,0},{2,1},{3,2},{4,3},{5,4},{6,5},{7,6},{8,7},{9,8},{10,9... | collective-permute-start | bytes 3145736 | tf_op jit(solution)/shard_map/ppermute | solution.py:27
  11.3 0.9 fusion.3
  12.2 0.7 collective-permute-start.3
  12.9 2.4 %pad_maximum_fusion = (bf16[2,256,2048]{2,1,0:T(8,128)(2,1)}, bf16[2,256,2048]{2,1,0:T(8,128)(2,1)}) fusion(bf16[1,256,2048]{2,1,0:T(8,128)(2,1)S(1)} %bitcast.11, bf16[1,256,2048]{2,1,0:T(8,128)(2,1)S(1)} %bitcast.15, bf16[1,256,2048]{2,1,0:T(8,128)(2,1)S(1)} %bitcast.16, bf16[1,256,2048]{2,1,0:T(8,128)(2,1)S(1)} %bitcast.17), kind=kLoop, calls=%fused_computation.5 | loop fusion | flops 2097152 | bytes 8388608 | tf_op jit(solution)/shard_map/stack | solution.py:90
  15.3 83.2 %collective-permute-done.1.refs_4_ = bf16[2,128,2048]{2,1,0:T(8,128)(2,1)S(1)} collective-permute-done((bf16[2,128,2048]{2,1,0:T(8,128)(2,1)S(1)}, bf16[2,128,2048]{2,1,0:T(8,128)(2,1)S(1)}, u32[]{:S(2)}, u32[]{:S(2)}) %collective-permute-start.1) | collective-permute-done | bytes 1048608 | tf_op jit(solution)/shard_map/ppermute | solution.py:27
  98.4 0.0 collective-permute-start.2
  98.4 0.0 collective-permute-done.refs_3_
  98.5 0.0 collective-permute-done.5.refs_6_
  98.5 0.9 copy-done.2
  99.4 0.3 copy-done.3
  99.8 18.1 %shard_map.76 = (bf16[256,2048]{1,0:T(8,128)(2,1)}, f32[2,256,2048]{2,1,0:T(8,128)}, bf16[2,128,1536]{2,1,0:T(8,128)(2,1)}, bf16[2,128,1536]{2,1,0:T(8,128)(2,1)...) custom-call(s32[2,4]{1,0:T(2,128)} %refs_0_.3, bf16[2,256,2048]{2,1,0:T(8,128)(2,1)} %get-tuple-element.32.refs_1_, ...), custom_call_target="tpu_custom_call" | custom-call | flops 2013265920 | bytes 11010048 | tf_op jit(solution)/shard_map/pallas_call | solution.py:121
  117.9 3.5 %collective-permute-start.10 = (bf16[2,256,1536]{2,1,0:T(8,128)(2,1)}, bf16[2,256,1536]{2,1,0:T(8,128)(2,1)S(1)}, u32[]{:S(2)}, u32[]{:S(2)}) collective-permute-start(bf16[2,256,1536]{2,1,0:T(8,128)(2,1)} %get-tuple-element.23), channel_id=1, source_target_pairs={{0,12},{1,13},{2,14},{3,15},{4,0},{5,1},{6,2},{7,3},{8,4},{9,5},{1... | collective-permute-start | bytes 4718600 | tf_op jit(solution)/shard_map/ppermute | solution.py:27
  121.4 0.0 collective-permute-start.12
  121.4 0.0 collective-permute-done.3.refs_6_
  121.4 0.5 collective-permute-done.2.refs_5_
  121.9 8.5 %shard_map.77 = (bf16[256,2048]{1,0:T(8,128)(2,1)}, f32[2,256,2048]{2,1,0:T(8,128)}, bf16[2,128,512]{2,1,0:T(8,128)(2,1)}, bf16[2,128,512]{2,1,0:T(8,128)(2,1)},...) custom-call(s32[2,4]{1,0:T(2,128)} %refs_0_.3, ...), custom_call_target="tpu_custom_call", output_to_operand_aliasing={{0}: (7, {}), {1}: (8, {})} | custom-call | flops 671088640 | bytes 3670016 | tf_op jit(solution)/shard_map/pallas_call | solution.py:121
  130.4 0.0 collective-permute-start.7
  130.4 22.1 %collective-permute-start.11 = (bf16[2,256,512]{2,1,0:T(8,128)(2,1)}, bf16[2,256,512]{2,1,0:T(8,128)(2,1)S(1)}, u32[]{:S(2)}, u32[]{:S(2)}) collective-permute-start(bf16[2,256,512]{2,1,0:T(8,128)(2,1)} %get-tuple-element.24), channel_id=1, source_target_pairs={{0,12},{1,13},{2,14},{3,15},{4,0},{5,1},{6,2},{7,3},{8,4},{9,5},{1... | collective-permute-start | bytes 1572872 | tf_op jit(solution)/shard_map/ppermute | solution.py:27
  152.5 2.4 %collective-permute-start.9 = (bf16[2,128,512]{2,1,0:T(8,128)(2,1)}, bf16[2,128,512]{2,1,0:T(8,128)(2,1)S(1)}, u32[]{:S(2)}, u32[]{:S(2)}) collective-permute-start(bf16[2,128,512]{2,1,0:T(8,128)(2,1)} %get-tuple-element.22), channel_id=1, source_target_pairs={{0,15},{1,0},{2,1},{3,2},{4,3},{5,4},{6,5},{7,6},{8,7},{9,8},{10,9... | collective-permute-start | bytes 786440 | tf_op jit(solution)/shard_map/ppermute | solution.py:27
  154.9 31.5 %collective-permute-done.7 = bf16[2,128,512]{2,1,0:T(8,128)(2,1)S(1)} collective-permute-done((bf16[2,128,512]{2,1,0:T(8,128)(2,1)}, bf16[2,128,512]{2,1,0:T(8,128)(2,1)S(1)}, u32[]{:S(2)}, u32[]{:S(2)}) %collective-permute-start.7) | collective-permute-done | bytes 262176 | tf_op jit(solution)/shard_map/ppermute | solution.py:27
  186.4 0.0 collective-permute-start.6
  186.4 3.8 %collective-permute-done.9 = bf16[2,128,512]{2,1,0:T(8,128)(2,1)S(1)} collective-permute-done((bf16[2,128,512]{2,1,0:T(8,128)(2,1)}, bf16[2,128,512]{2,1,0:T(8,128)(2,1)S(1)}, u32[]{:S(2)}, u32[]{:S(2)}) %collective-permute-start.9) | collective-permute-done | bytes 262176 | tf_op jit(solution)/shard_map/ppermute | solution.py:27
  190.1 4.6 %collective-permute-start.8 = (bf16[2,128,1536]{2,1,0:T(8,128)(2,1)}, bf16[2,128,1536]{2,1,0:T(8,128)(2,1)S(1)}, u32[]{:S(2)}, u32[]{:S(2)}) collective-permute-start(bf16[2,128,1536]{2,1,0:T(8,128)(2,1)} %get-tuple-element.21), channel_id=1, source_target_pairs={{0,15},{1,0},{2,1},{3,2},{4,3},{5,4},{6,5},{7,6},{8,7},{9,8},{10,9... | collective-permute-start | bytes 2359304 | tf_op jit(solution)/shard_map/ppermute | solution.py:27
  194.7 20.0 %collective-permute-done.13 = bf16[2,256,512]{2,1,0:T(8,128)(2,1)S(1)} collective-permute-done((bf16[2,256,512]{2,1,0:T(8,128)(2,1)}, bf16[2,256,512]{2,1,0:T(8,128)(2,1)S(1)}, u32[]{:S(2)}, u32[]{:S(2)}) %collective-permute-start.13) | collective-permute-done | bytes 524320 | tf_op jit(solution)/shard_map/ppermute | solution.py:27
  214.7 2.8 %add_convert_fusion = bf16[2,256,2048]{2,1,0:T(8,128)(2,1)S(1)} fusion(f32[2,256,2048]{2,1,0:T(8,128)} %get-tuple-element.18, bf16[2,128,512]{2,1,0:T(8,128)(2,1)S(1)} %collective-permute-done.9, bf16[2,128,1536]{2,1,0:T(8,128)(2,1)S(1)} %collective-permute-done.8, bf16[2,128,512]{2,1,0:T(8,128)(2,1)S(1)} %collective-permute-done.7, ...), kind=kLoop, calls=%fused_computation | loop fusion | flops 20971520 | bytes 12582912 | tf_op jit(solution)/shard_map/convert_element_type | solution.py:150
  217.6 1.6 slice_bitcast_fusion
  (16 shorter events, 0.0 us)
Async XLA Ops:
  0.6 6.8 %copy-start = (bf16[256,2048]{1,0:T(8,128)(2,1)S(1)}, bf16[256,2048]{1,0:T(8,128)(2,1)}, u32[]{:S(2)}) copy-start(bf16[256,2048]{1,0:T(8,128)(2,1)} %param.7) | copy-start | bytes 3145732
  0.6 6.8 %copy-start.1 = (bf16[256,2048]{1,0:T(8,128)(2,1)S(1)}, bf16[256,2048]{1,0:T(8,128)(2,1)}, u32[]{:S(2)}) copy-start(bf16[256,2048]{1,0:T(8,128)(2,1)} %param.6) | copy-start | bytes 3145732
  2.3 96.1 %collective-permute-start.5 = (bf16[2,256,1536]{2,1,0:T(8,128)(2,1)S(1)}, bf16[2,256,1536]{2,1,0:T(8,128)(2,1)}, u32[]{:S(2)}, u32[]{:S(2)}) collective-permute-start(bf16[2,256,1536]{2,1,0:T(8,128)(2,1)S(1)} %fusion), channel_id=1, source_target_pairs={{0,12},{1,13},{2,14},{3,15},{4,0},{5,1},{6,2},{7,3},{8,4},{9,5},{1... | collective-permute-start | bytes 4718600 | tf_op jit(solution)/shard_map/ppermute | solution.py:27
  7.4 91.1 %collective-permute-start.4 = (bf16[2,256,1536]{2,1,0:T(8,128)(2,1)S(1)}, bf16[2,256,1536]{2,1,0:T(8,128)(2,1)}, u32[]{:S(2)}, u32[]{:S(2)}) collective-permute-start(bf16[2,256,1536]{2,1,0:T(8,128)(2,1)S(1)} %fusion), channel_id=1, source_target_pairs={{0,4},{1,5},{2,6},{3,7},{4,8},{5,9},{6,10},{7,11},{8,12},{9,13},{1... | collective-permute-start | bytes 4718600 | tf_op jit(solution)/shard_map/ppermute | solution.py:27
  7.6 5.3 %copy-start.4 = (bf16[256,2048]{1,0:T(8,128)(2,1)S(1)}, bf16[256,2048]{1,0:T(8,128)(2,1)}, u32[]{:S(2)}) copy-start(bf16[256,2048]{1,0:T(8,128)(2,1)} %param.8) | copy-start | bytes 3145732
  7.6 5.3 %copy-start.5 = (bf16[256,2048]{1,0:T(8,128)(2,1)S(1)}, bf16[256,2048]{1,0:T(8,128)(2,1)}, u32[]{:S(2)}) copy-start(bf16[256,2048]{1,0:T(8,128)(2,1)} %param.5) | copy-start | bytes 3145732
  7.6 90.8 %collective-permute-start.1 = (bf16[2,128,2048]{2,1,0:T(8,128)(2,1)S(1)}, bf16[2,128,2048]{2,1,0:T(8,128)(2,1)S(1)}, u32[]{:S(2)}, u32[]{:S(2)}) collective-permute-start(bf16[2,128,2048]{2,1,0:T(8,128)(2,1)S(1)} %get-tuple-element.29), channel_id=1, source_target_pairs={{0,15},{1,0},{2,1},{3,2},{4,3},{5,4},{6,5},{7,6},{8,7},{9,8},{10,9... | collective-permute-start | bytes 3145736 | tf_op jit(solution)/shard_map/ppermute | solution.py:27
  11.3 87.1 %collective-permute-start = (bf16[2,128,2048]{2,1,0:T(8,128)(2,1)S(1)}, bf16[2,128,2048]{2,1,0:T(8,128)(2,1)S(1)}, u32[]{:S(2)}, u32[]{:S(2)}) collective-permute-start(bf16[2,128,2048]{2,1,0:T(8,128)(2,1)S(1)} %get-tuple-element.30), channel_id=1, source_target_pairs={{0,1},{1,2},{2,3},{3,4},{4,5},{5,6},{6,7},{7,8},{8,9},{9,10},{10,1... | collective-permute-start | bytes 3145736 | tf_op jit(solution)/shard_map/ppermute | solution.py:27
  12.2 109.2 %collective-permute-start.3 = (bf16[2,256,512]{2,1,0:T(8,128)(2,1)}, bf16[2,256,512]{2,1,0:T(8,128)(2,1)}, u32[]{:S(2)}, u32[]{:S(2)}) collective-permute-start(bf16[2,256,512]{2,1,0:T(8,128)(2,1)} %fusion.3), channel_id=1, source_target_pairs={{0,12},{1,13},{2,14},{3,15},{4,0},{5,1},{6,2},{7,3},{8,4},{9,5},{1... | collective-permute-start | bytes 1572872 | tf_op jit(solution)/shard_map/ppermute | solution.py:27
  98.4 1.0 copy-start.2
  98.4 23.5 %collective-permute-start.2 = (bf16[2,256,512]{2,1,0:T(8,128)(2,1)}, bf16[2,256,512]{2,1,0:T(8,128)(2,1)}, u32[]{:S(2)}, u32[]{:S(2)}) collective-permute-start(bf16[2,256,512]{2,1,0:T(8,128)(2,1)} %fusion.3), channel_id=1, source_target_pairs={{0,4},{1,5},{2,6},{3,7},{4,8},{5,9},{6,10},{7,11},{8,12},{9,13},{1... | collective-permute-start | bytes 1572872 | tf_op jit(solution)/shard_map/ppermute | solution.py:27
  98.4 1.3 copy-start.3
  117.9 96.8 %collective-permute-start.10 = (bf16[2,256,1536]{2,1,0:T(8,128)(2,1)}, bf16[2,256,1536]{2,1,0:T(8,128)(2,1)S(1)}, u32[]{:S(2)}, u32[]{:S(2)}) collective-permute-start(bf16[2,256,1536]{2,1,0:T(8,128)(2,1)} %get-tuple-element.23), channel_id=1, source_target_pairs={{0,12},{1,13},{2,14},{3,15},{4,0},{5,1},{6,2},{7,3},{8,4},{9,5},{1... | collective-permute-start | bytes 4718600 | tf_op jit(solution)/shard_map/ppermute | solution.py:27
  121.4 93.3 %collective-permute-start.12 = (bf16[2,256,1536]{2,1,0:T(8,128)(2,1)}, bf16[2,256,1536]{2,1,0:T(8,128)(2,1)S(1)}, u32[]{:S(2)}, u32[]{:S(2)}) collective-permute-start(bf16[2,256,1536]{2,1,0:T(8,128)(2,1)} %get-tuple-element.25), channel_id=1, source_target_pairs={{0,4},{1,5},{2,6},{3,7},{4,8},{5,9},{6,10},{7,11},{8,12},{9,13},{1... | collective-permute-start | bytes 4718600 | tf_op jit(solution)/shard_map/ppermute | solution.py:27
  130.4 55.9 %collective-permute-start.7 = (bf16[2,128,512]{2,1,0:T(8,128)(2,1)}, bf16[2,128,512]{2,1,0:T(8,128)(2,1)S(1)}, u32[]{:S(2)}, u32[]{:S(2)}) collective-permute-start(bf16[2,128,512]{2,1,0:T(8,128)(2,1)} %get-tuple-element.20), channel_id=1, source_target_pairs={{0,1},{1,2},{2,3},{3,4},{4,5},{5,6},{6,7},{7,8},{8,9},{9,10},{10,1... | collective-permute-start | bytes 786440 | tf_op jit(solution)/shard_map/ppermute | solution.py:27
  130.4 64.3 %collective-permute-start.11 = (bf16[2,256,512]{2,1,0:T(8,128)(2,1)}, bf16[2,256,512]{2,1,0:T(8,128)(2,1)S(1)}, u32[]{:S(2)}, u32[]{:S(2)}) collective-permute-start(bf16[2,256,512]{2,1,0:T(8,128)(2,1)} %get-tuple-element.24), channel_id=1, source_target_pairs={{0,12},{1,13},{2,14},{3,15},{4,0},{5,1},{6,2},{7,3},{8,4},{9,5},{1... | collective-permute-start | bytes 1572872 | tf_op jit(solution)/shard_map/ppermute | solution.py:27
  152.5 37.6 %collective-permute-start.9 = (bf16[2,128,512]{2,1,0:T(8,128)(2,1)}, bf16[2,128,512]{2,1,0:T(8,128)(2,1)S(1)}, u32[]{:S(2)}, u32[]{:S(2)}) collective-permute-start(bf16[2,128,512]{2,1,0:T(8,128)(2,1)} %get-tuple-element.22), channel_id=1, source_target_pairs={{0,15},{1,0},{2,1},{3,2},{4,3},{5,4},{6,5},{7,6},{8,7},{9,8},{10,9... | collective-permute-start | bytes 786440 | tf_op jit(solution)/shard_map/ppermute | solution.py:27
  186.4 28.3 %collective-permute-start.6 = (bf16[2,128,1536]{2,1,0:T(8,128)(2,1)}, bf16[2,128,1536]{2,1,0:T(8,128)(2,1)S(1)}, u32[]{:S(2)}, u32[]{:S(2)}) collective-permute-start(bf16[2,128,1536]{2,1,0:T(8,128)(2,1)} %get-tuple-element.19), channel_id=1, source_target_pairs={{0,1},{1,2},{2,3},{3,4},{4,5},{5,6},{6,7},{7,8},{8,9},{9,10},{10,1... | collective-permute-start | bytes 2359304 | tf_op jit(solution)/shard_map/ppermute | solution.py:27
  190.1 24.6 %collective-permute-start.8 = (bf16[2,128,1536]{2,1,0:T(8,128)(2,1)}, bf16[2,128,1536]{2,1,0:T(8,128)(2,1)S(1)}, u32[]{:S(2)}, u32[]{:S(2)}) collective-permute-start(bf16[2,128,1536]{2,1,0:T(8,128)(2,1)} %get-tuple-element.21), channel_id=1, source_target_pairs={{0,15},{1,0},{2,1},{3,2},{4,3},{5,4},{6,5},{7,6},{8,7},{9,8},{10,9... | collective-permute-start | bytes 2359304 | tf_op jit(solution)/shard_map/ppermute | solution.py:27
  194.7 20.0 %collective-permute-start.13 = (bf16[2,256,512]{2,1,0:T(8,128)(2,1)}, bf16[2,256,512]{2,1,0:T(8,128)(2,1)S(1)}, u32[]{:S(2)}, u32[]{:S(2)}) collective-permute-start(bf16[2,256,512]{2,1,0:T(8,128)(2,1)} %get-tuple-element.26), channel_id=1, source_target_pairs={{0,4},{1,5},{2,6},{3,7},{4,8},{5,9},{6,10},{7,11},{8,12},{9,13},{1... | collective-permute-start | bytes 1572872 | tf_op jit(solution)/shard_map/ppermute | solution.py:27

commit v7 on v6

--- a/solution.py
+++ b/solution.py
@@ -5,7 +5,7 @@
 from jax import lax
 from jax.experimental import pallas as pl
 from jax.experimental.pallas import tpu as pltpu
-from jax.sharding import PartitionSpec as P
+from jax.sharding import Mesh, PartitionSpec as P
 
 BLK = 128
 LOCAL_HEADS = 16
@@ -19,6 +19,24 @@
 TN = (((0,), (0,)), ((), ()))
 F32 = jnp.float32
 BF16 = jnp.bfloat16
+
+
+SEQ = ("pair", "core")
+
+
+def crossing(tree):
+    count = lax.axis_size(SEQ)
+    route = [(i, (i - 1 if i % 2 == 0 else i + 1) % count) for i in range(count)]
+    return lax.ppermute(tree, SEQ, route)
+
+
+def swap_edges(for_left, for_right):
+    core = lax.axis_index("core")
+    even = core == 0
+    across = crossing(jnp.where(even, for_left, for_right))
+    gathered = lax.all_gather(jnp.where(even, for_right, for_left), "core")
+    partner = lax.dynamic_index_in_dim(gathered, 1 - core, keepdims=False)
+    return jnp.where(even, across, partner), jnp.where(even, partner, across)
 
 
 def shifted(tree, axis, distance):
@@ -95,9 +113,8 @@
     chunked = [kv[:, :, b * width_step:(b + n) * width_step] for b, n in zip(bases, CHUNK_STEPS)]
     far = []
     for part in chunked:
-        far.append((shifted(part, "seq", FRAME_DEV), shifted(part, "seq", -FRAME_DEV)))
-    left = shifted(kv[:, rows - BLK:], "seq", 1)
-    right = shifted(kv[:, :BLK], "seq", -1)
+        far.append((shifted(part, SEQ, FRAME_DEV), shifted(part, SEQ, -FRAME_DEV)))
+    left, right = swap_edges(kv[:, :BLK], kv[:, rows - BLK:])
 
     d_queries = own = None
     received = []
@@ -139,8 +156,8 @@
             cost_estimate=cost,
         )(key_lists, qd, kv, left, right, far[c][0], far[c][1], *extra_args)
         received.append((
-            shifted(to_right, "seq", 1), shifted(to_left, "seq", -1),
-            shifted(to_late, "seq", FRAME_DEV), shifted(to_early, "seq", -FRAME_DEV),
+            shifted(to_right, SEQ, 1), shifted(to_left, SEQ, -1),
+            shifted(to_late, SEQ, FRAME_DEV), shifted(to_early, SEQ, -FRAME_DEV),
         ))
     from_left, from_right, from_early, from_late = (
         jnp.concatenate([r[k] for r in received], axis=-1) for k in range(4)
@@ -152,10 +169,12 @@
 
 
 def solution(mesh):
-    spec = P(("groups", "seq"), None)
+    groups, seq = mesh.devices.shape
+    paired = Mesh(mesh.devices.reshape(groups, seq // 2, 2), ("groups",) + SEQ)
+    spec = P(("groups",) + SEQ, None)
     return jax.shard_map(
         body,
-        mesh=mesh,
+        mesh=paired,
         in_specs=(spec, spec, spec, spec, spec),
         out_specs=(spec, spec, spec),
         check_vma=False,

time: 219 us -> 242 us (1.11)
  between operations: 0.73 us -> 14.1 us
  waiting for transfers between devices: 139 us -> 148 us
  other arithmetic: 7.9 us -> 14.4 us
  starting transfers between devices: 42 us -> 36.4 us
    ppermute x0 -> x1, waiting for transfers between devices: none -> 11.5 us  [crossing(): return lax.ppermute(tree, SEQ, route)]
    ppermute x14 -> x12, starting transfers between devices: 42 us -> 30.9 us  [shifted(): return lax.ppermute(tree, axis, route)]
    select_n x0 -> x2, other arithmetic: none -> 6.39 us  [the longest x1 3.39 us: swap_edges(): gathered = lax.all_gather(jnp.where(even, for_right, for_left), 'core')]
    ppermute x0 -> x1, starting transfers between devices: none -> 5.48 us  [crossing(): return lax.ppermute(tree, SEQ, route)]
    ppermute x14 -> x12, waiting for transfers between devices: 139 us -> 136 us  [shifted(): return lax.ppermute(tree, axis, route)]
    another operation x4 -> x3, other arithmetic: 5.07 us -> 3.7 us  [body(): kv = jnp.stack([keys, values])]
  transfers between devices with their start and end apart: 14 -> 14, of which waited for: 5 -> 6; matrix products, arithmetic and copies ran while one was open for 2% -> 3% of each run, Pallas kernels for 12% -> 11%
where the time goes in v7:
time: 242 us
  waiting for transfers between devices  148 us (61%)
  starting transfers between devices  36.4 us (15%)
  Pallas kernels  26.7 us (11%)
  other arithmetic  14.4 us (6%)
  between operations  14.1 us (6%)
    ppermute x12, waiting for transfers between devices, shifted(): return lax.ppermute(tree, axis, route)  136 us
    ppermute x12, starting transfers between devices, shifted(): return lax.ppermute(tree, axis, route)  30.9 us
    pallas_call x2, Pallas kernels, body(): pl.pallas_call(lambda *refs, a=aliased: attend_kernel(*refs, scale=scale,...  26.7 us
    ppermute x1, waiting for transfers between devices, crossing(): return lax.ppermute(tree, SEQ, route)  11.5 us
    ppermute x1, starting transfers between devices, crossing(): return lax.ppermute(tree, SEQ, route)  5.48 us
  transfers between devices with their start and end apart: 14, of which 6 were waited for; matrix products, arithmetic and copies ran while one was open for 3% of the time, Pallas kernels for 11%

profile of v7, /device:TPU:0, one launch (start us, length us, event | category | flops | bytes accessed | tf_op | source)
XLA Modules:
  0.0 241.9 jit_solution(3295289338451196676)
XLA Ops:
  7.2 0.0 all-gather.3.cloned.1.call-start
  7.2 3.4 %broadcast_select_fusion = (bf16[2,128,2048]{2,1,0:T(8,128)(2,1)}, bf16[2,128,2048]{2,1,0:T(8,128)(2,1)S(1)}) fusion(pred[]{:T(512)S(6)} %eq.3, bf16[1,256,2048]{2,1,0:T(8,128)(2,1)} %bitcast.12, bf16[1,256,2048]{2,1,0:T(8,128)(2,1)} %bitcast.16), kind=kLoop, calls=%fused_computation.18 | loop fusion | flops 3145728 | bytes 4194305 | tf_op jit(solution)/shard_map/jit(_where)/select_n | solution.py:37
  10.6 0.0 all-gather.3.cloned.1.call-update
  10.7 5.5 %collective-permute-start = (bf16[2,128,2048]{2,1,0:T(8,128)(2,1)S(1)}, bf16[2,128,2048]{2,1,0:T(8,128)(2,1)}, u32[]{:S(2)}, u32[]{:S(2)}) collective-permute-start(bf16[2,128,2048]{2,1,0:T(8,128)(2,1)S(1)} %get-tuple-element.32), channel_id=1, source_target_pairs={{0,15},{1,2},{2,1},{3,4},{4,3},{5,6},{6,5},{7,8},{8,7},{9,10},{10,... | collective-permute-start | bytes 3145736 | tf_op jit(solution)/shard_map/ppermute | solution.py:30
  16.1 1.3 fusion
  17.4 0.4 collective-permute-start.4
  17.9 1.6 collective-permute-start.3
  19.5 0.9 fusion.3
  20.3 2.2 collective-permute-start.2
  22.6 0.0 collective-permute-start.1
  22.6 1.6 pad_maximum_fusion.refs_2_
  24.1 0.7 copy-done.3
  24.9 1.5 pad_maximum_fusion.1.refs_1_
  26.4 11.5 %collective-permute-done = bf16[2,128,2048]{2,1,0:T(8,128)(2,1)} collective-permute-done((bf16[2,128,2048]{2,1,0:T(8,128)(2,1)S(1)}, bf16[2,128,2048]{2,1,0:T(8,128)(2,1)}, u32[]{:S(2)}, u32[]{:S(2)}) %collective-permute-start) | collective-permute-done | bytes 1048608 | tf_op jit(solution)/shard_map/ppermute | solution.py:30
  37.9 3.0 %bitcast_select_fusion = (bf16[2,128,2048]{2,1,0:T(8,128)(2,1)}, bf16[2,128,2048]{2,1,0:T(8,128)(2,1)}) fusion(bf16[2,128,2048]{2,1,0:T(8,128)(2,1)} %collective-permute-done, pred[]{:T(512)S(6)} %eq.3, bf16[2,2,128,2048]{3,2,1,0:T(8,128)(2,1)} %bitcast.22, s32[]{:T(128)S(6)} %select_n.27), kind=kLoop, calls=%fused_computation.16 | loop fusion | flops 1048576 | bytes 4194309 | tf_op jit(solution)/shard_map/jit(_where)/select_n | solution.py:39
  40.9 53.7 %collective-permute-done.4.refs_6_ = bf16[2,256,1536]{2,1,0:T(8,128)(2,1)} collective-permute-done((bf16[2,256,1536]{2,1,0:T(8,128)(2,1)}, bf16[2,256,1536]{2,1,0:T(8,128)(2,1)}, u32[]{:S(2)}, u32[]{:S(2)}) %collective-permute-start.4) | collective-permute-done | bytes 1572896 | tf_op jit(solution)/shard_map/ppermute | solution.py:45
  94.6 11.9 %collective-permute-done.3.refs_5_ = bf16[2,256,1536]{2,1,0:T(8,128)(2,1)} collective-permute-done((bf16[2,256,1536]{2,1,0:T(8,128)(2,1)}, bf16[2,256,1536]{2,1,0:T(8,128)(2,1)}, u32[]{:S(2)}, u32[]{:S(2)}) %collective-permute-start.3) | collective-permute-done | bytes 1572896 | tf_op jit(solution)/shard_map/ppermute | solution.py:45
  106.5 18.1 %shard_map.76 = (bf16[256,2048]{1,0:T(8,128)(2,1)}, f32[2,256,2048]{2,1,0:T(8,128)}, bf16[2,128,1536]{2,1,0:T(8,128)(2,1)}, bf16[2,128,1536]{2,1,0:T(8,128)(2,1)...) custom-call(s32[2,4]{1,0:T(2,128)} %refs_0_.3, bf16[2,256,2048]{2,1,0:T(8,128)(2,1)} %pad_maximum_fusion.1.refs_1_, ...), custom_call_target="tpu_custom_call" | custom-call | flops 2013265920 | bytes 11010048 | tf_op jit(solution)/shard_map/pallas_call | solution.py:138
  124.7 0.1 collective-permute-start.9
  124.7 2.0 collective-permute-start.11
  126.7 0.0 collective-permute-done.2.refs_6_
  126.7 0.0 collective-permute-done.1.refs_5_
  126.7 8.5 %shard_map.77 = (bf16[256,2048]{1,0:T(8,128)(2,1)}, f32[2,256,2048]{2,1,0:T(8,128)}, bf16[2,128,512]{2,1,0:T(8,128)(2,1)}, bf16[2,128,512]{2,1,0:T(8,128)(2,1)},...) custom-call(s32[2,4]{1,0:T(2,128)} %refs_0_.3, ...), custom_call_target="tpu_custom_call", output_to_operand_aliasing={{0}: (7, {}), {1}: (8, {})} | custom-call | flops 671088640 | bytes 3670016 | tf_op jit(solution)/shard_map/pallas_call | solution.py:138
  135.3 1.9 collective-permute-start.10
  137.1 18.0 %collective-permute-start.8 = (bf16[2,128,512]{2,1,0:T(8,128)(2,1)}, bf16[2,128,512]{2,1,0:T(8,128)(2,1)S(1)}, u32[]{:S(2)}, u32[]{:S(2)}) collective-permute-start(bf16[2,128,512]{2,1,0:T(8,128)(2,1)} %get-tuple-element.22), channel_id=1, source_target_pairs={{0,15},{1,0},{2,1},{3,2},{4,3},{5,4},{6,5},{7,6},{8,7},{9,8},{10,9... | collective-permute-start | bytes 786440 | tf_op jit(solution)/shard_map/ppermute | solution.py:45
  155.2 39.4 %collective-permute-done.6 = bf16[2,128,512]{2,1,0:T(8,128)(2,1)S(1)} collective-permute-done((bf16[2,128,512]{2,1,0:T(8,128)(2,1)}, bf16[2,128,512]{2,1,0:T(8,128)(2,1)S(1)}, u32[]{:S(2)}, u32[]{:S(2)}) %collective-permute-start.6) | collective-permute-done | bytes 262176 | tf_op jit(solution)/shard_map/ppermute | solution.py:45
  194.6 11.4 %collective-permute-done.8 = bf16[2,128,512]{2,1,0:T(8,128)(2,1)S(1)} collective-permute-done((bf16[2,128,512]{2,1,0:T(8,128)(2,1)}, bf16[2,128,512]{2,1,0:T(8,128)(2,1)S(1)}, u32[]{:S(2)}, u32[]{:S(2)}) %collective-permute-start.8) | collective-permute-done | bytes 262176 | tf_op jit(solution)/shard_map/ppermute | solution.py:45
  206.0 4.6 %collective-permute-start.7 = (bf16[2,128,1536]{2,1,0:T(8,128)(2,1)}, bf16[2,128,1536]{2,1,0:T(8,128)(2,1)S(1)}, u32[]{:S(2)}, u32[]{:S(2)}) collective-permute-start(bf16[2,128,1536]{2,1,0:T(8,128)(2,1)} %get-tuple-element.21), channel_id=1, source_target_pairs={{0,15},{1,0},{2,1},{3,2},{4,3},{5,4},{6,5},{7,6},{8,7},{9,8},{10,9... | collective-permute-start | bytes 2359304 | tf_op jit(solution)/shard_map/ppermute | solution.py:45
  210.6 20.0 %collective-permute-done.12 = bf16[2,256,512]{2,1,0:T(8,128)(2,1)S(1)} collective-permute-done((bf16[2,256,512]{2,1,0:T(8,128)(2,1)}, bf16[2,256,512]{2,1,0:T(8,128)(2,1)S(1)}, u32[]{:S(2)}, u32[]{:S(2)}) %collective-permute-start.12) | collective-permute-done | bytes 524320 | tf_op jit(solution)/shard_map/ppermute | solution.py:45
  230.7 0.0 collective-permute-done.11
  230.7 2.8 %add_convert_fusion = bf16[2,256,2048]{2,1,0:T(8,128)(2,1)S(1)} fusion(f32[2,256,2048]{2,1,0:T(8,128)} %get-tuple-element.18, bf16[2,128,512]{2,1,0:T(8,128)(2,1)S(1)} %collective-permute-done.8, bf16[2,128,1536]{2,1,0:T(8,128)(2,1)S(1)} %collective-permute-done.7, bf16[2,128,512]{2,1,0:T(8,128)(2,1)S(1)} %collective-permute-done.6, ...), kind=kLoop, calls=%fused_computation | loop fusion | flops 20971520 | bytes 12582912 | tf_op jit(solution)/shard_map/convert_element_type | solution.py:167
  233.5 1.6 slice_bitcast_fusion
  (15 shorter events, 0.0 us)
Async XLA Ops:
  7.2 30.8 %all-gather.3.cloned.1.call-start = ((), (), s32[]{:S(2)}) async-start(), calls=%async_computation | async-start | bytes 3145728 | tf_op jit(solution)/shard_map/all_gather | solution.py:37
  7.2 8.9 %copy-start = (bf16[256,2048]{1,0:T(8,128)(2,1)S(1)}, bf16[256,2048]{1,0:T(8,128)(2,1)}, u32[]{:S(2)}) copy-start(bf16[256,2048]{1,0:T(8,128)(2,1)} %param.7) | copy-start | bytes 3145732
  7.2 8.9 %copy-start.1 = (bf16[256,2048]{1,0:T(8,128)(2,1)S(1)}, bf16[256,2048]{1,0:T(8,128)(2,1)}, u32[]{:S(2)}) copy-start(bf16[256,2048]{1,0:T(8,128)(2,1)} %param.6) | copy-start | bytes 3145732
  10.7 27.3 %collective-permute-start = (bf16[2,128,2048]{2,1,0:T(8,128)(2,1)S(1)}, bf16[2,128,2048]{2,1,0:T(8,128)(2,1)}, u32[]{:S(2)}, u32[]{:S(2)}) collective-permute-start(bf16[2,128,2048]{2,1,0:T(8,128)(2,1)S(1)} %get-tuple-element.32), channel_id=1, source_target_pairs={{0,15},{1,2},{2,1},{3,4},{4,3},{5,6},{6,5},{7,8},{8,7},{9,10},{10,... | collective-permute-start | bytes 3145736 | tf_op jit(solution)/shard_map/ppermute | solution.py:30
  17.4 77.2 %collective-permute-start.4 = (bf16[2,256,1536]{2,1,0:T(8,128)(2,1)}, bf16[2,256,1536]{2,1,0:T(8,128)(2,1)}, u32[]{:S(2)}, u32[]{:S(2)}) collective-permute-start(bf16[2,256,1536]{2,1,0:T(8,128)(2,1)} %fusion), channel_id=1, source_target_pairs={{0,12},{1,13},{2,14},{3,15},{4,0},{5,1},{6,2},{7,3},{8,4},{9,5},{1... | collective-permute-start | bytes 4718600 | tf_op jit(solution)/shard_map/ppermute | solution.py:45
  17.9 88.6 %collective-permute-start.3 = (bf16[2,256,1536]{2,1,0:T(8,128)(2,1)}, bf16[2,256,1536]{2,1,0:T(8,128)(2,1)}, u32[]{:S(2)}, u32[]{:S(2)}) collective-permute-start(bf16[2,256,1536]{2,1,0:T(8,128)(2,1)} %fusion), channel_id=1, source_target_pairs={{0,4},{1,5},{2,6},{3,7},{4,8},{5,9},{6,10},{7,11},{8,12},{9,13},{1... | collective-permute-start | bytes 4718600 | tf_op jit(solution)/shard_map/ppermute | solution.py:45
  20.3 106.4 %collective-permute-start.2 = (bf16[2,256,512]{2,1,0:T(8,128)(2,1)}, bf16[2,256,512]{2,1,0:T(8,128)(2,1)}, u32[]{:S(2)}, u32[]{:S(2)}) collective-permute-start(bf16[2,256,512]{2,1,0:T(8,128)(2,1)} %fusion.3), channel_id=1, source_target_pairs={{0,12},{1,13},{2,14},{3,15},{4,0},{5,1},{6,2},{7,3},{8,4},{9,5},{1... | collective-permute-start | bytes 1572872 | tf_op jit(solution)/shard_map/ppermute | solution.py:45
  22.6 104.2 %collective-permute-start.1 = (bf16[2,256,512]{2,1,0:T(8,128)(2,1)}, bf16[2,256,512]{2,1,0:T(8,128)(2,1)}, u32[]{:S(2)}, u32[]{:S(2)}) collective-permute-start(bf16[2,256,512]{2,1,0:T(8,128)(2,1)} %fusion.3), channel_id=1, source_target_pairs={{0,4},{1,5},{2,6},{3,7},{4,8},{5,9},{6,10},{7,11},{8,12},{9,13},{1... | collective-permute-start | bytes 1572872 | tf_op jit(solution)/shard_map/ppermute | solution.py:45
  22.6 1.6 copy-start.2
  22.6 2.3 copy-start.3
  124.7 106.0 %collective-permute-start.9 = (bf16[2,256,1536]{2,1,0:T(8,128)(2,1)}, bf16[2,256,1536]{2,1,0:T(8,128)(2,1)S(1)}, u32[]{:S(2)}, u32[]{:S(2)}) collective-permute-start(bf16[2,256,1536]{2,1,0:T(8,128)(2,1)} %get-tuple-element.23), channel_id=1, source_target_pairs={{0,12},{1,13},{2,14},{3,15},{4,0},{5,1},{6,2},{7,3},{8,4},{9,5},{1... | collective-permute-start | bytes 4718600 | tf_op jit(solution)/shard_map/ppermute | solution.py:45
  124.7 106.0 %collective-permute-start.11 = (bf16[2,256,1536]{2,1,0:T(8,128)(2,1)}, bf16[2,256,1536]{2,1,0:T(8,128)(2,1)S(1)}, u32[]{:S(2)}, u32[]{:S(2)}) collective-permute-start(bf16[2,256,1536]{2,1,0:T(8,128)(2,1)} %get-tuple-element.25), channel_id=1, source_target_pairs={{0,4},{1,5},{2,6},{3,7},{4,8},{5,9},{6,10},{7,11},{8,12},{9,13},{1... | collective-permute-start | bytes 4718600 | tf_op jit(solution)/shard_map/ppermute | solution.py:45
  135.3 59.3 %collective-permute-start.6 = (bf16[2,128,512]{2,1,0:T(8,128)(2,1)}, bf16[2,128,512]{2,1,0:T(8,128)(2,1)S(1)}, u32[]{:S(2)}, u32[]{:S(2)}) collective-permute-start(bf16[2,128,512]{2,1,0:T(8,128)(2,1)} %get-tuple-element.20), channel_id=1, source_target_pairs={{0,1},{1,2},{2,3},{3,4},{4,5},{5,6},{6,7},{7,8},{8,9},{9,10},{10,1... | collective-permute-start | bytes 786440 | tf_op jit(solution)/shard_map/ppermute | solution.py:45
  135.3 75.4 %collective-permute-start.10 = (bf16[2,256,512]{2,1,0:T(8,128)(2,1)}, bf16[2,256,512]{2,1,0:T(8,128)(2,1)S(1)}, u32[]{:S(2)}, u32[]{:S(2)}) collective-permute-start(bf16[2,256,512]{2,1,0:T(8,128)(2,1)} %get-tuple-element.24), channel_id=1, source_target_pairs={{0,12},{1,13},{2,14},{3,15},{4,0},{5,1},{6,2},{7,3},{8,4},{9,5},{1... | collective-permute-start | bytes 1572872 | tf_op jit(solution)/shard_map/ppermute | solution.py:45
  137.1 68.9 %collective-permute-start.8 = (bf16[2,128,512]{2,1,0:T(8,128)(2,1)}, bf16[2,128,512]{2,1,0:T(8,128)(2,1)S(1)}, u32[]{:S(2)}, u32[]{:S(2)}) collective-permute-start(bf16[2,128,512]{2,1,0:T(8,128)(2,1)} %get-tuple-element.22), channel_id=1, source_target_pairs={{0,15},{1,0},{2,1},{3,2},{4,3},{5,4},{6,5},{7,6},{8,7},{9,8},{10,9... | collective-permute-start | bytes 786440 | tf_op jit(solution)/shard_map/ppermute | solution.py:45
  194.6 36.1 %collective-permute-start.5 = (bf16[2,128,1536]{2,1,0:T(8,128)(2,1)}, bf16[2,128,1536]{2,1,0:T(8,128)(2,1)S(1)}, u32[]{:S(2)}, u32[]{:S(2)}) collective-permute-start(bf16[2,128,1536]{2,1,0:T(8,128)(2,1)} %get-tuple-element.19), channel_id=1, source_target_pairs={{0,1},{1,2},{2,3},{3,4},{4,5},{5,6},{6,7},{7,8},{8,9},{9,10},{10,1... | collective-permute-start | bytes 2359304 | tf_op jit(solution)/shard_map/ppermute | solution.py:45
  206.0 24.7 %collective-permute-start.7 = (bf16[2,128,1536]{2,1,0:T(8,128)(2,1)}, bf16[2,128,1536]{2,1,0:T(8,128)(2,1)S(1)}, u32[]{:S(2)}, u32[]{:S(2)}) collective-permute-start(bf16[2,128,1536]{2,1,0:T(8,128)(2,1)} %get-tuple-element.21), channel_id=1, source_target_pairs={{0,15},{1,0},{2,1},{3,2},{4,3},{5,4},{6,5},{7,6},{8,7},{9,8},{10,9... | collective-permute-start | bytes 2359304 | tf_op jit(solution)/shard_map/ppermute | solution.py:45
  210.6 20.0 %collective-permute-start.12 = (bf16[2,256,512]{2,1,0:T(8,128)(2,1)}, bf16[2,256,512]{2,1,0:T(8,128)(2,1)S(1)}, u32[]{:S(2)}, u32[]{:S(2)}) collective-permute-start(bf16[2,256,512]{2,1,0:T(8,128)(2,1)} %get-tuple-element.26), channel_id=1, source_target_pairs={{0,4},{1,5},{2,6},{3,7},{4,8},{5,9},{6,10},{7,11},{8,12},{9,13},{1... | collective-permute-start | bytes 1572872 | tf_op jit(solution)/shard_map/ppermute | solution.py:45
Sparse Core Ops, SparseCore 0:
  10.8 13.2 all-gather.2

commit v8 on v6

--- a/solution.py
+++ b/solution.py
@@ -13,7 +13,7 @@
 FRAME_DEV = 4
 BLK_DEV = 2
 STEP_HEADS = 4
-CHUNK_STEPS = (3, 1)
+CHUNKS = ((4, 3), (2, 2))
 
 NT = (((1,), (1,)), ((), ()))
 TN = (((0,), (0,)), ((), ()))
@@ -36,7 +36,7 @@
 
 
 def attend_kernel(kl_ref, qd_ref, kv_ref, left_ref, right_ref, early_ref, late_ref, *rest,
-                  scale, aliased):
+                  scale, aliased, step_heads):
     if aliased:
         rest = rest[2:]
     dq_ref, own_ref, to_left, to_right, to_early, to_late, acc_early, acc_late = rest
@@ -48,7 +48,7 @@
         to_side = to_left if i == 0 else to_right
         early = lax.rem(kl_ref[i, 2], BLK_DEV)
         late = lax.rem(kl_ref[i, 3], BLK_DEV)
-        for hh in range(STEP_HEADS):
+        for hh in range(step_heads):
             c = cols(hh)
             q = qd_ref[0, rows, c]
             do = qd_ref[1, rows, c]
@@ -89,10 +89,10 @@
 
     kv = jnp.stack([keys, values])
     qd = jnp.stack([queries, d_out])
-    width_step = HEAD_SIZE * STEP_HEADS
-    assert sum(CHUNK_STEPS) == steps
-    bases = [sum(CHUNK_STEPS[:c]) for c in range(len(CHUNK_STEPS))]
-    chunked = [kv[:, :, b * width_step:(b + n) * width_step] for b, n in zip(bases, CHUNK_STEPS)]
+    spans = [step_heads * HEAD_SIZE * count for step_heads, count in CHUNKS]
+    starts = [sum(spans[:c]) for c in range(len(CHUNKS))]
+    assert sum(spans) == width
+    chunked = [kv[:, :, a:a + n] for a, n in zip(starts, spans)]
     far = []
     for part in chunked:
         far.append((shifted(part, "seq", FRAME_DEV), shifted(part, "seq", -FRAME_DEV)))
@@ -101,9 +101,11 @@
 
     d_queries = own = None
     received = []
-    for c, (base, chunk_steps) in enumerate(zip(bases, CHUNK_STEPS)):
-        chunk_width = chunk_steps * width_step
-        heads = chunk_steps * STEP_HEADS
+    for c, (step_heads, chunk_steps) in enumerate(CHUNKS):
+        width_step = HEAD_SIZE * step_heads
+        base = starts[c] // width_step
+        chunk_width = spans[c]
+        heads = chunk_steps * step_heads
         cost = pl.CostEstimate(
             flops=2 * BLK * 4 * BLK * HEAD_SIZE * 5 * BLK_DEV * heads,
             transcendentals=2 * BLK * 4 * BLK * BLK_DEV * heads,
@@ -119,7 +121,8 @@
         extra_args = [d_queries, own] if aliased else []
         aliases = {7: 0, 8: 1} if aliased else {}
         d_queries, own, to_left, to_right, to_early, to_late = pl.pallas_call(
-            lambda *refs, a=aliased: attend_kernel(*refs, scale=scale, aliased=a),
+            lambda *refs, a=aliased, k=step_heads: attend_kernel(
+                *refs, scale=scale, aliased=a, step_heads=k),
             grid_spec=pltpu.PrefetchScalarGridSpec(
                 num_scalar_prefetch=1,
                 grid=(chunk_steps,),

time: 219 us -> 219 us (level)
  no operation moved by 1% of the time
where the time goes in v8:
time: 219 us
  waiting for transfers between devices  139 us (63%)
  starting transfers between devices  42.1 us (19%)
  Pallas kernels  26.1 us (12%)
  other arithmetic  7.9 us (4%)
  local copies, waits for them, and re-layouts  2.87 us (1%)
    ppermute x14, waiting for transfers between devices, shifted(): return lax.ppermute(tree, axis, route)  139 us
    ppermute x14, starting transfers between devices, shifted(): return lax.ppermute(tree, axis, route)  42.1 us
    pallas_call x2, Pallas kernels, body(): pl.pallas_call(lambda *refs, a=aliased, k=step_heads: attend_kernel(*refs...  26.1 us
    another operation x4, other arithmetic, body(): kv = jnp.stack([keys, values])  5.07 us
  transfers between devices with their start and end apart: 14, of which 5 were waited for; matrix products, arithmetic and copies ran while one was open for 2% of the time, Pallas kernels for 12%

profile of v8, /device:TPU:0, one launch (start us, length us, event | category | flops | bytes accessed | tf_op | source)
XLA Modules:
  0.0 219.1 jit_solution(2553164296498652757)
XLA Ops:
  0.7 1.7 fusion
  2.3 5.1 %collective-permute-start.5 = (bf16[2,256,1536]{2,1,0:T(8,128)(2,1)S(1)}, bf16[2,256,1536]{2,1,0:T(8,128)(2,1)}, u32[]{:S(2)}, u32[]{:S(2)}) collective-permute-start(bf16[2,256,1536]{2,1,0:T(8,128)(2,1)S(1)} %fusion), channel_id=1, source_target_pairs={{0,12},{1,13},{2,14},{3,15},{4,0},{5,1},{6,2},{7,3},{8,4},{9,5},{1... | collective-permute-start | bytes 4718600 | tf_op jit(solution)/shard_map/ppermute | solution.py:27
  7.4 0.0 collective-permute-start.4
  7.4 0.2 fusion.2
  7.6 0.0 copy-start.4
  7.6 0.0 copy-start.5
  7.6 3.7 %collective-permute-start.1 = (bf16[2,128,2048]{2,1,0:T(8,128)(2,1)S(1)}, bf16[2,128,2048]{2,1,0:T(8,128)(2,1)S(1)}, u32[]{:S(2)}, u32[]{:S(2)}) collective-permute-start(bf16[2,128,2048]{2,1,0:T(8,128)(2,1)S(1)} %get-tuple-element.29), channel_id=1, source_target_pairs={{0,15},{1,0},{2,1},{3,2},{4,3},{5,4},{6,5},{7,6},{8,7},{9,8},{10,9... | collective-permute-start | bytes 3145736 | tf_op jit(solution)/shard_map/ppermute | solution.py:27
  11.3 0.9 fusion.3
  12.2 0.7 collective-permute-start.3
  12.9 2.4 %pad_maximum_fusion = (bf16[2,256,2048]{2,1,0:T(8,128)(2,1)}, bf16[2,256,2048]{2,1,0:T(8,128)(2,1)}) fusion(bf16[1,256,2048]{2,1,0:T(8,128)(2,1)S(1)} %bitcast.11, bf16[1,256,2048]{2,1,0:T(8,128)(2,1)S(1)} %bitcast.15, bf16[1,256,2048]{2,1,0:T(8,128)(2,1)S(1)} %bitcast.16, bf16[1,256,2048]{2,1,0:T(8,128)(2,1)S(1)} %bitcast.17), kind=kLoop, calls=%fused_computation.5 | loop fusion | flops 2097152 | bytes 8388608 | tf_op jit(solution)/shard_map/stack | solution.py:90
  15.3 83.2 %collective-permute-done.1.refs_4_ = bf16[2,128,2048]{2,1,0:T(8,128)(2,1)S(1)} collective-permute-done((bf16[2,128,2048]{2,1,0:T(8,128)(2,1)S(1)}, bf16[2,128,2048]{2,1,0:T(8,128)(2,1)S(1)}, u32[]{:S(2)}, u32[]{:S(2)}) %collective-permute-start.1) | collective-permute-done | bytes 1048608 | tf_op jit(solution)/shard_map/ppermute | solution.py:27
  98.4 0.0 collective-permute-start.2
  98.4 0.0 collective-permute-done.refs_3_
  98.5 0.0 collective-permute-done.5.refs_6_
  98.5 0.9 copy-done.2
  99.4 0.3 copy-done.3
  99.8 18.1 %shard_map.76 = (bf16[256,2048]{1,0:T(8,128)(2,1)}, f32[2,256,2048]{2,1,0:T(8,128)}, bf16[2,128,1536]{2,1,0:T(8,128)(2,1)}, bf16[2,128,1536]{2,1,0:T(8,128)(2,1)...) custom-call(s32[2,4]{1,0:T(2,128)} %refs_0_.3, bf16[2,256,2048]{2,1,0:T(8,128)(2,1)} %get-tuple-element.32.refs_1_, ...), custom_call_target="tpu_custom_call" | custom-call | flops 2013265920 | bytes 11010048 | tf_op jit(solution)/shard_map/pallas_call | solution.py:123
  117.9 3.5 %collective-permute-start.10 = (bf16[2,256,1536]{2,1,0:T(8,128)(2,1)}, bf16[2,256,1536]{2,1,0:T(8,128)(2,1)S(1)}, u32[]{:S(2)}, u32[]{:S(2)}) collective-permute-start(bf16[2,256,1536]{2,1,0:T(8,128)(2,1)} %get-tuple-element.23), channel_id=1, source_target_pairs={{0,12},{1,13},{2,14},{3,15},{4,0},{5,1},{6,2},{7,3},{8,4},{9,5},{1... | collective-permute-start | bytes 4718600 | tf_op jit(solution)/shard_map/ppermute | solution.py:27
  121.4 0.0 collective-permute-start.12
  121.4 0.0 collective-permute-done.3.refs_6_
  121.4 0.5 collective-permute-done.2.refs_5_
  121.9 8.0 %shard_map.77 = (bf16[256,2048]{1,0:T(8,128)(2,1)}, f32[2,256,2048]{2,1,0:T(8,128)}, bf16[2,128,512]{2,1,0:T(8,128)(2,1)}, bf16[2,128,512]{2,1,0:T(8,128)(2,1)},...) custom-call(s32[2,4]{1,0:T(2,128)} %refs_0_.3, ...), custom_call_target="tpu_custom_call", output_to_operand_aliasing={{0}: (7, {}), {1}: (8, {})} | custom-call | flops 671088640 | bytes 3670016 | tf_op jit(solution)/shard_map/pallas_call | solution.py:123
  129.9 0.1 collective-permute-start.7
  129.9 22.1 %collective-permute-start.11 = (bf16[2,256,512]{2,1,0:T(8,128)(2,1)}, bf16[2,256,512]{2,1,0:T(8,128)(2,1)S(1)}, u32[]{:S(2)}, u32[]{:S(2)}) collective-permute-start(bf16[2,256,512]{2,1,0:T(8,128)(2,1)} %get-tuple-element.24), channel_id=1, source_target_pairs={{0,12},{1,13},{2,14},{3,15},{4,0},{5,1},{6,2},{7,3},{8,4},{9,5},{1... | collective-permute-start | bytes 1572872 | tf_op jit(solution)/shard_map/ppermute | solution.py:27
  152.1 2.3 %collective-permute-start.9 = (bf16[2,128,512]{2,1,0:T(8,128)(2,1)}, bf16[2,128,512]{2,1,0:T(8,128)(2,1)S(1)}, u32[]{:S(2)}, u32[]{:S(2)}) collective-permute-start(bf16[2,128,512]{2,1,0:T(8,128)(2,1)} %get-tuple-element.22), channel_id=1, source_target_pairs={{0,15},{1,0},{2,1},{3,2},{4,3},{5,4},{6,5},{7,6},{8,7},{9,8},{10,9... | collective-permute-start | bytes 786440 | tf_op jit(solution)/shard_map/ppermute | solution.py:27
  154.4 32.0 %collective-permute-done.7 = bf16[2,128,512]{2,1,0:T(8,128)(2,1)S(1)} collective-permute-done((bf16[2,128,512]{2,1,0:T(8,128)(2,1)}, bf16[2,128,512]{2,1,0:T(8,128)(2,1)S(1)}, u32[]{:S(2)}, u32[]{:S(2)}) %collective-permute-start.7) | collective-permute-done | bytes 262176 | tf_op jit(solution)/shard_map/ppermute | solution.py:27
  186.4 0.0 collective-permute-start.6
  186.4 3.8 %collective-permute-done.9 = bf16[2,128,512]{2,1,0:T(8,128)(2,1)S(1)} collective-permute-done((bf16[2,128,512]{2,1,0:T(8,128)(2,1)}, bf16[2,128,512]{2,1,0:T(8,128)(2,1)S(1)}, u32[]{:S(2)}, u32[]{:S(2)}) %collective-permute-start.9) | collective-permute-done | bytes 262176 | tf_op jit(solution)/shard_map/ppermute | solution.py:27
  190.1 4.6 %collective-permute-start.8 = (bf16[2,128,1536]{2,1,0:T(8,128)(2,1)}, bf16[2,128,1536]{2,1,0:T(8,128)(2,1)S(1)}, u32[]{:S(2)}, u32[]{:S(2)}) collective-permute-start(bf16[2,128,1536]{2,1,0:T(8,128)(2,1)} %get-tuple-element.21), channel_id=1, source_target_pairs={{0,15},{1,0},{2,1},{3,2},{4,3},{5,4},{6,5},{7,6},{8,7},{9,8},{10,9... | collective-permute-start | bytes 2359304 | tf_op jit(solution)/shard_map/ppermute | solution.py:27
  194.7 20.0 %collective-permute-done.13 = bf16[2,256,512]{2,1,0:T(8,128)(2,1)S(1)} collective-permute-done((bf16[2,256,512]{2,1,0:T(8,128)(2,1)}, bf16[2,256,512]{2,1,0:T(8,128)(2,1)S(1)}, u32[]{:S(2)}, u32[]{:S(2)}) %collective-permute-start.13) | collective-permute-done | bytes 524320 | tf_op jit(solution)/shard_map/ppermute | solution.py:27
  214.7 2.8 %add_convert_fusion = bf16[2,256,2048]{2,1,0:T(8,128)(2,1)S(1)} fusion(f32[2,256,2048]{2,1,0:T(8,128)} %get-tuple-element.18, bf16[2,128,512]{2,1,0:T(8,128)(2,1)S(1)} %collective-permute-done.9, bf16[2,128,1536]{2,1,0:T(8,128)(2,1)S(1)} %collective-permute-done.8, bf16[2,128,512]{2,1,0:T(8,128)(2,1)S(1)} %collective-permute-done.7, ...), kind=kLoop, calls=%fused_computation | loop fusion | flops 20971520 | bytes 12582912 | tf_op jit(solution)/shard_map/convert_element_type | solution.py:153
  217.6 1.6 slice_bitcast_fusion
  (16 shorter events, 0.0 us)
Async XLA Ops:
  0.6 6.8 %copy-start = (bf16[256,2048]{1,0:T(8,128)(2,1)S(1)}, bf16[256,2048]{1,0:T(8,128)(2,1)}, u32[]{:S(2)}) copy-start(bf16[256,2048]{1,0:T(8,128)(2,1)} %param.7) | copy-start | bytes 3145732
  0.6 6.8 %copy-start.1 = (bf16[256,2048]{1,0:T(8,128)(2,1)S(1)}, bf16[256,2048]{1,0:T(8,128)(2,1)}, u32[]{:S(2)}) copy-start(bf16[256,2048]{1,0:T(8,128)(2,1)} %param.6) | copy-start | bytes 3145732
  2.3 96.1 %collective-permute-start.5 = (bf16[2,256,1536]{2,1,0:T(8,128)(2,1)S(1)}, bf16[2,256,1536]{2,1,0:T(8,128)(2,1)}, u32[]{:S(2)}, u32[]{:S(2)}) collective-permute-start(bf16[2,256,1536]{2,1,0:T(8,128)(2,1)S(1)} %fusion), channel_id=1, source_target_pairs={{0,12},{1,13},{2,14},{3,15},{4,0},{5,1},{6,2},{7,3},{8,4},{9,5},{1... | collective-permute-start | bytes 4718600 | tf_op jit(solution)/shard_map/ppermute | solution.py:27
  7.4 91.1 %collective-permute-start.4 = (bf16[2,256,1536]{2,1,0:T(8,128)(2,1)S(1)}, bf16[2,256,1536]{2,1,0:T(8,128)(2,1)}, u32[]{:S(2)}, u32[]{:S(2)}) collective-permute-start(bf16[2,256,1536]{2,1,0:T(8,128)(2,1)S(1)} %fusion), channel_id=1, source_target_pairs={{0,4},{1,5},{2,6},{3,7},{4,8},{5,9},{6,10},{7,11},{8,12},{9,13},{1... | collective-permute-start | bytes 4718600 | tf_op jit(solution)/shard_map/ppermute | solution.py:27
  7.6 5.3 %copy-start.4 = (bf16[256,2048]{1,0:T(8,128)(2,1)S(1)}, bf16[256,2048]{1,0:T(8,128)(2,1)}, u32[]{:S(2)}) copy-start(bf16[256,2048]{1,0:T(8,128)(2,1)} %param.8) | copy-start | bytes 3145732
  7.6 5.3 %copy-start.5 = (bf16[256,2048]{1,0:T(8,128)(2,1)S(1)}, bf16[256,2048]{1,0:T(8,128)(2,1)}, u32[]{:S(2)}) copy-start(bf16[256,2048]{1,0:T(8,128)(2,1)} %param.5) | copy-start | bytes 3145732
  7.6 90.8 %collective-permute-start.1 = (bf16[2,128,2048]{2,1,0:T(8,128)(2,1)S(1)}, bf16[2,128,2048]{2,1,0:T(8,128)(2,1)S(1)}, u32[]{:S(2)}, u32[]{:S(2)}) collective-permute-start(bf16[2,128,2048]{2,1,0:T(8,128)(2,1)S(1)} %get-tuple-element.29), channel_id=1, source_target_pairs={{0,15},{1,0},{2,1},{3,2},{4,3},{5,4},{6,5},{7,6},{8,7},{9,8},{10,9... | collective-permute-start | bytes 3145736 | tf_op jit(solution)/shard_map/ppermute | solution.py:27
  11.3 87.1 %collective-permute-start = (bf16[2,128,2048]{2,1,0:T(8,128)(2,1)S(1)}, bf16[2,128,2048]{2,1,0:T(8,128)(2,1)S(1)}, u32[]{:S(2)}, u32[]{:S(2)}) collective-permute-start(bf16[2,128,2048]{2,1,0:T(8,128)(2,1)S(1)} %get-tuple-element.30), channel_id=1, source_target_pairs={{0,1},{1,2},{2,3},{3,4},{4,5},{5,6},{6,7},{7,8},{8,9},{9,10},{10,1... | collective-permute-start | bytes 3145736 | tf_op jit(solution)/shard_map/ppermute | solution.py:27
  12.2 109.2 %collective-permute-start.3 = (bf16[2,256,512]{2,1,0:T(8,128)(2,1)}, bf16[2,256,512]{2,1,0:T(8,128)(2,1)}, u32[]{:S(2)}, u32[]{:S(2)}) collective-permute-start(bf16[2,256,512]{2,1,0:T(8,128)(2,1)} %fusion.3), channel_id=1, source_target_pairs={{0,12},{1,13},{2,14},{3,15},{4,0},{5,1},{6,2},{7,3},{8,4},{9,5},{1... | collective-permute-start | bytes 1572872 | tf_op jit(solution)/shard_map/ppermute | solution.py:27
  98.4 1.0 copy-start.2
  98.4 23.5 %collective-permute-start.2 = (bf16[2,256,512]{2,1,0:T(8,128)(2,1)}, bf16[2,256,512]{2,1,0:T(8,128)(2,1)}, u32[]{:S(2)}, u32[]{:S(2)}) collective-permute-start(bf16[2,256,512]{2,1,0:T(8,128)(2,1)} %fusion.3), channel_id=1, source_target_pairs={{0,4},{1,5},{2,6},{3,7},{4,8},{5,9},{6,10},{7,11},{8,12},{9,13},{1... | collective-permute-start | bytes 1572872 | tf_op jit(solution)/shard_map/ppermute | solution.py:27
  98.4 1.3 copy-start.3
  117.9 96.8 %collective-permute-start.10 = (bf16[2,256,1536]{2,1,0:T(8,128)(2,1)}, bf16[2,256,1536]{2,1,0:T(8,128)(2,1)S(1)}, u32[]{:S(2)}, u32[]{:S(2)}) collective-permute-start(bf16[2,256,1536]{2,1,0:T(8,128)(2,1)} %get-tuple-element.23), channel_id=1, source_target_pairs={{0,12},{1,13},{2,14},{3,15},{4,0},{5,1},{6,2},{7,3},{8,4},{9,5},{1... | collective-permute-start | bytes 4718600 | tf_op jit(solution)/shard_map/ppermute | solution.py:27
  121.4 93.3 %collective-permute-start.12 = (bf16[2,256,1536]{2,1,0:T(8,128)(2,1)}, bf16[2,256,1536]{2,1,0:T(8,128)(2,1)S(1)}, u32[]{:S(2)}, u32[]{:S(2)}) collective-permute-start(bf16[2,256,1536]{2,1,0:T(8,128)(2,1)} %get-tuple-element.25), channel_id=1, source_target_pairs={{0,4},{1,5},{2,6},{3,7},{4,8},{5,9},{6,10},{7,11},{8,12},{9,13},{1... | collective-permute-start | bytes 4718600 | tf_op jit(solution)/shard_map/ppermute | solution.py:27
  129.9 56.5 %collective-permute-start.7 = (bf16[2,128,512]{2,1,0:T(8,128)(2,1)}, bf16[2,128,512]{2,1,0:T(8,128)(2,1)S(1)}, u32[]{:S(2)}, u32[]{:S(2)}) collective-permute-start(bf16[2,128,512]{2,1,0:T(8,128)(2,1)} %get-tuple-element.20), channel_id=1, source_target_pairs={{0,1},{1,2},{2,3},{3,4},{4,5},{5,6},{6,7},{7,8},{8,9},{9,10},{10,1... | collective-permute-start | bytes 786440 | tf_op jit(solution)/shard_map/ppermute | solution.py:27
  129.9 64.8 %collective-permute-start.11 = (bf16[2,256,512]{2,1,0:T(8,128)(2,1)}, bf16[2,256,512]{2,1,0:T(8,128)(2,1)S(1)}, u32[]{:S(2)}, u32[]{:S(2)}) collective-permute-start(bf16[2,256,512]{2,1,0:T(8,128)(2,1)} %get-tuple-element.24), channel_id=1, source_target_pairs={{0,12},{1,13},{2,14},{3,15},{4,0},{5,1},{6,2},{7,3},{8,4},{9,5},{1... | collective-permute-start | bytes 1572872 | tf_op jit(solution)/shard_map/ppermute | solution.py:27
  152.1 38.1 %collective-permute-start.9 = (bf16[2,128,512]{2,1,0:T(8,128)(2,1)}, bf16[2,128,512]{2,1,0:T(8,128)(2,1)S(1)}, u32[]{:S(2)}, u32[]{:S(2)}) collective-permute-start(bf16[2,128,512]{2,1,0:T(8,128)(2,1)} %get-tuple-element.22), channel_id=1, source_target_pairs={{0,15},{1,0},{2,1},{3,2},{4,3},{5,4},{6,5},{7,6},{8,7},{9,8},{10,9... | collective-permute-start | bytes 786440 | tf_op jit(solution)/shard_map/ppermute | solution.py:27
  186.4 28.3 %collective-permute-start.6 = (bf16[2,128,1536]{2,1,0:T(8,128)(2,1)}, bf16[2,128,1536]{2,1,0:T(8,128)(2,1)S(1)}, u32[]{:S(2)}, u32[]{:S(2)}) collective-permute-start(bf16[2,128,1536]{2,1,0:T(8,128)(2,1)} %get-tuple-element.19), channel_id=1, source_target_pairs={{0,1},{1,2},{2,3},{3,4},{4,5},{5,6},{6,7},{7,8},{8,9},{9,10},{10,1... | collective-permute-start | bytes 2359304 | tf_op jit(solution)/shard_map/ppermute | solution.py:27
  190.1 24.6 %collective-permute-start.8 = (bf16[2,128,1536]{2,1,0:T(8,128)(2,1)}, bf16[2,128,1536]{2,1,0:T(8,128)(2,1)S(1)}, u32[]{:S(2)}, u32[]{:S(2)}) collective-permute-start(bf16[2,128,1536]{2,1,0:T(8,128)(2,1)} %get-tuple-element.21), channel_id=1, source_target_pairs={{0,15},{1,0},{2,1},{3,2},{4,3},{5,4},{6,5},{7,6},{8,7},{9,8},{10,9... | collective-permute-start | bytes 2359304 | tf_op jit(solution)/shard_map/ppermute | solution.py:27
  194.7 20.0 %collective-permute-start.13 = (bf16[2,256,512]{2,1,0:T(8,128)(2,1)}, bf16[2,256,512]{2,1,0:T(8,128)(2,1)S(1)}, u32[]{:S(2)}, u32[]{:S(2)}) collective-permute-start(bf16[2,256,512]{2,1,0:T(8,128)(2,1)} %get-tuple-element.26), channel_id=1, source_target_pairs={{0,4},{1,5},{2,6},{3,7},{4,8},{5,9},{6,10},{7,11},{8,12},{9,13},{1... | collective-permute-start | bytes 1572872 | tf_op jit(solution)/shard_map/ppermute | solution.py:27

commit v9 on v8

--- a/solution.py
+++ b/solution.py
@@ -145,12 +145,19 @@
             shifted(to_right, "seq", 1), shifted(to_left, "seq", -1),
             shifted(to_late, "seq", FRAME_DEV), shifted(to_early, "seq", -FRAME_DEV),
         ))
-    from_left, from_right, from_early, from_late = (
-        jnp.concatenate([r[k] for r in received], axis=-1) for k in range(4)
+    from_left, from_right, from_late = (
+        jnp.concatenate([r[k] for r in received], axis=-1) for k in (0, 1, 3)
     )
     side = jnp.concatenate([from_left, from_right], axis=1).astype(F32)
-    total = own + side + from_late.astype(F32) + from_early.astype(F32)
-    grads = total.astype(BF16)
+    settled = [r[2] for r in received[:-1]]
+    early_settled = jnp.concatenate(
+        settled + [jnp.zeros_like(received[-1][2])], axis=-1
+    ).astype(F32)
+    partial = lax.optimization_barrier(own + side + from_late.astype(F32) + early_settled)
+    last = jnp.concatenate(
+        [jnp.zeros(r[2].shape, BF16) for r in received[:-1]] + [received[-1][2]], axis=-1
+    )
+    grads = [(partial[n] + last[n].astype(F32)).astype(BF16) for n in range(2)]
     return (d_queries, grads[0], grads[1])
 
 

time: 219 us -> 231 us (1.055)
  waiting for transfers between devices: 139 us -> 152 us
    ppermute x14, waiting for transfers between devices: 139 us -> 152 us  [shifted(): return lax.ppermute(tree, axis, route)]
    add x0 -> x1, other arithmetic: none -> 2.74 us  [body(): own + side + from_late.astype(F32) + early_settled]
  transfers between devices with their start and end apart: 14 -> 14, of which waited for: 5 -> 5; matrix products, arithmetic and copies ran while one was open for 2% -> 3% of each run, Pallas kernels for 12% -> 11%
where the time goes in v9:
time: 231 us
  waiting for transfers between devices  152 us (66%)
  starting transfers between devices  41 us (18%)
  Pallas kernels  26 us (11%)
  other arithmetic  9.54 us (4%)
    ppermute x14, waiting for transfers between devices, shifted(): return lax.ppermute(tree, axis, route)  152 us
    ppermute x14, starting transfers between devices, shifted(): return lax.ppermute(tree, axis, route)  41 us
    pallas_call x2, Pallas kernels, body(): pl.pallas_call(lambda *refs, a=aliased, k=step_heads: attend_kernel(*refs...  26 us
    another operation x4, other arithmetic, body(): kv = jnp.stack([keys, values])  5.07 us
  transfers between devices with their start and end apart: 14, of which 5 were waited for; matrix products, arithmetic and copies ran while one was open for 3% of the time, Pallas kernels for 11%

profile of v9, /device:TPU:0, one launch (start us, length us, event | category | flops | bytes accessed | tf_op | source)
XLA Modules:
  0.0 230.8 jit_solution(13612527244879291761)
XLA Ops:
  0.7 1.7 fusion.2
  2.3 5.1 %collective-permute-start.5 = (bf16[2,256,1536]{2,1,0:T(8,128)(2,1)S(1)}, bf16[2,256,1536]{2,1,0:T(8,128)(2,1)}, u32[]{:S(2)}, u32[]{:S(2)}) collective-permute-start(bf16[2,256,1536]{2,1,0:T(8,128)(2,1)S(1)} %fusion.2), channel_id=1, source_target_pairs={{0,12},{1,13},{2,14},{3,15},{4,0},{5,1},{6,2},{7,3},{8,4},{9,5},{1... | collective-permute-start | bytes 4718600 | tf_op jit(solution)/shard_map/ppermute | solution.py:27
  7.4 0.2 fusion.6
  7.6 0.0 copy-start.4
  7.6 0.0 copy-start.5
  7.6 3.7 %collective-permute-start.1 = (bf16[2,128,2048]{2,1,0:T(8,128)(2,1)S(1)}, bf16[2,128,2048]{2,1,0:T(8,128)(2,1)S(1)}, u32[]{:S(2)}, u32[]{:S(2)}) collective-permute-start(bf16[2,128,2048]{2,1,0:T(8,128)(2,1)S(1)} %get-tuple-element.29), channel_id=1, source_target_pairs={{0,15},{1,0},{2,1},{3,2},{4,3},{5,4},{6,5},{7,6},{8,7},{9,8},{10,9... | collective-permute-start | bytes 3145736 | tf_op jit(solution)/shard_map/ppermute | solution.py:27
  11.3 0.0 collective-permute-start
  11.3 0.9 fusion.7
  12.2 0.7 collective-permute-start.3
  12.9 2.4 %pad_maximum_fusion = (bf16[2,256,2048]{2,1,0:T(8,128)(2,1)}, bf16[2,256,2048]{2,1,0:T(8,128)(2,1)}) fusion(bf16[1,256,2048]{2,1,0:T(8,128)(2,1)S(1)} %bitcast.11, bf16[1,256,2048]{2,1,0:T(8,128)(2,1)S(1)} %bitcast.15, bf16[1,256,2048]{2,1,0:T(8,128)(2,1)S(1)} %bitcast.16, bf16[1,256,2048]{2,1,0:T(8,128)(2,1)S(1)} %bitcast.17), kind=kLoop, calls=%fused_computation.5 | loop fusion | flops 2097152 | bytes 8388608 | tf_op jit(solution)/shard_map/stack | solution.py:90
  15.3 83.2 %collective-permute-done.1.refs_4_ = bf16[2,128,2048]{2,1,0:T(8,128)(2,1)S(1)} collective-permute-done((bf16[2,128,2048]{2,1,0:T(8,128)(2,1)S(1)}, bf16[2,128,2048]{2,1,0:T(8,128)(2,1)S(1)}, u32[]{:S(2)}, u32[]{:S(2)}) %collective-permute-start.1) | collective-permute-done | bytes 1048608 | tf_op jit(solution)/shard_map/ppermute | solution.py:27
  98.4 0.0 collective-permute-done.refs_3_
  98.5 0.0 collective-permute-done.4.refs_5_
  98.5 0.9 copy-done.2
  99.4 0.3 copy-done.3
  99.8 18.1 %shard_map.76 = (bf16[256,2048]{1,0:T(8,128)(2,1)}, f32[2,256,2048]{2,1,0:T(8,128)}, bf16[2,128,1536]{2,1,0:T(8,128)(2,1)}, bf16[2,128,1536]{2,1,0:T(8,128)(2,1)...) custom-call(s32[2,4]{1,0:T(2,128)} %refs_0_.3, bf16[2,256,2048]{2,1,0:T(8,128)(2,1)} %get-tuple-element.32.refs_1_, ...), custom_call_target="tpu_custom_call" | custom-call | flops 2013265920 | bytes 11010048 | tf_op jit(solution)/shard_map/pallas_call | solution.py:123
  117.9 3.5 %collective-permute-start.10 = (bf16[2,256,1536]{2,1,0:T(8,128)(2,1)}, bf16[2,256,1536]{2,1,0:T(8,128)(2,1)S(1)}, u32[]{:S(2)}, u32[]{:S(2)}) collective-permute-start(bf16[2,256,1536]{2,1,0:T(8,128)(2,1)} %get-tuple-element.23), channel_id=1, source_target_pairs={{0,12},{1,13},{2,14},{3,15},{4,0},{5,1},{6,2},{7,3},{8,4},{9,5},{1... | collective-permute-start | bytes 4718600 | tf_op jit(solution)/shard_map/ppermute | solution.py:27
  121.4 0.0 collective-permute-done.3.refs_6_
  121.4 0.5 collective-permute-done.2.refs_5_
  121.9 7.9 %shard_map.77 = (bf16[256,2048]{1,0:T(8,128)(2,1)}, f32[2,256,2048]{2,1,0:T(8,128)}, bf16[2,128,512]{2,1,0:T(8,128)(2,1)}, bf16[2,128,512]{2,1,0:T(8,128)(2,1)},...) custom-call(s32[2,4]{1,0:T(2,128)} %refs_0_.3, ...), custom_call_target="tpu_custom_call", output_to_operand_aliasing={{0}: (7, {}), {1}: (8, {})} | custom-call | flops 671088640 | bytes 3670016 | tf_op jit(solution)/shard_map/pallas_call | solution.py:123
  129.8 0.1 collective-permute-start.7
  129.9 23.0 %collective-permute-start.9 = (bf16[2,128,512]{2,1,0:T(8,128)(2,1)}, bf16[2,128,512]{2,1,0:T(8,128)(2,1)S(1)}, u32[]{:S(2)}, u32[]{:S(2)}) collective-permute-start(bf16[2,128,512]{2,1,0:T(8,128)(2,1)} %get-tuple-element.22), channel_id=1, source_target_pairs={{0,15},{1,0},{2,1},{3,2},{4,3},{5,4},{6,5},{7,6},{8,7},{9,8},{10,9... | collective-permute-start | bytes 786440 | tf_op jit(solution)/shard_map/ppermute | solution.py:27
  152.9 39.0 %collective-permute-done.7 = bf16[2,128,512]{2,1,0:T(8,128)(2,1)S(1)} collective-permute-done((bf16[2,128,512]{2,1,0:T(8,128)(2,1)}, bf16[2,128,512]{2,1,0:T(8,128)(2,1)S(1)}, u32[]{:S(2)}, u32[]{:S(2)}) %collective-permute-start.7) | collective-permute-done | bytes 262176 | tf_op jit(solution)/shard_map/ppermute | solution.py:27
  191.9 0.0 collective-permute-start.8
  191.9 0.0 collective-permute-done.9
  191.9 2.7 %collective-permute-start.11 = (bf16[2,256,512]{2,1,0:T(8,128)(2,1)}, bf16[2,256,512]{2,1,0:T(8,128)(2,1)S(1)}, u32[]{:S(2)}, u32[]{:S(2)}) collective-permute-start(bf16[2,256,512]{2,1,0:T(8,128)(2,1)} %get-tuple-element.24), channel_id=1, source_target_pairs={{0,12},{1,13},{2,14},{3,15},{4,0},{5,1},{6,2},{7,3},{8,4},{9,5},{1... | collective-permute-start | bytes 1572872 | tf_op jit(solution)/shard_map/ppermute | solution.py:27
  194.6 23.2 %collective-permute-done.11 = bf16[2,256,512]{2,1,0:T(8,128)(2,1)S(1)} collective-permute-done((bf16[2,256,512]{2,1,0:T(8,128)(2,1)}, bf16[2,256,512]{2,1,0:T(8,128)(2,1)S(1)}, u32[]{:S(2)}, u32[]{:S(2)}) %collective-permute-start.11) | collective-permute-done | bytes 524320 | tf_op jit(solution)/shard_map/ppermute | solution.py:27
  217.8 2.3 collective-permute-start.13
  220.1 0.0 collective-permute-done.8
  220.1 2.7 %convert_add_fusion = f32[2,256,2048]{2,1,0:T(8,128)S(1)} fusion(f32[2,256,2048]{2,1,0:T(8,128)} %get-tuple-element.18, bf16[2,128,512]{2,1,0:T(8,128)(2,1)S(1)} %collective-permute-done.9, bf16[2,128,1536]{2,1,0:T(8,128)(2,1)S(1)} %collective-permute-done.8, bf16[2,128,512]{2,1,0:T(8,128)(2,1)S(1)} %collective-permute-done.7, ...), kind=kLoop, calls=%fused_computation | loop fusion | flops 16777216 | bytes 14155776 | tf_op jit(solution)/shard_map/add | solution.py:156
  222.8 6.3 %collective-permute-done.13 = bf16[2,256,512]{2,1,0:T(8,128)(2,1)S(1)} collective-permute-done((bf16[2,256,512]{2,1,0:T(8,128)(2,1)}, bf16[2,256,512]{2,1,0:T(8,128)(2,1)S(1)}, u32[]{:S(2)}, u32[]{:S(2)}) %collective-permute-start.13) | collective-permute-done | bytes 524320 | tf_op jit(solution)/shard_map/ppermute | solution.py:27
  229.1 1.7 fusion.4
  (16 shorter events, 0.0 us)
Async XLA Ops:
  0.6 6.8 %copy-start = (bf16[256,2048]{1,0:T(8,128)(2,1)S(1)}, bf16[256,2048]{1,0:T(8,128)(2,1)}, u32[]{:S(2)}) copy-start(bf16[256,2048]{1,0:T(8,128)(2,1)} %param.7) | copy-start | bytes 3145732
  0.6 6.8 %copy-start.1 = (bf16[256,2048]{1,0:T(8,128)(2,1)S(1)}, bf16[256,2048]{1,0:T(8,128)(2,1)}, u32[]{:S(2)}) copy-start(bf16[256,2048]{1,0:T(8,128)(2,1)} %param.6) | copy-start | bytes 3145732
  2.3 96.1 %collective-permute-start.5 = (bf16[2,256,1536]{2,1,0:T(8,128)(2,1)S(1)}, bf16[2,256,1536]{2,1,0:T(8,128)(2,1)}, u32[]{:S(2)}, u32[]{:S(2)}) collective-permute-start(bf16[2,256,1536]{2,1,0:T(8,128)(2,1)S(1)} %fusion.2), channel_id=1, source_target_pairs={{0,12},{1,13},{2,14},{3,15},{4,0},{5,1},{6,2},{7,3},{8,4},{9,5},{1... | collective-permute-start | bytes 4718600 | tf_op jit(solution)/shard_map/ppermute | solution.py:27
  7.4 91.1 %collective-permute-start.4 = (bf16[2,256,1536]{2,1,0:T(8,128)(2,1)S(1)}, bf16[2,256,1536]{2,1,0:T(8,128)(2,1)}, u32[]{:S(2)}, u32[]{:S(2)}) collective-permute-start(bf16[2,256,1536]{2,1,0:T(8,128)(2,1)S(1)} %fusion.2), channel_id=1, source_target_pairs={{0,4},{1,5},{2,6},{3,7},{4,8},{5,9},{6,10},{7,11},{8,12},{9,13},{1... | collective-permute-start | bytes 4718600 | tf_op jit(solution)/shard_map/ppermute | solution.py:27
  7.6 5.3 %copy-start.4 = (bf16[256,2048]{1,0:T(8,128)(2,1)S(1)}, bf16[256,2048]{1,0:T(8,128)(2,1)}, u32[]{:S(2)}) copy-start(bf16[256,2048]{1,0:T(8,128)(2,1)} %param.8) | copy-start | bytes 3145732
  7.6 5.3 %copy-start.5 = (bf16[256,2048]{1,0:T(8,128)(2,1)S(1)}, bf16[256,2048]{1,0:T(8,128)(2,1)}, u32[]{:S(2)}) copy-start(bf16[256,2048]{1,0:T(8,128)(2,1)} %param.5) | copy-start | bytes 3145732
  7.6 90.8 %collective-permute-start.1 = (bf16[2,128,2048]{2,1,0:T(8,128)(2,1)S(1)}, bf16[2,128,2048]{2,1,0:T(8,128)(2,1)S(1)}, u32[]{:S(2)}, u32[]{:S(2)}) collective-permute-start(bf16[2,128,2048]{2,1,0:T(8,128)(2,1)S(1)} %get-tuple-element.29), channel_id=1, source_target_pairs={{0,15},{1,0},{2,1},{3,2},{4,3},{5,4},{6,5},{7,6},{8,7},{9,8},{10,9... | collective-permute-start | bytes 3145736 | tf_op jit(solution)/shard_map/ppermute | solution.py:27
  11.3 87.1 %collective-permute-start = (bf16[2,128,2048]{2,1,0:T(8,128)(2,1)S(1)}, bf16[2,128,2048]{2,1,0:T(8,128)(2,1)S(1)}, u32[]{:S(2)}, u32[]{:S(2)}) collective-permute-start(bf16[2,128,2048]{2,1,0:T(8,128)(2,1)S(1)} %get-tuple-element.30), channel_id=1, source_target_pairs={{0,1},{1,2},{2,3},{3,4},{4,5},{5,6},{6,7},{7,8},{8,9},{9,10},{10,1... | collective-permute-start | bytes 3145736 | tf_op jit(solution)/shard_map/ppermute | solution.py:27
  12.2 109.2 %collective-permute-start.3 = (bf16[2,256,512]{2,1,0:T(8,128)(2,1)}, bf16[2,256,512]{2,1,0:T(8,128)(2,1)}, u32[]{:S(2)}, u32[]{:S(2)}) collective-permute-start(bf16[2,256,512]{2,1,0:T(8,128)(2,1)} %fusion.7), channel_id=1, source_target_pairs={{0,12},{1,13},{2,14},{3,15},{4,0},{5,1},{6,2},{7,3},{8,4},{9,5},{1... | collective-permute-start | bytes 1572872 | tf_op jit(solution)/shard_map/ppermute | solution.py:27
  98.4 1.0 copy-start.2
  98.4 23.5 %collective-permute-start.2 = (bf16[2,256,512]{2,1,0:T(8,128)(2,1)}, bf16[2,256,512]{2,1,0:T(8,128)(2,1)}, u32[]{:S(2)}, u32[]{:S(2)}) collective-permute-start(bf16[2,256,512]{2,1,0:T(8,128)(2,1)} %fusion.7), channel_id=1, source_target_pairs={{0,4},{1,5},{2,6},{3,7},{4,8},{5,9},{6,10},{7,11},{8,12},{9,13},{1... | collective-permute-start | bytes 1572872 | tf_op jit(solution)/shard_map/ppermute | solution.py:27
  98.4 1.3 copy-start.3
  117.9 102.2 %collective-permute-start.10 = (bf16[2,256,1536]{2,1,0:T(8,128)(2,1)}, bf16[2,256,1536]{2,1,0:T(8,128)(2,1)S(1)}, u32[]{:S(2)}, u32[]{:S(2)}) collective-permute-start(bf16[2,256,1536]{2,1,0:T(8,128)(2,1)} %get-tuple-element.23), channel_id=1, source_target_pairs={{0,12},{1,13},{2,14},{3,15},{4,0},{5,1},{6,2},{7,3},{8,4},{9,5},{1... | collective-permute-start | bytes 4718600 | tf_op jit(solution)/shard_map/ppermute | solution.py:27
  121.4 98.7 %collective-permute-start.12 = (bf16[2,256,1536]{2,1,0:T(8,128)(2,1)}, bf16[2,256,1536]{2,1,0:T(8,128)(2,1)S(1)}, u32[]{:S(2)}, u32[]{:S(2)}) collective-permute-start(bf16[2,256,1536]{2,1,0:T(8,128)(2,1)} %get-tuple-element.25), channel_id=1, source_target_pairs={{0,4},{1,5},{2,6},{3,7},{4,8},{5,9},{6,10},{7,11},{8,12},{9,13},{1... | collective-permute-start | bytes 4718600 | tf_op jit(solution)/shard_map/ppermute | solution.py:27
  129.8 62.0 %collective-permute-start.7 = (bf16[2,128,512]{2,1,0:T(8,128)(2,1)}, bf16[2,128,512]{2,1,0:T(8,128)(2,1)S(1)}, u32[]{:S(2)}, u32[]{:S(2)}) collective-permute-start(bf16[2,128,512]{2,1,0:T(8,128)(2,1)} %get-tuple-element.20), channel_id=1, source_target_pairs={{0,1},{1,2},{2,3},{3,4},{4,5},{5,6},{6,7},{7,8},{8,9},{9,10},{10,1... | collective-permute-start | bytes 786440 | tf_op jit(solution)/shard_map/ppermute | solution.py:27
  129.9 62.0 %collective-permute-start.9 = (bf16[2,128,512]{2,1,0:T(8,128)(2,1)}, bf16[2,128,512]{2,1,0:T(8,128)(2,1)S(1)}, u32[]{:S(2)}, u32[]{:S(2)}) collective-permute-start(bf16[2,128,512]{2,1,0:T(8,128)(2,1)} %get-tuple-element.22), channel_id=1, source_target_pairs={{0,15},{1,0},{2,1},{3,2},{4,3},{5,4},{6,5},{7,6},{8,7},{9,8},{10,9... | collective-permute-start | bytes 786440 | tf_op jit(solution)/shard_map/ppermute | solution.py:27
  152.9 67.2 %collective-permute-start.6 = (bf16[2,128,1536]{2,1,0:T(8,128)(2,1)}, bf16[2,128,1536]{2,1,0:T(8,128)(2,1)S(1)}, u32[]{:S(2)}, u32[]{:S(2)}) collective-permute-start(bf16[2,128,1536]{2,1,0:T(8,128)(2,1)} %get-tuple-element.19), channel_id=1, source_target_pairs={{0,1},{1,2},{2,3},{3,4},{4,5},{5,6},{6,7},{7,8},{8,9},{9,10},{10,1... | collective-permute-start | bytes 2359304 | tf_op jit(solution)/shard_map/ppermute | solution.py:27
  191.9 28.2 %collective-permute-start.8 = (bf16[2,128,1536]{2,1,0:T(8,128)(2,1)}, bf16[2,128,1536]{2,1,0:T(8,128)(2,1)S(1)}, u32[]{:S(2)}, u32[]{:S(2)}) collective-permute-start(bf16[2,128,1536]{2,1,0:T(8,128)(2,1)} %get-tuple-element.21), channel_id=1, source_target_pairs={{0,15},{1,0},{2,1},{3,2},{4,3},{5,4},{6,5},{7,6},{8,7},{9,8},{10,9... | collective-permute-start | bytes 2359304 | tf_op jit(solution)/shard_map/ppermute | solution.py:27
  191.9 25.9 %collective-permute-start.11 = (bf16[2,256,512]{2,1,0:T(8,128)(2,1)}, bf16[2,256,512]{2,1,0:T(8,128)(2,1)S(1)}, u32[]{:S(2)}, u32[]{:S(2)}) collective-permute-start(bf16[2,256,512]{2,1,0:T(8,128)(2,1)} %get-tuple-element.24), channel_id=1, source_target_pairs={{0,12},{1,13},{2,14},{3,15},{4,0},{5,1},{6,2},{7,3},{8,4},{9,5},{1... | collective-permute-start | bytes 1572872 | tf_op jit(solution)/shard_map/ppermute | solution.py:27
  217.8 11.3 %collective-permute-start.13 = (bf16[2,256,512]{2,1,0:T(8,128)(2,1)}, bf16[2,256,512]{2,1,0:T(8,128)(2,1)S(1)}, u32[]{:S(2)}, u32[]{:S(2)}) collective-permute-start(bf16[2,256,512]{2,1,0:T(8,128)(2,1)} %get-tuple-element.26), channel_id=1, source_target_pairs={{0,4},{1,5},{2,6},{3,7},{4,8},{5,9},{6,10},{7,11},{8,12},{9,13},{1... | collective-permute-start | bytes 1572872 | tf_op jit(solution)/shard_map/ppermute | solution.py:27

commit v10 on v7

--- a/solution.py
+++ b/solution.py
@@ -155,10 +155,15 @@
             input_output_aliases=aliases,
             cost_estimate=cost,
         )(key_lists, qd, kv, left, right, far[c][0], far[c][1], *extra_args)
-        received.append((
-            shifted(to_right, SEQ, 1), shifted(to_left, SEQ, -1),
+        received.append([
+            (to_left, to_right),
             shifted(to_late, SEQ, FRAME_DEV), shifted(to_early, SEQ, -FRAME_DEV),
-        ))
+        ])
+    tied = lax.optimization_barrier(([r[0] for r in received], d_queries, own))
+    sides, d_queries, own = tied
+    for r, (to_left, to_right) in zip(received, sides):
+        from_left, from_right = swap_edges(to_left, to_right)
+        r[0:1] = [from_left, from_right]
     from_left, from_right, from_early, from_late = (
         jnp.concatenate([r[k] for r in received], axis=-1) for k in range(4)
     )

time: 242 us -> 248 us (1.025)
  starting transfers between devices: 36.4 us -> 21.5 us
  waiting for transfers between devices: 148 us -> 162 us
  other arithmetic: 14.4 us -> 19.2 us
  blocking collectives: 0 us -> 2.48 us
    ppermute x1 -> x3, waiting for transfers between devices: 11.5 us -> 86 us  [crossing(): return lax.ppermute(tree, SEQ, route)]
    ppermute x12 -> x8, waiting for transfers between devices: 136 us -> 75.6 us  [shifted(): return lax.ppermute(tree, axis, route)]
    ppermute x12 -> x8, starting transfers between devices: 30.9 us -> 6.41 us  [shifted(): return lax.ppermute(tree, axis, route)]
    ppermute x1 -> x3, starting transfers between devices: 5.48 us -> 15 us  [crossing(): return lax.ppermute(tree, SEQ, route)]
    select_n x1 -> x3, other arithmetic: 2.99 us -> 5.27 us  [swap_edges(): return (jnp.where(even, across, partner), jnp.where(even, partner, across))]
    select_n x1 -> x3, other arithmetic: 3.39 us -> 5.65 us  [swap_edges(): gathered = lax.all_gather(jnp.where(even, for_right, for_left), 'core')]
  transfers between devices with their start and end apart: 14 -> 13, of which waited for: 6 -> 6; matrix products, arithmetic and copies ran while one was open for 3% -> 5% of each run, Pallas kernels for 11% -> 7%
where the time goes in v10:
time: 248 us
  waiting for transfers between devices  162 us (65%)
  Pallas kernels  26.8 us (11%)
  starting transfers between devices  21.5 us (9%)
  other arithmetic  19.2 us (8%)
  between operations  14.2 us (6%)
  blocking collectives  2.48 us (1%)
    ppermute x3, waiting for transfers between devices, crossing(): return lax.ppermute(tree, SEQ, route)  86 us
    ppermute x8, waiting for transfers between devices, shifted(): return lax.ppermute(tree, axis, route)  75.6 us
    pallas_call x2, Pallas kernels, body(): pl.pallas_call(lambda *refs, a=aliased: attend_kernel(*refs, scale=scale,...  26.8 us
    ppermute x3, starting transfers between devices, crossing(): return lax.ppermute(tree, SEQ, route)  15 us
    ppermute x8, starting transfers between devices, shifted(): return lax.ppermute(tree, axis, route)  6.41 us
    select_n x3, other arithmetic, swap_edges(): gathered = lax.all_gather(jnp.where(even, for_right, for_left), 'core')  5.65 us
    select_n x3, other arithmetic, swap_edges(): return (jnp.where(even, across, partner), jnp.where(even, partner, across))  5.27 us
  transfers between devices with their start and end apart: 13, of which 6 were waited for; matrix products, arithmetic and copies ran while one was open for 5% of the time, Pallas kernels for 7%

profile of v10, /device:TPU:0, one launch (start us, length us, event | category | flops | bytes accessed | tf_op | source)
XLA Modules:
  0.0 248.2 jit_solution(4235396825977685361)
XLA Ops:
  7.2 3.4 %broadcast_select_fusion = (bf16[2,128,2048]{2,1,0:T(8,128)(2,1)}, bf16[2,128,2048]{2,1,0:T(8,128)(2,1)S(1)}) fusion(pred[]{:T(512)S(6)} %eq.2, bf16[1,256,2048]{2,1,0:T(8,128)(2,1)} %bitcast.20, bf16[1,256,2048]{2,1,0:T(8,128)(2,1)} %bitcast.24), kind=kLoop, calls=%fused_computation.18 | loop fusion | flops 3145728 | bytes 4194305 | tf_op jit(solution)/shard_map/jit(_where)/select_n | solution.py:37
  10.7 0.0 all-gather.8.cloned.1.call-start
  10.7 5.5 %collective-permute-start = (bf16[2,128,2048]{2,1,0:T(8,128)(2,1)S(1)}, bf16[2,128,2048]{2,1,0:T(8,128)(2,1)}, u32[]{:S(2)}, u32[]{:S(2)}) collective-permute-start(bf16[2,128,2048]{2,1,0:T(8,128)(2,1)S(1)} %get-tuple-element.46), channel_id=1, source_target_pairs={{0,15},{1,2},{2,1},{3,4},{4,3},{5,6},{6,5},{7,8},{8,7},{9,10},{10,... | collective-permute-start | bytes 3145736 | tf_op jit(solution)/shard_map/ppermute | solution.py:30
  16.2 1.3 fusion
  17.5 0.4 collective-permute-start.2
  17.9 1.6 collective-permute-start.1
  19.5 0.9 fusion.3
  20.4 2.2 collective-permute-start.4
  22.6 1.6 pad_maximum_fusion.refs_2_
  24.2 0.7 copy-done.4
  24.9 1.6 pad_maximum_fusion.1.refs_1_
  26.5 11.5 %collective-permute-done = bf16[2,128,2048]{2,1,0:T(8,128)(2,1)} collective-permute-done((bf16[2,128,2048]{2,1,0:T(8,128)(2,1)S(1)}, bf16[2,128,2048]{2,1,0:T(8,128)(2,1)}, u32[]{:S(2)}, u32[]{:S(2)}) %collective-permute-start) | collective-permute-done | bytes 1048608 | tf_op jit(solution)/shard_map/ppermute | solution.py:30
  38.0 3.0 %bitcast_select_fusion = (bf16[2,128,2048]{2,1,0:T(8,128)(2,1)}, bf16[2,128,2048]{2,1,0:T(8,128)(2,1)}) fusion(bf16[2,128,2048]{2,1,0:T(8,128)(2,1)} %collective-permute-done, pred[]{:T(512)S(6)} %eq.2, bf16[2,2,128,2048]{3,2,1,0:T(8,128)(2,1)} %bitcast.31, s32[]{:T(128)S(6)} %select_n.71), kind=kLoop, calls=%fused_computation.16 | loop fusion | flops 1048576 | bytes 4194309 | tf_op jit(solution)/shard_map/jit(_where)/select_n | solution.py:39
  41.0 53.7 %collective-permute-done.2.refs_6_ = bf16[2,256,1536]{2,1,0:T(8,128)(2,1)} collective-permute-done((bf16[2,256,1536]{2,1,0:T(8,128)(2,1)}, bf16[2,256,1536]{2,1,0:T(8,128)(2,1)}, u32[]{:S(2)}, u32[]{:S(2)}) %collective-permute-start.2) | collective-permute-done | bytes 1572896 | tf_op jit(solution)/shard_map/ppermute | solution.py:45
  94.7 11.9 %collective-permute-done.1.refs_5_ = bf16[2,256,1536]{2,1,0:T(8,128)(2,1)} collective-permute-done((bf16[2,256,1536]{2,1,0:T(8,128)(2,1)}, bf16[2,256,1536]{2,1,0:T(8,128)(2,1)}, u32[]{:S(2)}, u32[]{:S(2)}) %collective-permute-start.1) | collective-permute-done | bytes 1572896 | tf_op jit(solution)/shard_map/ppermute | solution.py:45
  106.6 18.1 %shard_map.76 = (bf16[256,2048]{1,0:T(8,128)(2,1)}, f32[2,256,2048]{2,1,0:T(8,128)}, bf16[2,128,1536]{2,1,0:T(8,128)(2,1)}, bf16[2,128,1536]{2,1,0:T(8,128)(2,1)...) custom-call(s32[2,4]{1,0:T(2,128)} %refs_0_.3, bf16[2,256,2048]{2,1,0:T(8,128)(2,1)} %pad_maximum_fusion.1.refs_1_, ...), custom_call_target="tpu_custom_call" | custom-call | flops 2013265920 | bytes 11010048 | tf_op jit(solution)/shard_map/pallas_call | solution.py:138
  124.7 8.7 %shard_map.77 = (bf16[256,2048]{1,0:T(8,128)(2,1)}, f32[2,256,2048]{2,1,0:T(8,128)}, bf16[2,128,512]{2,1,0:T(8,128)(2,1)}, bf16[2,128,512]{2,1,0:T(8,128)(2,1)},...) custom-call(s32[2,4]{1,0:T(2,128)} %refs_0_.3, ...), custom_call_target="tpu_custom_call", output_to_operand_aliasing={{0}: (7, {}), {1}: (8, {})} | custom-call | flops 671088640 | bytes 3670016 | tf_op jit(solution)/shard_map/pallas_call | solution.py:138
  133.4 1.2 broadcast_select_fusion.2
  134.7 0.1 collective-permute-start.7
  134.8 2.0 collective-permute-start.9
  136.8 9.5 %collective-permute-start.5 = (bf16[2,128,1536]{2,1,0:T(8,128)(2,1)}, bf16[2,128,1536]{2,1,0:T(8,128)(2,1)}, u32[]{:S(2)}, u32[]{:S(2)}) collective-permute-start(bf16[2,128,1536]{2,1,0:T(8,128)(2,1)} %get-tuple-element.48), channel_id=1, source_target_pairs={{0,15},{1,2},{2,1},{3,4},{4,3},{5,6},{6,5},{7,8},{8,7},{9,10},{10,... | collective-permute-start | bytes 2359304 | tf_op jit(solution)/shard_map/ppermute | solution.py:30
  146.2 1.0 broadcast_select_fusion.4
  147.2 0.1 collective-permute-start.6
  147.3 0.1 collective-permute-start.8
  147.4 2.5 all-gather.2
  149.9 74.5 %collective-permute-done.6 = bf16[2,128,512]{2,1,0:T(8,128)(2,1)S(1)} collective-permute-done((bf16[2,128,512]{2,1,0:T(8,128)(2,1)S(1)}, bf16[2,128,512]{2,1,0:T(8,128)(2,1)S(1)}, u32[]{:S(2)}, u32[]{:S(2)}) %collective-permute-start.6) | collective-permute-done | bytes 262176 | tf_op jit(solution)/shard_map/ppermute | solution.py:30
  224.4 0.8 bitcast_select_fusion.5
  225.2 1.5 bitcast_select_fusion.3
  226.7 3.4 %collective-permute-done.8 = bf16[2,256,512]{2,1,0:T(8,128)(2,1)} collective-permute-done((bf16[2,256,512]{2,1,0:T(8,128)(2,1)}, bf16[2,256,512]{2,1,0:T(8,128)(2,1)}, u32[]{:S(2)}, u32[]{:S(2)}) %collective-permute-start.8) | collective-permute-done | bytes 524320 | tf_op jit(solution)/shard_map/ppermute | solution.py:45
  230.1 6.6 %collective-permute-done.10 = bf16[2,256,512]{2,1,0:T(8,128)(2,1)} collective-permute-done((bf16[2,256,512]{2,1,0:T(8,128)(2,1)}, bf16[2,256,512]{2,1,0:T(8,128)(2,1)}, u32[]{:S(2)}, u32[]{:S(2)}) %collective-permute-start.10) | collective-permute-done | bytes 524320 | tf_op jit(solution)/shard_map/ppermute | solution.py:45
  236.7 3.0 %add_convert_fusion = bf16[2,256,2048]{2,1,0:T(8,128)(2,1)S(1)} fusion(f32[2,256,2048]{2,1,0:T(8,128)} %get-tuple-element.30, bf16[2,128,512]{2,1,0:T(8,128)(2,1)S(1)} %copy-done.2, bf16[2,128,1536]{2,1,0:T(8,128)(2,1)S(1)} %get-tuple-element.42, bf16[2,128,512]{2,1,0:T(8,128)(2,1)S(1)} %get-tuple-element.49, bf16[2,128,1536]{2,1,0:T(8,128)(2,1)S(1)} %get-tuple-element.41, ...), kind=kLoop, calls=%fused_computation | loop fusion | flops 20971520 | bytes 12582912 | tf_op jit(solution)/shard_map/convert_element_type | solution.py:172
  239.8 1.6 slice_bitcast_fusion
  (27 shorter events, 0.1 us)
Async XLA Ops:
  7.2 30.8 %all-gather.6.cloned.1.call-start = ((), (), s32[]{:S(2)}) async-start(), calls=%async_computation | async-start | bytes 3145728 | tf_op jit(solution)/shard_map/all_gather | solution.py:37
  7.2 9.0 %copy-start = (bf16[256,2048]{1,0:T(8,128)(2,1)S(1)}, bf16[256,2048]{1,0:T(8,128)(2,1)}, u32[]{:S(2)}) copy-start(bf16[256,2048]{1,0:T(8,128)(2,1)} %param.7) | copy-start | bytes 3145732
  7.2 9.0 %copy-start.1 = (bf16[256,2048]{1,0:T(8,128)(2,1)S(1)}, bf16[256,2048]{1,0:T(8,128)(2,1)}, u32[]{:S(2)}) copy-start(bf16[256,2048]{1,0:T(8,128)(2,1)} %param.6) | copy-start | bytes 3145732
  10.7 214.5 %all-gather.8.cloned.1.call-start = ((), (), s32[]{:S(2)}) async-start(), calls=%async_computation.1 | async-start | bytes 2359296 | tf_op jit(solution)/shard_map/all_gather | solution.py:37
  10.7 27.3 %collective-permute-start = (bf16[2,128,2048]{2,1,0:T(8,128)(2,1)S(1)}, bf16[2,128,2048]{2,1,0:T(8,128)(2,1)}, u32[]{:S(2)}, u32[]{:S(2)}) collective-permute-start(bf16[2,128,2048]{2,1,0:T(8,128)(2,1)S(1)} %get-tuple-element.46), channel_id=1, source_target_pairs={{0,15},{1,2},{2,1},{3,4},{4,3},{5,6},{6,5},{7,8},{8,7},{9,10},{10,... | collective-permute-start | bytes 3145736 | tf_op jit(solution)/shard_map/ppermute | solution.py:30
  17.5 77.2 %collective-permute-start.2 = (bf16[2,256,1536]{2,1,0:T(8,128)(2,1)}, bf16[2,256,1536]{2,1,0:T(8,128)(2,1)}, u32[]{:S(2)}, u32[]{:S(2)}) collective-permute-start(bf16[2,256,1536]{2,1,0:T(8,128)(2,1)} %fusion), channel_id=1, source_target_pairs={{0,12},{1,13},{2,14},{3,15},{4,0},{5,1},{6,2},{7,3},{8,4},{9,5},{1... | collective-permute-start | bytes 4718600 | tf_op jit(solution)/shard_map/ppermute | solution.py:45
  17.9 88.7 %collective-permute-start.1 = (bf16[2,256,1536]{2,1,0:T(8,128)(2,1)}, bf16[2,256,1536]{2,1,0:T(8,128)(2,1)}, u32[]{:S(2)}, u32[]{:S(2)}) collective-permute-start(bf16[2,256,1536]{2,1,0:T(8,128)(2,1)} %fusion), channel_id=1, source_target_pairs={{0,4},{1,5},{2,6},{3,7},{4,8},{5,9},{6,10},{7,11},{8,12},{9,13},{1... | collective-permute-start | bytes 4718600 | tf_op jit(solution)/shard_map/ppermute | solution.py:45
  20.4 104.3 %collective-permute-start.4 = (bf16[2,256,512]{2,1,0:T(8,128)(2,1)}, bf16[2,256,512]{2,1,0:T(8,128)(2,1)}, u32[]{:S(2)}, u32[]{:S(2)}) collective-permute-start(bf16[2,256,512]{2,1,0:T(8,128)(2,1)} %fusion.3), channel_id=1, source_target_pairs={{0,12},{1,13},{2,14},{3,15},{4,0},{5,1},{6,2},{7,3},{8,4},{9,5},{1... | collective-permute-start | bytes 1572872 | tf_op jit(solution)/shard_map/ppermute | solution.py:45
  22.6 102.1 %collective-permute-start.3 = (bf16[2,256,512]{2,1,0:T(8,128)(2,1)}, bf16[2,256,512]{2,1,0:T(8,128)(2,1)}, u32[]{:S(2)}, u32[]{:S(2)}) collective-permute-start(bf16[2,256,512]{2,1,0:T(8,128)(2,1)} %fusion.3), channel_id=1, source_target_pairs={{0,4},{1,5},{2,6},{3,7},{4,8},{5,9},{6,10},{7,11},{8,12},{9,13},{1... | collective-permute-start | bytes 1572872 | tf_op jit(solution)/shard_map/ppermute | solution.py:45
  22.6 1.6 copy-start.3
  22.6 2.3 copy-start.4
  124.7 8.7 %copy-start.5 = (bf16[2,128,1536]{2,1,0:T(8,128)(2,1)S(1)}, bf16[2,128,1536]{2,1,0:T(8,128)(2,1)}, u32[]{:S(2)}) copy-start(bf16[2,128,1536]{2,1,0:T(8,128)(2,1)} %get-tuple-element.31) | copy-start | bytes 2359300
  124.7 8.7 %copy-start.6 = (bf16[2,128,1536]{2,1,0:T(8,128)(2,1)S(1)}, bf16[2,128,1536]{2,1,0:T(8,128)(2,1)}, u32[]{:S(2)}) copy-start(bf16[2,128,1536]{2,1,0:T(8,128)(2,1)} %get-tuple-element.32) | copy-start | bytes 2359300
  133.4 12.8 %copy-start.7 = (bf16[2,128,512]{2,1,0:T(8,128)(2,1)S(1)}, bf16[2,128,512]{2,1,0:T(8,128)(2,1)}, u32[]{:S(2)}) copy-start(bf16[2,128,512]{2,1,0:T(8,128)(2,1)} %get-tuple-element.33) | copy-start | bytes 786436
  134.7 102.0 %collective-permute-start.7 = (bf16[2,256,1536]{2,1,0:T(8,128)(2,1)}, bf16[2,256,1536]{2,1,0:T(8,128)(2,1)S(1)}, u32[]{:S(2)}, u32[]{:S(2)}) collective-permute-start(bf16[2,256,1536]{2,1,0:T(8,128)(2,1)} %get-tuple-element.35), channel_id=1, source_target_pairs={{0,12},{1,13},{2,14},{3,15},{4,0},{5,1},{6,2},{7,3},{8,4},{9,5},{1... | collective-permute-start | bytes 4718600 | tf_op jit(solution)/shard_map/ppermute | solution.py:45
  134.8 102.0 %collective-permute-start.9 = (bf16[2,256,1536]{2,1,0:T(8,128)(2,1)}, bf16[2,256,1536]{2,1,0:T(8,128)(2,1)S(1)}, u32[]{:S(2)}, u32[]{:S(2)}) collective-permute-start(bf16[2,256,1536]{2,1,0:T(8,128)(2,1)} %get-tuple-element.37), channel_id=1, source_target_pairs={{0,4},{1,5},{2,6},{3,7},{4,8},{5,9},{6,10},{7,11},{8,12},{9,13},{1... | collective-permute-start | bytes 4718600 | tf_op jit(solution)/shard_map/ppermute | solution.py:45
  136.8 88.4 %collective-permute-start.5 = (bf16[2,128,1536]{2,1,0:T(8,128)(2,1)}, bf16[2,128,1536]{2,1,0:T(8,128)(2,1)}, u32[]{:S(2)}, u32[]{:S(2)}) collective-permute-start(bf16[2,128,1536]{2,1,0:T(8,128)(2,1)} %get-tuple-element.48), channel_id=1, source_target_pairs={{0,15},{1,2},{2,1},{3,4},{4,3},{5,6},{6,5},{7,8},{8,7},{9,10},{10,... | collective-permute-start | bytes 2359304 | tf_op jit(solution)/shard_map/ppermute | solution.py:30
  147.2 77.2 %collective-permute-start.6 = (bf16[2,128,512]{2,1,0:T(8,128)(2,1)S(1)}, bf16[2,128,512]{2,1,0:T(8,128)(2,1)S(1)}, u32[]{:S(2)}, u32[]{:S(2)}) collective-permute-start(bf16[2,128,512]{2,1,0:T(8,128)(2,1)S(1)} %get-tuple-element.52), channel_id=1, source_target_pairs={{0,15},{1,2},{2,1},{3,4},{4,3},{5,6},{6,5},{7,8},{8,7},{9,10},{10,... | collective-permute-start | bytes 786440 | tf_op jit(solution)/shard_map/ppermute | solution.py:30
  147.3 82.8 %collective-permute-start.8 = (bf16[2,256,512]{2,1,0:T(8,128)(2,1)}, bf16[2,256,512]{2,1,0:T(8,128)(2,1)}, u32[]{:S(2)}, u32[]{:S(2)}) collective-permute-start(bf16[2,256,512]{2,1,0:T(8,128)(2,1)} %get-tuple-element.36), channel_id=1, source_target_pairs={{0,12},{1,13},{2,14},{3,15},{4,0},{5,1},{6,2},{7,3},{8,4},{9,5},{1... | collective-permute-start | bytes 1572872 | tf_op jit(solution)/shard_map/ppermute | solution.py:45
  224.4 12.3 %collective-permute-start.10 = (bf16[2,256,512]{2,1,0:T(8,128)(2,1)}, bf16[2,256,512]{2,1,0:T(8,128)(2,1)}, u32[]{:S(2)}, u32[]{:S(2)}) collective-permute-start(bf16[2,256,512]{2,1,0:T(8,128)(2,1)} %get-tuple-element.38), channel_id=1, source_target_pairs={{0,4},{1,5},{2,6},{3,7},{4,8},{5,9},{6,10},{7,11},{8,12},{9,13},{1... | collective-permute-start | bytes 1572872 | tf_op jit(solution)/shard_map/ppermute | solution.py:45
  225.2 11.6 %copy-start.2 = (bf16[2,128,512]{2,1,0:T(8,128)(2,1)S(1)}, bf16[2,128,512]{2,1,0:T(8,128)(2,1)}, u32[]{:S(2)}) copy-start(bf16[2,128,512]{2,1,0:T(8,128)(2,1)} %get-tuple-element.50) | copy-start | bytes 786436
Sparse Core Ops, SparseCore 0:
  10.8 13.2 all-gather.5
  134.8 15.0 all-gather.7

commit v11 on v6

--- a/solution.py
+++ b/solution.py
@@ -19,6 +19,19 @@
 TN = (((0,), (0,)), ((), ()))
 F32 = jnp.float32
 BF16 = jnp.bfloat16
+
+
+def paired_route(tree, step_even, step_odd):
+    count = lax.axis_size("seq")
+    route = [(i, (i + (step_even if i % 2 == 0 else step_odd)) % count) for i in range(count)]
+    return lax.ppermute(tree, "seq", route)
+
+
+def swap_edges(for_left, for_right):
+    even = lax.rem(lax.axis_index("seq"), 2) == 0
+    across = paired_route(jnp.where(even, for_left, for_right), -1, 1)
+    beside = paired_route(jnp.where(even, for_right, for_left), 1, -1)
+    return jnp.where(even, across, beside), jnp.where(even, beside, across)
 
 
 def shifted(tree, axis, distance):
@@ -96,8 +109,7 @@
     far = []
     for part in chunked:
         far.append((shifted(part, "seq", FRAME_DEV), shifted(part, "seq", -FRAME_DEV)))
-    left = shifted(kv[:, rows - BLK:], "seq", 1)
-    right = shifted(kv[:, :BLK], "seq", -1)
+    left, right = swap_edges(kv[:, :BLK], kv[:, rows - BLK:])
 
     d_queries = own = None
     received = []
@@ -139,7 +151,7 @@
             cost_estimate=cost,
         )(key_lists, qd, kv, left, right, far[c][0], far[c][1], *extra_args)
         received.append((
-            shifted(to_right, "seq", 1), shifted(to_left, "seq", -1),
+            *swap_edges(to_left, to_right),
             shifted(to_late, "seq", FRAME_DEV), shifted(to_early, "seq", -FRAME_DEV),
         ))
     from_left, from_right, from_early, from_late = (

time: 219 us -> 240 us (1.096)
  waiting for transfers between devices: 139 us -> 173 us
  starting transfers between devices: 42 us -> 21.9 us
  other arithmetic: 7.9 us -> 14 us
    ppermute x0 -> x6, waiting for transfers between devices: none -> 84.4 us  [paired_route(): return lax.ppermute(tree, 'seq', route)]
    ppermute x14 -> x8, waiting for transfers between devices: 139 us -> 88.7 us  [shifted(): return lax.ppermute(tree, axis, route)]
    ppermute x14 -> x8, starting transfers between devices: 42 us -> 8.43 us  [shifted(): return lax.ppermute(tree, axis, route)]
    ppermute x0 -> x6, starting transfers between devices: none -> 13.5 us  [paired_route(): return lax.ppermute(tree, 'seq', route)]
    select_n x0 -> x6, other arithmetic: none -> 9.34 us  [the longest x2 3.85 us: swap_edges(): across = paired_route(jnp.where(even, for_left, for_right), -1, 1)]
    another operation x4 -> x3, other arithmetic: 5.07 us -> 3.41 us  [body(): kv = jnp.stack([keys, values])]
  transfers between devices with their start and end apart: 14 -> 14, of which waited for: 5 -> 6; matrix products, arithmetic and copies ran while one was open for 2% -> 4% of each run, Pallas kernels for 12% -> 11%
where the time goes in v11:
time: 240 us; the launch traced here: 239 us
  waiting for transfers between devices  173 us (72%)
  Pallas kernels  26.6 us (11%)
  starting transfers between devices  21.9 us (9%)
  other arithmetic  14 us (6%)
  local copies, waits for them, and re-layouts  2.82 us (1%)
    ppermute x8, waiting for transfers between devices, shifted(): return lax.ppermute(tree, axis, route)  88.7 us
    ppermute x6, waiting for transfers between devices, paired_route(): return lax.ppermute(tree, 'seq', route)  84.4 us
    pallas_call x2, Pallas kernels, body(): pl.pallas_call(lambda *refs, a=aliased: attend_kernel(*refs, scale=scale,...  26.6 us
    ppermute x6, starting transfers between devices, paired_route(): return lax.ppermute(tree, 'seq', route)  13.5 us
    ppermute x8, starting transfers between devices, shifted(): return lax.ppermute(tree, axis, route)  8.43 us
  transfers between devices with their start and end apart: 14, of which 6 were waited for; matrix products, arithmetic and copies ran while one was open for 4% of the time, Pallas kernels for 11%

profile of v11, /device:TPU:0, one launch (start us, length us, event | category | flops | bytes accessed | tf_op | source)
XLA Modules:
  0.0 239.2 jit_solution(3951727919166235646)
XLA Ops:
  0.7 2.5 %broadcast_select_fusion.2 = (bf16[2,128,2048]{2,1,0:T(8,128)(2,1)S(1)}, bf16[2,128,2048]{2,1,0:T(8,128)(2,1)S(1)}) fusion(pred[]{:T(512)S(6)} %eq.2, bf16[1,256,2048]{2,1,0:T(8,128)(2,1)} %bitcast.8, bf16[1,256,2048]{2,1,0:T(8,128)(2,1)} %bitcast.12), kind=kLoop, calls=%fused_computation.18 | loop fusion | flops 3145728 | bytes 4194305 | tf_op jit(solution)/shard_map/jit(_where)/select_n | solution.py:33
  3.2 0.5 collective-permute-start.1
  3.7 5.6 %collective-permute-start = (bf16[2,128,2048]{2,1,0:T(8,128)(2,1)S(1)}, bf16[2,128,2048]{2,1,0:T(8,128)(2,1)S(1)}, u32[]{:S(2)}, u32[]{:S(2)}) collective-permute-start(bf16[2,128,2048]{2,1,0:T(8,128)(2,1)S(1)} %get-tuple-element.32), channel_id=1, source_target_pairs={{0,15},{1,2},{2,1},{3,4},{4,3},{5,6},{6,5},{7,8},{8,7},{9,10},{10,... | collective-permute-start | bytes 3145736 | tf_op jit(solution)/shard_map/ppermute | solution.py:27
  9.4 0.1 fusion
  9.5 0.0 copy-start.5
  9.5 0.0 copy-start.6
  9.5 0.5 collective-permute-start.5
  10.0 1.6 collective-permute-start.4
  11.6 0.9 fusion.3
  12.5 2.2 collective-permute-start.3
  14.7 2.4 pad_maximum_fusion
  17.1 0.0 collective-permute-done.1
  17.1 0.0 collective-permute-start.2
  17.1 15.8 %collective-permute-done = bf16[2,128,2048]{2,1,0:T(8,128)(2,1)S(1)} collective-permute-done((bf16[2,128,2048]{2,1,0:T(8,128)(2,1)S(1)}, bf16[2,128,2048]{2,1,0:T(8,128)(2,1)S(1)}, u32[]{:S(2)}, u32[]{:S(2)}) %collective-permute-start) | collective-permute-done | bytes 1048608 | tf_op jit(solution)/shard_map/ppermute | solution.py:27
  32.9 1.5 broadcast_select_fusion
  34.4 51.3 %collective-permute-done.5.refs_6_ = bf16[2,256,1536]{2,1,0:T(8,128)(2,1)S(1)} collective-permute-done((bf16[2,256,1536]{2,1,0:T(8,128)(2,1)S(1)}, bf16[2,256,1536]{2,1,0:T(8,128)(2,1)S(1)}, u32[]{:S(2)}, u32[]{:S(2)}) %collective-permute-start.5) | collective-permute-done | bytes 1572896 | tf_op jit(solution)/shard_map/ppermute | solution.py:40
  85.7 15.6 %collective-permute-done.4.refs_5_ = bf16[2,256,1536]{2,1,0:T(8,128)(2,1)S(1)} collective-permute-done((bf16[2,256,1536]{2,1,0:T(8,128)(2,1)S(1)}, bf16[2,256,1536]{2,1,0:T(8,128)(2,1)S(1)}, u32[]{:S(2)}, u32[]{:S(2)}) %collective-permute-start.4) | collective-permute-done | bytes 1572896 | tf_op jit(solution)/shard_map/ppermute | solution.py:40
  101.3 1.2 copy-done.4
  102.5 18.1 %shard_map.76 = (bf16[256,2048]{1,0:T(8,128)(2,1)}, f32[2,256,2048]{2,1,0:T(8,128)}, bf16[2,128,1536]{2,1,0:T(8,128)(2,1)}, bf16[2,128,1536]{2,1,0:T(8,128)(2,1)...) custom-call(s32[2,4]{1,0:T(2,128)} %refs_0_.3, bf16[2,256,2048]{2,1,0:T(8,128)(2,1)} %get-tuple-element.42.refs_1_, ...), custom_call_target="tpu_custom_call" | custom-call | flops 2013265920 | bytes 11010048 | tf_op jit(solution)/shard_map/pallas_call | solution.py:133
  120.7 2.7 %broadcast_select_fusion.7 = (bf16[2,128,1536]{2,1,0:T(8,128)(2,1)}, bf16[2,128,1536]{2,1,0:T(8,128)(2,1)}) fusion(bf16[2,128,1536]{2,1,0:T(8,128)(2,1)} %get-tuple-element.19, bf16[2,128,1536]{2,1,0:T(8,128)(2,1)} %get-tuple-element.20, pred[]{:T(512)S(6)} %eq.2), kind=kLoop, calls=%fused_computation.23 | loop fusion | flops 786432 | bytes 3145729 | tf_op jit(solution)/shard_map/jit(_where)/select_n | solution.py:32
  123.4 6.0 %collective-permute-start.6 = (bf16[2,128,1536]{2,1,0:T(8,128)(2,1)}, bf16[2,128,1536]{2,1,0:T(8,128)(2,1)}, u32[]{:S(2)}, u32[]{:S(2)}) collective-permute-start(bf16[2,128,1536]{2,1,0:T(8,128)(2,1)} %get-tuple-element.35), channel_id=1, source_target_pairs={{0,15},{1,2},{2,1},{3,4},{4,3},{5,6},{6,5},{7,8},{8,7},{9,10},{10,... | collective-permute-start | bytes 2359304 | tf_op jit(solution)/shard_map/ppermute | solution.py:27
  129.4 2.0 collective-permute-start.12
  131.4 8.5 %shard_map.77 = (bf16[256,2048]{1,0:T(8,128)(2,1)}, f32[2,256,2048]{2,1,0:T(8,128)}, bf16[2,128,512]{2,1,0:T(8,128)(2,1)}, bf16[2,128,512]{2,1,0:T(8,128)(2,1)},...) custom-call(s32[2,4]{1,0:T(2,128)} %refs_0_.3, ...), custom_call_target="tpu_custom_call", output_to_operand_aliasing={{0}: (7, {}), {1}: (8, {})} | custom-call | flops 671088640 | bytes 3670016 | tf_op jit(solution)/shard_map/pallas_call | solution.py:133
  139.9 1.1 broadcast_select_fusion.11
  141.0 1.4 collective-permute-start.8
  142.4 67.1 %collective-permute-done.8 = bf16[2,128,512]{2,1,0:T(8,128)(2,1)S(1)} collective-permute-done((bf16[2,128,512]{2,1,0:T(8,128)(2,1)S(1)}, bf16[2,128,512]{2,1,0:T(8,128)(2,1)S(1)}, u32[]{:S(2)}, u32[]{:S(2)}) %collective-permute-start.8) | collective-permute-done | bytes 262176 | tf_op jit(solution)/shard_map/ppermute | solution.py:27
  209.5 1.5 collective-permute-done.9
  211.1 2.1 collective-permute-start.13
  213.1 1.5 broadcast_select_fusion.5
  214.6 21.8 %collective-permute-done.11 = bf16[2,256,512]{2,1,0:T(8,128)(2,1)S(1)} collective-permute-done((bf16[2,256,512]{2,1,0:T(8,128)(2,1)}, bf16[2,256,512]{2,1,0:T(8,128)(2,1)S(1)}, u32[]{:S(2)}, u32[]{:S(2)}) %collective-permute-start.11) | collective-permute-done | bytes 524320 | tf_op jit(solution)/shard_map/ppermute | solution.py:40
  236.4 1.2 add_convert_fusion
  237.7 1.6 slice_bitcast_fusion
  (25 shorter events, 0.1 us)
Async XLA Ops:
  0.6 8.7 %copy-start.1 = (bf16[256,2048]{1,0:T(8,128)(2,1)S(1)}, bf16[256,2048]{1,0:T(8,128)(2,1)}, u32[]{:S(2)}) copy-start(bf16[256,2048]{1,0:T(8,128)(2,1)} %param.7) | copy-start | bytes 3145732
  0.6 8.7 %copy-start.2 = (bf16[256,2048]{1,0:T(8,128)(2,1)S(1)}, bf16[256,2048]{1,0:T(8,128)(2,1)}, u32[]{:S(2)}) copy-start(bf16[256,2048]{1,0:T(8,128)(2,1)} %param.6) | copy-start | bytes 3145732
  3.2 13.9 %collective-permute-start.1 = (bf16[2,128,2048]{2,1,0:T(8,128)(2,1)S(1)}, bf16[2,128,2048]{2,1,0:T(8,128)(2,1)S(1)}, u32[]{:S(2)}, u32[]{:S(2)}) collective-permute-start(bf16[2,128,2048]{2,1,0:T(8,128)(2,1)S(1)} %get-tuple-element.31), channel_id=1, source_target_pairs={{0,1},{1,0},{2,3},{3,2},{4,5},{5,4},{6,7},{7,6},{8,9},{9,8},{10,11... | collective-permute-start | bytes 3145736 | tf_op jit(solution)/shard_map/ppermute | solution.py:27
  3.7 29.2 %collective-permute-start = (bf16[2,128,2048]{2,1,0:T(8,128)(2,1)S(1)}, bf16[2,128,2048]{2,1,0:T(8,128)(2,1)S(1)}, u32[]{:S(2)}, u32[]{:S(2)}) collective-permute-start(bf16[2,128,2048]{2,1,0:T(8,128)(2,1)S(1)} %get-tuple-element.32), channel_id=1, source_target_pairs={{0,15},{1,2},{2,1},{3,4},{4,3},{5,6},{6,5},{7,8},{8,7},{9,10},{10,... | collective-permute-start | bytes 3145736 | tf_op jit(solution)/shard_map/ppermute | solution.py:27
  9.5 5.2 %copy-start.5 = (bf16[256,2048]{1,0:T(8,128)(2,1)S(1)}, bf16[256,2048]{1,0:T(8,128)(2,1)}, u32[]{:S(2)}) copy-start(bf16[256,2048]{1,0:T(8,128)(2,1)} %param.8) | copy-start | bytes 3145732
  9.5 5.2 %copy-start.6 = (bf16[256,2048]{1,0:T(8,128)(2,1)S(1)}, bf16[256,2048]{1,0:T(8,128)(2,1)}, u32[]{:S(2)}) copy-start(bf16[256,2048]{1,0:T(8,128)(2,1)} %param.5) | copy-start | bytes 3145732
  9.5 76.2 %collective-permute-start.5 = (bf16[2,256,1536]{2,1,0:T(8,128)(2,1)S(1)}, bf16[2,256,1536]{2,1,0:T(8,128)(2,1)S(1)}, u32[]{:S(2)}, u32[]{:S(2)}) collective-permute-start(bf16[2,256,1536]{2,1,0:T(8,128)(2,1)S(1)} %fusion), channel_id=1, source_target_pairs={{0,12},{1,13},{2,14},{3,15},{4,0},{5,1},{6,2},{7,3},{8,4},{9,5},{1... | collective-permute-start | bytes 4718600 | tf_op jit(solution)/shard_map/ppermute | solution.py:40
  10.0 91.2 %collective-permute-start.4 = (bf16[2,256,1536]{2,1,0:T(8,128)(2,1)S(1)}, bf16[2,256,1536]{2,1,0:T(8,128)(2,1)S(1)}, u32[]{:S(2)}, u32[]{:S(2)}) collective-permute-start(bf16[2,256,1536]{2,1,0:T(8,128)(2,1)S(1)} %fusion), channel_id=1, source_target_pairs={{0,4},{1,5},{2,6},{3,7},{4,8},{5,9},{6,10},{7,11},{8,12},{9,13},{1... | collective-permute-start | bytes 4718600 | tf_op jit(solution)/shard_map/ppermute | solution.py:40
  12.5 116.9 %collective-permute-start.3 = (bf16[2,256,512]{2,1,0:T(8,128)(2,1)}, bf16[2,256,512]{2,1,0:T(8,128)(2,1)}, u32[]{:S(2)}, u32[]{:S(2)}) collective-permute-start(bf16[2,256,512]{2,1,0:T(8,128)(2,1)} %fusion.3), channel_id=1, source_target_pairs={{0,12},{1,13},{2,14},{3,15},{4,0},{5,1},{6,2},{7,3},{8,4},{9,5},{1... | collective-permute-start | bytes 1572872 | tf_op jit(solution)/shard_map/ppermute | solution.py:40
  17.1 114.3 %collective-permute-start.2 = (bf16[2,256,512]{2,1,0:T(8,128)(2,1)}, bf16[2,256,512]{2,1,0:T(8,128)(2,1)}, u32[]{:S(2)}, u32[]{:S(2)}) collective-permute-start(bf16[2,256,512]{2,1,0:T(8,128)(2,1)} %fusion.3), channel_id=1, source_target_pairs={{0,4},{1,5},{2,6},{3,7},{4,8},{5,9},{6,10},{7,11},{8,12},{9,13},{1... | collective-permute-start | bytes 1572872 | tf_op jit(solution)/shard_map/ppermute | solution.py:40
  85.7 15.6 %copy-start.3 = (bf16[2,256,1536]{2,1,0:T(8,128)(2,1)}, bf16[2,256,1536]{2,1,0:T(8,128)(2,1)S(1)}, u32[]{:S(2)}) copy-start(bf16[2,256,1536]{2,1,0:T(8,128)(2,1)S(1)} %collective-permute-done.5.refs_6_) | copy-start | bytes 4718596
  101.3 1.2 copy-start.4
  123.4 87.7 %collective-permute-start.6 = (bf16[2,128,1536]{2,1,0:T(8,128)(2,1)}, bf16[2,128,1536]{2,1,0:T(8,128)(2,1)}, u32[]{:S(2)}, u32[]{:S(2)}) collective-permute-start(bf16[2,128,1536]{2,1,0:T(8,128)(2,1)} %get-tuple-element.35), channel_id=1, source_target_pairs={{0,15},{1,2},{2,1},{3,4},{4,3},{5,6},{6,5},{7,8},{8,7},{9,10},{10,... | collective-permute-start | bytes 2359304 | tf_op jit(solution)/shard_map/ppermute | solution.py:27
  129.4 83.8 %collective-permute-start.7 = (bf16[2,128,1536]{2,1,0:T(8,128)(2,1)}, bf16[2,128,1536]{2,1,0:T(8,128)(2,1)}, u32[]{:S(2)}, u32[]{:S(2)}) collective-permute-start(bf16[2,128,1536]{2,1,0:T(8,128)(2,1)} %get-tuple-element.36), channel_id=1, source_target_pairs={{0,1},{1,0},{2,3},{3,2},{4,5},{5,4},{6,7},{7,6},{8,9},{9,8},{10,11... | collective-permute-start | bytes 2359304 | tf_op jit(solution)/shard_map/ppermute | solution.py:27
  129.4 107.1 %collective-permute-start.10 = (bf16[2,256,1536]{2,1,0:T(8,128)(2,1)}, bf16[2,256,1536]{2,1,0:T(8,128)(2,1)S(1)}, u32[]{:S(2)}, u32[]{:S(2)}) collective-permute-start(bf16[2,256,1536]{2,1,0:T(8,128)(2,1)} %get-tuple-element.23), channel_id=1, source_target_pairs={{0,12},{1,13},{2,14},{3,15},{4,0},{5,1},{6,2},{7,3},{8,4},{9,5},{1... | collective-permute-start | bytes 4718600 | tf_op jit(solution)/shard_map/ppermute | solution.py:40
  129.4 107.1 %collective-permute-start.12 = (bf16[2,256,1536]{2,1,0:T(8,128)(2,1)}, bf16[2,256,1536]{2,1,0:T(8,128)(2,1)S(1)}, u32[]{:S(2)}, u32[]{:S(2)}) collective-permute-start(bf16[2,256,1536]{2,1,0:T(8,128)(2,1)} %get-tuple-element.25), channel_id=1, source_target_pairs={{0,4},{1,5},{2,6},{3,7},{4,8},{5,9},{6,10},{7,11},{8,12},{9,13},{1... | collective-permute-start | bytes 4718600 | tf_op jit(solution)/shard_map/ppermute | solution.py:40
  139.9 71.2 %copy-start.7 = (bf16[2,256,512]{2,1,0:T(8,128)(2,1)S(1)}, bf16[2,256,512]{2,1,0:T(8,128)(2,1)}, u32[]{:S(2)}) copy-start(bf16[2,256,512]{2,1,0:T(8,128)(2,1)} %get-tuple-element.26) | copy-start | bytes 1572868
  141.0 68.4 %collective-permute-start.8 = (bf16[2,128,512]{2,1,0:T(8,128)(2,1)S(1)}, bf16[2,128,512]{2,1,0:T(8,128)(2,1)S(1)}, u32[]{:S(2)}, u32[]{:S(2)}) collective-permute-start(bf16[2,128,512]{2,1,0:T(8,128)(2,1)S(1)} %get-tuple-element.39), channel_id=1, source_target_pairs={{0,15},{1,2},{2,1},{3,4},{4,3},{5,6},{6,5},{7,8},{8,7},{9,10},{10,... | collective-permute-start | bytes 786440 | tf_op jit(solution)/shard_map/ppermute | solution.py:27
  209.5 1.5 collective-permute-start.9
  211.0 25.4 %copy-start = (f32[2,256,2048]{2,1,0:T(8,128)S(1)}, f32[2,256,2048]{2,1,0:T(8,128)}, u32[]{:S(2)}) copy-start(f32[2,256,2048]{2,1,0:T(8,128)} %get-tuple-element.18) | copy-start | bytes 12582916
  211.0 25.4 %collective-permute-start.11 = (bf16[2,256,512]{2,1,0:T(8,128)(2,1)}, bf16[2,256,512]{2,1,0:T(8,128)(2,1)S(1)}, u32[]{:S(2)}, u32[]{:S(2)}) collective-permute-start(bf16[2,256,512]{2,1,0:T(8,128)(2,1)} %get-tuple-element.24), channel_id=1, source_target_pairs={{0,12},{1,13},{2,14},{3,15},{4,0},{5,1},{6,2},{7,3},{8,4},{9,5},{1... | collective-permute-start | bytes 1572872 | tf_op jit(solution)/shard_map/ppermute | solution.py:40
  211.1 25.3 %collective-permute-start.13 = (bf16[2,256,512]{2,1,0:T(8,128)(2,1)S(1)}, bf16[2,256,512]{2,1,0:T(8,128)(2,1)S(1)}, u32[]{:S(2)}, u32[]{:S(2)}) collective-permute-start(bf16[2,256,512]{2,1,0:T(8,128)(2,1)S(1)} %copy-done.7), channel_id=1, source_target_pairs={{0,4},{1,5},{2,6},{3,7},{4,8},{5,9},{6,10},{7,11},{8,12},{9,13},{1... | collective-permute-start | bytes 1572872 | tf_op jit(solution)/shard_map/ppermute | solution.py:40
